TPU v7x, 32 devices: a whole 2x2x4 slice. The times are simulated.
32 devices in a mesh: test: 4 (over z), cell: 8 (over y, x, core).
Axes of the slice: x: 2, y: 2, z: 4, core: 2. Of those that a mesh axis runs over, the one named last changes fastest.
Arguments:
- log_perm: float32 [128, 16, 256], P('cell'), may hold values from -1 to 1
- panel: float32 [8, 128, 16, 256], P('test', 'cell'), may hold values from -4 to 4
- wells: int32 [4, 8], P('test'), may hold values from 0 to 524287
- rates: float32 [4, 8], P('test'), may hold values from 1 to 10
- recharge: float32 [4, 128, 16, 256], P('test', 'cell'), may hold values from 0.25 to 4
- gauge: float32 [128, 16, 256], P('cell'), may hold values from 0.25 to 4
Outputs:
- hessian_panel: float32 [8, 128, 16, 256], P('test', 'cell')
Inputs may be any that keep to these rules, and one draw needn't show every extreme that they name: `wells`: each entry names a cell of the whole grid, numbered x * 16 * 256 + y * 256 + z; a test may name a cell more than once.
All inputs are finite; a program needn't handle non-finite values.
Results may differ from a plain program's by a relative error of at most 0.0001.
Values sent between devices are 32-bit elements; how exact they have to be, the bound alone decides.
No kernel may reach another device: no remote copies, remote signals or barrier semaphores. Data moves between devices by JAX's collectives and lax.ppermute only.
A program may use at most 64 MiB of HBM per device.

v0:
```python
import functools
import math

import jax
import jax.numpy as jnp
from jax import lax
from jax.experimental import pallas as pl
from jax.experimental.pallas import tpu as pltpu
from jax.sharding import PartitionSpec as P

CHEB = 4


storage = 0.02


def with_halo(cells, axis, dim, width):
    count = lax.axis_size(axis)
    ends = count - 1
    head = lax.slice_in_dim(cells, 0, width, axis=dim)
    tail = lax.slice_in_dim(cells, cells.shape[dim] - width, cells.shape[dim], axis=dim)
    return jnp.concatenate(
        [
            lax.ppermute(tail, axis, [(i, i + 1) for i in range(ends)]),
            cells,
            lax.ppermute(head, axis, [(i + 1, i) for i in range(ends)]),
        ],
        axis=dim,
    )


INTERPRET = False


def solve_kernel(b_ref, k_ref, m_ref, o_ref, sol, res, da, db, *, offset, first, keeps, pushes):
    rows, rows_y, depth_z = sol.shape
    iy = lax.broadcasted_iota(jnp.int32, (rows_y, depth_z), 0)
    iz = lax.broadcasted_iota(jnp.int32, (rows_y, depth_z), 1)

    def init(r, c):
        value = b_ref[0, r]
        res[r] = value
        da[r] = value * first
        sol[r] = jnp.zeros_like(value)
        return c

    lax.fori_loop(0, rows, init, 0)
    bufs = (da, db)
    for turn in range(CHEB):
        src = bufs[turn % 2]
        dst = bufs[(turn + 1) % 2]
        keep = keeps[turn]
        push = pushes[turn]

        def step(r, c, src=src, dst=dst, keep=keep, push=push):
            here = src[r]
            face = r - 1 + offset
            total = k_ref[0, face] * (here - src[r + 1])
            total = total + k_ref[1, face] * (here - src[r - 1])
            up = jnp.where(iy < rows_y - 1, pltpu.roll(here, rows_y - 1, 0), 0.0)
            down = jnp.where(iy > 0, pltpu.roll(here, 1, 0), 0.0)
            total = total + k_ref[2, face] * (here - up) + k_ref[3, face] * (here - down)
            up = jnp.where(iz < depth_z - 1, pltpu.roll(here, depth_z - 1, 1), 0.0)
            down = jnp.where(iz > 0, pltpu.roll(here, 1, 1), 0.0)
            total = total + k_ref[4, face] * (here - up) + k_ref[5, face] * (here - down)
            image = storage * here + total
            sol[r] = sol[r] + here
            fresh = res[r] - image
            res[r] = fresh
            dst[r] = (keep * here + push * fresh) * m_ref[r + offset]
            return c

        lax.fori_loop(turn + 1, rows - 1 - turn, step, 0)
    final = bufs[CHEB % 2]

    def out(r, c):
        o_ref[0, r - CHEB] = sol[r] + final[r]
        return c

    lax.fori_loop(CHEB, rows - CHEB, out, 0)


def kernel_solve(right_side, face_stack, mask_full, offset, first, keeps, pushes):
    fields, rows, rows_y, depth_z = right_side.shape
    body = functools.partial(
        solve_kernel,
        offset=offset,
        first=first,
        keeps=tuple(keeps),
        pushes=tuple(pushes),
    )
    return pl.pallas_call(
        body,
        grid=(fields,),
        in_specs=[
            pl.BlockSpec((1, rows, rows_y, depth_z), lambda f: (f, 0, 0, 0)),
            pl.BlockSpec(face_stack.shape, lambda f: (0, 0, 0, 0)),
            pl.BlockSpec(mask_full.shape, lambda f: (0, 0, 0)),
        ],
        out_specs=pl.BlockSpec((1, rows - 2 * CHEB, rows_y, depth_z), lambda f: (f, 0, 0, 0)),
        out_shape=jax.ShapeDtypeStruct((fields, rows - 2 * CHEB, rows_y, depth_z), jnp.float32),
        scratch_shapes=[pltpu.VMEM((rows, rows_y, depth_z), jnp.float32) for _ in range(4)],
        compiler_params=pltpu.CompilerParams(vmem_limit_bytes=48 * 1024 * 1024),
        interpret=INTERPRET,
    )(right_side, face_stack, mask_full)


def cheb_table(count):
    highest = storage + 12.0 * math.e
    theta = 0.5 * (highest + storage)
    spread = 0.5 * (highest - storage)
    sigma = theta / spread
    rho = 1.0 / sigma
    keeps = []
    pushes = []
    for turn in range(count):
        after = 1.0 / (2.0 * sigma - rho)
        keeps.append(after * rho)
        pushes.append(2.0 * after / spread)
        rho = after
    return (1.0 / theta, keeps, pushes)


def neighbours(field, back):
    axis = field.ndim - back
    widths = [(0, 0)] * field.ndim
    widths[axis] = (1, 1)
    padded = jnp.pad(field, widths)
    length = field.shape[axis]
    return (
        lax.slice_in_dim(padded, 2, length + 2, axis=axis),
        lax.slice_in_dim(padded, 0, length, axis=axis),
    )


def diffuse(weight_ext, field_ext):
    weight = weight_ext[..., 1:-1, :, :]
    field = field_ext[..., 1:-1, :, :]
    total = 0.5 * (weight + weight_ext[..., 2:, :, :]) * (field - field_ext[..., 2:, :, :])
    total = total + 0.5 * (weight + weight_ext[..., :-2, :, :]) * (
        field - field_ext[..., :-2, :, :]
    )
    for back in (2, 1):
        weight_up, weight_down = neighbours(weight, back)
        field_up, field_down = neighbours(field, back)
        total = (
            total
            + 0.5 * (weight + weight_up) * (field - field_up)
            + 0.5 * (weight + weight_down) * (field - field_down)
        )
    return total


def faces(weight_ext):
    weight = weight_ext[1:-1]
    weight_up_y, weight_down_y = neighbours(weight, 2)
    weight_up_z, weight_down_z = neighbours(weight, 1)
    return (
        0.5 * (weight + weight_ext[2:]),
        0.5 * (weight + weight_ext[:-2]),
        0.5 * (weight + weight_up_y),
        0.5 * (weight + weight_down_y),
        0.5 * (weight + weight_up_z),
        0.5 * (weight + weight_down_z),
    )


def apply_faces(face, field_ext):
    field = field_ext[..., 1:-1, :, :]
    total = face[0] * (field - field_ext[..., 2:, :, :])
    total = total + face[1] * (field - field_ext[..., :-2, :, :])
    for back, up, down in ((2, face[2], face[3]), (1, face[4], face[5])):
        field_up, field_down = neighbours(field, back)
        total = total + up * (field - field_up) + down * (field - field_down)
    return total


def pairs(left_ext, right_ext):
    left = left_ext[..., 1:-1, :, :]
    right = right_ext[..., 1:-1, :, :]
    total = (left - left_ext[..., 2:, :, :]) * (right - right_ext[..., 2:, :, :])
    total = total + (left - left_ext[..., :-2, :, :]) * (right - right_ext[..., :-2, :, :])
    for back in (2, 1):
        left_up, left_down = neighbours(left, back)
        right_up, right_down = neighbours(right, back)
        total = (
            total
            + (left - left_up) * (right - right_up)
            + (left - left_down) * (right - right_down)
        )
    return total


def inner(field):
    return field[..., 1:-1, :, :]


def shards(log_perm, panel, wells, rates, recharge, gauge):
    place = lax.axis_index("cell")
    parts = lax.axis_size("cell")
    slab, rows_y, depth_z = log_perm.shape
    cols = panel.shape[0]
    tests_here, well_count = wells.shape
    first, keeps, pushes = cheb_table(CHEB)
    reach = 2 * CHEB + 1
    rows_ext = slab + 2 * reach
    perm = jnp.exp(log_perm)
    scaled = perm[None] * panel
    stacked = jnp.concatenate([perm[None], scaled, recharge], axis=0)
    ext = with_halo(stacked, "cell", 1, reach)
    perm_ext = ext[0]
    scaled_ext = ext[1 : 1 + cols]
    rech_own = ext[1 + cols :]
    cells = slab * rows_y * depth_z
    packed = jnp.concatenate(
        [recharge.reshape(tests_here, cells), wells.astype(jnp.float32), rates], axis=1
    )
    groups = lax.axis_size("test")
    tests = groups * tests_here
    others = jnp.concatenate(
        [
            lax.ppermute(packed, "test", [(i, (i + shift) % groups) for i in range(groups)])
            for shift in range(1, groups)
        ]
        or [packed[:0]],
        axis=0,
    )
    rech_others = with_halo(
        others[:, :cells].reshape(tests - tests_here, slab, rows_y, depth_z), "cell", 1, reach
    )
    wells_others = others[:, cells : cells + well_count].astype(jnp.int32)
    rates_others = others[:, cells + well_count :]

    gx = place * slab - reach + jnp.arange(rows_ext, dtype=jnp.int32)
    mask_ext = ((gx >= 0) & (gx < parts * slab)).astype(jnp.float32)[:, None, None]
    flat = (
        gx[:, None, None] * (rows_y * depth_z)
        + jnp.arange(rows_y, dtype=jnp.int32)[None, :, None] * depth_z
        + jnp.arange(depth_z, dtype=jnp.int32)[None, None, :]
    )

    perm_faces = faces(perm_ext)

    def rows_of(field, halo):
        return lax.slice_in_dim(field, reach - halo, reach + slab + halo, axis=field.ndim - 3)

    face_stack = jnp.stack(perm_faces)
    mask_full = jnp.broadcast_to(mask_ext, (rows_ext, rows_y, depth_z))

    def solve(right_side, halo):
        lead = right_side.shape[:-3]
        flat_side = right_side.reshape((-1,) + right_side.shape[-3:])
        result = kernel_solve(
            flat_side, face_stack, mask_full, reach - halo, first, keeps, pushes
        )
        return result.reshape(lead + result.shape[-3:]), halo - CHEB

    def solve_xla(right_side, halo):
        solution = jnp.zeros_like(right_side)
        residual = right_side
        direction = right_side * first
        for turn in range(CHEB):
            face = tuple(part[reach - halo : reach + slab + halo - 2] for part in perm_faces)
            image = storage * inner(direction) + apply_faces(face, direction)
            solution = inner(solution) + inner(direction)
            residual = inner(residual) - image
            halo -= 1
            direction = (keeps[turn] * inner(direction) + pushes[turn] * residual) * rows_of(
                mask_ext, halo
            )
        return solution + direction, halo

    def chain(rech_ext, well_rows, rate_rows):
        count = rech_ext.shape[0]
        hits = well_rows[:, :, None, None, None] == flat[None, None]
        points = jnp.sum(jnp.where(hits, rate_rows[:, :, None, None, None], 0.0), axis=1)
        own_hits = hits[:, :, reach : reach + slab]
        counts = jnp.sum(own_hits.astype(jnp.float32), axis=1)
        observe = gauge[None] + counts
        state, state_halo = solve(rech_ext + points, reach)
        forcing = -diffuse(rows_of(scaled_ext, state_halo)[None], state[:, None])
        forcing = forcing * rows_of(mask_ext, state_halo - 1)
        forcing = forcing.reshape(count * cols, slab + 2 * CHEB, rows_y, depth_z)
        change, _ = solve(forcing, CHEB)
        weighted = (
            change.reshape(count, cols, slab, rows_y, depth_z) * observe[:, None]
        ).reshape(count * cols, slab, rows_y, depth_z)
        weighted_ext = with_halo(weighted, "cell", 1, CHEB + 1)
        adjoint, _ = solve(weighted_ext, CHEB + 1)
        adjoint = adjoint.reshape(count, cols, slab + 2, rows_y, depth_z)
        state = lax.slice_in_dim(state, CHEB, state.shape[1] - CHEB, axis=1)
        return jnp.sum(pairs(state[:, None], adjoint), axis=0)

    contrib = chain(rech_own, wells, rates)
    if tests > tests_here:
        contrib = contrib + chain(rech_others, wells_others, rates_others)
    return -0.5 * perm[None] * contrib


def solution(mesh):
    return jax.shard_map(
        shards,
        mesh=mesh,
        in_specs=(
            P("cell", None, None),
            P("test", "cell", None, None),
            P("test", None),
            P("test", None),
            P("test", "cell", None, None),
            P("cell", None, None),
        ),
        out_specs=P("test", "cell", None, None),
        check_vma=False,
    )
```

profile of v0, /device:TPU:11, one launch (start us, length us, event | category | flops | bytes accessed | tf_op | source)
XLA Modules:
  0.0 235.3 jit_solution(14080328552533230065)
XLA Ops:
  5.4 1.4 collective-permute-start.6
  6.7 1.7 broadcast_multiply_fusion.2
  9.9 4.6 %collective-permute-start = (f32[4,9,16,256]{3,2,1,0:T(8,128)}, f32[4,9,16,256]{3,2,1,0:T(8,128)}, u32[]{:S(2)}, u32[]{:S(2)}) collective-permute-start(f32[4,9,16,256]{3,2,1,0:T(8,128)} %get-tuple-element.16), channel_id=1, source_target_pairs={{0,1},{1,2},{2,3},{3,4},{4,5},{5,6},{6,7},{8,9},{9,10},{10,11},{11... | collective-permute-start | bytes 1769480 | tf_op jit(solution)/shard_map/ppermute | solution.py:24
  14.5 1.9 collective-permute-start.1
  18.3 7.9 %collective-permute-done.5 = f32[1,65552]{1,0:T(1,128)S(1)} collective-permute-done((f32[1,65552]{1,0:T(1,128)S(1)}, f32[1,65552]{1,0:T(1,128)S(1)}, u32[]{:S(2)}, u32[]{:S(2)}) %collective-permute-start.5) | collective-permute-done | bytes 262240 | tf_op jit(solution)/shard_map/ppermute | solution.py:222
  26.2 2.8 %collective-permute-done.6 = f32[1,65552]{1,0:T(1,128)S(1)} collective-permute-done((f32[1,65552]{1,0:T(1,128)S(1)}, f32[1,65552]{1,0:T(1,128)S(1)}, u32[]{:S(2)}, u32[]{:S(2)}) %collective-permute-start.6) | collective-permute-done | bytes 262240 | tf_op jit(solution)/shard_map/ppermute | solution.py:222
  31.0 3.5 %collective-permute-start.7 = (f32[3,9,16,256]{3,2,1,0:T(8,128)}, f32[3,9,16,256]{3,2,1,0:T(8,128)}, u32[]{:S(2)}, u32[]{:S(2)}) collective-permute-start(f32[3,9,16,256]{3,2,1,0:T(8,128)} %get-tuple-element.33), channel_id=1, source_target_pairs={{0,1},{1,2},{2,3},{3,4},{4,5},{5,6},{6,7},{8,9},{9,10},{10,11},{11... | collective-permute-start | bytes 1327112 | tf_op jit(solution)/shard_map/ppermute | solution.py:24
  34.5 1.9 collective-permute-start.8
  36.5 1.8 broadcast_compare_fusion
  39.1 1.4 select_reduce_fusion
  40.5 1.5 pad_maximum_fusion.1
  43.0 10.4 %shard_map.64 = f32[1,26,16,256]{3,2,1,0:T(8,128)S(1)} custom-call(f32[1,34,16,256]{3,2,1,0:T(8,128)S(1)} %slice_add_fusion.2.b_ref, f32[6,32,16,256]{3,2,1,0:T(8,128)S(1)} %fusion.55.k_ref, f32[34,16,256]{2,1,0:T(8,128)S(1)} %broadcast_in_dim.72.m_ref), custom_call_target="tpu_custom_call" | custom-call | tf_op jit(solution)/shard_map/pallas_call | solution.py:92
  55.1 13.7 %shard_map.65 = f32[2,16,16,256]{3,2,1,0:T(8,128)S(1)} custom-call(f32[2,24,16,256]{3,2,1,0:T(8,128)S(1)} %get-tuple-element.21.b_ref, f32[6,32,16,256]{3,2,1,0:T(8,128)S(1)} %fusion.55.k_ref, f32[34,16,256]{2,1,0:T(8,128)S(1)} %broadcast_in_dim.72.m_ref), custom_call_target="tpu_custom_call" | custom-call | tf_op jit(solution)/shard_map/pallas_call | solution.py:92
  69.5 4.5 %collective-permute-start.2 = (f32[2,5,16,256]{3,2,1,0:T(8,128)}, f32[2,5,16,256]{3,2,1,0:T(8,128)}, u32[]{:S(2)}, u32[]{:S(2)}) collective-permute-start(f32[2,5,16,256]{3,2,1,0:T(8,128)} %get-tuple-element.35), channel_id=1, source_target_pairs={{0,1},{1,2},{2,3},{3,4},{4,5},{5,6},{6,7},{8,9},{9,10},{10,11},{11... | collective-permute-start | bytes 491528 | tf_op jit(solution)/shard_map/ppermute | solution.py:24
  74.1 2.1 collective-permute-start.3
  78.5 1.5 maximum_add_fusion.b_ref
  80.0 33.1 %shard_map.67 = f32[3,26,16,256]{3,2,1,0:T(8,128)S(1)} custom-call(f32[3,34,16,256]{3,2,1,0:T(8,128)S(1)} %maximum_add_fusion.b_ref, f32[6,32,16,256]{3,2,1,0:T(8,128)} %copy-done, f32[34,16,256]{2,1,0:T(8,128)S(1)} %broadcast_in_dim.72.m_ref), custom_call_target="tpu_custom_call" | custom-call | tf_op jit(solution)/shard_map/pallas_call | solution.py:92
  114.3 1.5 add_negate_fusion
  116.3 42.7 %shard_map.68 = f32[6,16,16,256]{3,2,1,0:T(8,128)S(1)} custom-call(f32[6,24,16,256]{3,2,1,0:T(8,128)S(1)} %bitcast_multiply_fusion.b_ref, f32[6,32,16,256]{3,2,1,0:T(8,128)} %copy-done, f32[34,16,256]{2,1,0:T(8,128)S(1)} %broadcast_in_dim.72.m_ref), custom_call_target="tpu_custom_call" | custom-call | tf_op jit(solution)/shard_map/pallas_call | solution.py:92
  159.4 1.9 collective-permute-start.10
  161.3 4.5 %collective-permute-start.9 = (f32[6,5,16,256]{3,2,1,0:T(8,128)S(1)}, f32[6,5,16,256]{3,2,1,0:T(8,128)}, u32[]{:S(2)}, u32[]{:S(2)}) collective-permute-start(f32[6,5,16,256]{3,2,1,0:T(8,128)S(1)} %get-tuple-element.7), channel_id=1, source_target_pairs={{0,1},{1,2},{2,3},{3,4},{4,5},{5,6},{6,7},{8,9},{9,10},{10,11},{11... | collective-permute-start | bytes 1474568 | tf_op jit(solution)/shard_map/ppermute | solution.py:24
  168.2 15.1 %shard_map.66 = f32[2,18,16,256]{3,2,1,0:T(8,128)S(1)} custom-call(f32[2,26,16,256]{3,2,1,0:T(8,128)S(1)} %pad_maximum_fusion.4.b_ref, f32[6,32,16,256]{3,2,1,0:T(8,128)S(1)} %copy-done.1, f32[34,16,256]{2,1,0:T(8,128)S(1)} %broadcast_in_dim.72.m_ref), custom_call_target="tpu_custom_call" | custom-call | tf_op jit(solution)/shard_map/pallas_call | solution.py:92
  184.7 47.0 %shard_map.69 = f32[6,18,16,256]{3,2,1,0:T(8,128)S(1)} custom-call(f32[6,26,16,256]{3,2,1,0:T(8,128)S(1)} %pad_maximum_fusion.b_ref, f32[6,32,16,256]{3,2,1,0:T(8,128)} %copy-done, f32[34,16,256]{2,1,0:T(8,128)S(1)} %broadcast_in_dim.72.m_ref), custom_call_target="tpu_custom_call" | custom-call | tf_op jit(solution)/shard_map/pallas_call | solution.py:92
  231.8 2.1 fusion.6
  (100 shorter events, 23.9 us)
Async XLA Ops:
  0.0 8.5 %copy-start.11 = (f32[2,16,16,256]{3,2,1,0:T(8,128)S(1)}, f32[2,16,16,256]{3,2,1,0:T(8,128)}, u32[]{:S(2)}) copy-start(f32[2,16,16,256]{3,2,1,0:T(8,128)} %param.7) | copy-start | bytes 1572868
  0.0 8.6 %copy-start.2 = (f32[1,16,16,256]{3,2,1,0:T(8,128)S(1)}, f32[1,16,16,256]{3,2,1,0:T(8,128)}, u32[]{:S(2)}) copy-start(f32[1,16,16,256]{3,2,1,0:T(8,128)} %param.10) | copy-start | bytes 786436
  2.9 15.3 %collective-permute-start.4 = (f32[1,65552]{1,0:T(1,128)S(1)}, f32[1,65552]{1,0:T(1,128)S(1)}, u32[]{:S(2)}, u32[]{:S(2)}) collective-permute-start(f32[1,65552]{1,0:T(1,128)S(1)} %dynamic-update-slice.2), channel_id=1, source_target_pairs={{0,8},{8,16},{16,24},{24,0},{1,9},{9,17},{17,25},{25,1},{2,10},{10... | collective-permute-start | bytes 786632 | tf_op jit(solution)/shard_map/ppermute | solution.py:222
  4.3 21.9 %collective-permute-start.5 = (f32[1,65552]{1,0:T(1,128)S(1)}, f32[1,65552]{1,0:T(1,128)S(1)}, u32[]{:S(2)}, u32[]{:S(2)}) collective-permute-start(f32[1,65552]{1,0:T(1,128)S(1)} %dynamic-update-slice.2), channel_id=1, source_target_pairs={{0,16},{8,24},{16,0},{24,8},{1,17},{9,25},{17,1},{25,9},{2,18},{10... | collective-permute-start | bytes 786632 | tf_op jit(solution)/shard_map/ppermute | solution.py:222
  5.4 23.6 %collective-permute-start.6 = (f32[1,65552]{1,0:T(1,128)S(1)}, f32[1,65552]{1,0:T(1,128)S(1)}, u32[]{:S(2)}, u32[]{:S(2)}) collective-permute-start(f32[1,65552]{1,0:T(1,128)S(1)} %dynamic-update-slice.2), channel_id=1, source_target_pairs={{0,24},{8,0},{16,8},{24,16},{1,25},{9,1},{17,9},{25,17},{2,26},{10... | collective-permute-start | bytes 786632 | tf_op jit(solution)/shard_map/ppermute | solution.py:222
  8.7 8.0 %copy-start.12 = (s32[1,8]{1,0:T(1,128)S(1)}, s32[1,8]{1,0:T(1,128)}, u32[]{:S(2)}) copy-start(s32[1,8]{1,0:T(1,128)} %param.8) | copy-start | bytes 100
  9.9 7.8 %copy-start.3 = (f32[16,16,256]{2,1,0:T(8,128)S(1)}, f32[16,16,256]{2,1,0:T(8,128)}, u32[]{:S(2)}) copy-start(f32[16,16,256]{2,1,0:T(8,128)} %param.11) | copy-start | bytes 786436
  9.9 30.6 %collective-permute-start = (f32[4,9,16,256]{3,2,1,0:T(8,128)}, f32[4,9,16,256]{3,2,1,0:T(8,128)}, u32[]{:S(2)}, u32[]{:S(2)}) collective-permute-start(f32[4,9,16,256]{3,2,1,0:T(8,128)} %get-tuple-element.16), channel_id=1, source_target_pairs={{0,1},{1,2},{2,3},{3,4},{4,5},{5,6},{6,7},{8,9},{9,10},{10,11},{11... | collective-permute-start | bytes 1769480 | tf_op jit(solution)/shard_map/ppermute | solution.py:24
  14.5 26.0 %collective-permute-start.1 = (f32[4,9,16,256]{3,2,1,0:T(8,128)}, f32[4,9,16,256]{3,2,1,0:T(8,128)}, u32[]{:S(2)}, u32[]{:S(2)}) collective-permute-start(f32[4,9,16,256]{3,2,1,0:T(8,128)} %get-tuple-element.17), channel_id=1, source_target_pairs={{1,0},{2,1},{3,2},{4,3},{5,4},{6,5},{7,6},{9,8},{10,9},{11,10},{12... | collective-permute-start | bytes 1769480 | tf_op jit(solution)/shard_map/ppermute | solution.py:26
  17.7 36.2 %copy-start.14 = (f32[24]{0:T(128)}, f32[24]{0:T(128)S(1)}, u32[]{:S(2)}) copy-start(f32[24]{0:T(128)S(1)} %slice.272) | copy-start | bytes 292
  31.0 47.5 %collective-permute-start.7 = (f32[3,9,16,256]{3,2,1,0:T(8,128)}, f32[3,9,16,256]{3,2,1,0:T(8,128)}, u32[]{:S(2)}, u32[]{:S(2)}) collective-permute-start(f32[3,9,16,256]{3,2,1,0:T(8,128)} %get-tuple-element.33), channel_id=1, source_target_pairs={{0,1},{1,2},{2,3},{3,4},{4,5},{5,6},{6,7},{8,9},{9,10},{10,11},{11... | collective-permute-start | bytes 1327112 | tf_op jit(solution)/shard_map/ppermute | solution.py:24
  34.5 44.0 %collective-permute-start.8 = (f32[3,9,16,256]{3,2,1,0:T(8,128)}, f32[3,9,16,256]{3,2,1,0:T(8,128)}, u32[]{:S(2)}, u32[]{:S(2)}) collective-permute-start(f32[3,9,16,256]{3,2,1,0:T(8,128)} %get-tuple-element.34), channel_id=1, source_target_pairs={{1,0},{2,1},{3,2},{4,3},{5,4},{6,5},{7,6},{9,8},{10,9},{11,10},{12... | collective-permute-start | bytes 1327112 | tf_op jit(solution)/shard_map/ppermute | solution.py:26
  42.8 12.3 %copy-start = (f32[6,32,16,256]{3,2,1,0:T(8,128)}, f32[6,32,16,256]{3,2,1,0:T(8,128)S(1)}, u32[]{:S(2)}) copy-start(f32[6,32,16,256]{3,2,1,0:T(8,128)S(1)} %fusion.55.k_ref) | copy-start | bytes 9437188
  69.5 97.1 %collective-permute-start.2 = (f32[2,5,16,256]{3,2,1,0:T(8,128)}, f32[2,5,16,256]{3,2,1,0:T(8,128)}, u32[]{:S(2)}, u32[]{:S(2)}) collective-permute-start(f32[2,5,16,256]{3,2,1,0:T(8,128)} %get-tuple-element.35), channel_id=1, source_target_pairs={{0,1},{1,2},{2,3},{3,4},{4,5},{5,6},{6,7},{8,9},{9,10},{10,11},{11... | collective-permute-start | bytes 491528 | tf_op jit(solution)/shard_map/ppermute | solution.py:24
  74.1 92.6 %collective-permute-start.3 = (f32[2,5,16,256]{3,2,1,0:T(8,128)S(1)}, f32[2,5,16,256]{3,2,1,0:T(8,128)}, u32[]{:S(2)}, u32[]{:S(2)}) collective-permute-start(f32[2,5,16,256]{3,2,1,0:T(8,128)S(1)} %get-tuple-element.36), channel_id=1, source_target_pairs={{1,0},{2,1},{3,2},{4,3},{5,4},{6,5},{7,6},{9,8},{10,9},{11,10},{12... | collective-permute-start | bytes 491528 | tf_op jit(solution)/shard_map/ppermute | solution.py:26
  159.4 24.0 %collective-permute-start.10 = (f32[6,5,16,256]{3,2,1,0:T(8,128)S(1)}, f32[6,5,16,256]{3,2,1,0:T(8,128)S(1)}, u32[]{:S(2)}, u32[]{:S(2)}) collective-permute-start(f32[6,5,16,256]{3,2,1,0:T(8,128)S(1)} %get-tuple-element.8), channel_id=1, source_target_pairs={{1,0},{2,1},{3,2},{4,3},{5,4},{6,5},{7,6},{9,8},{10,9},{11,10},{12... | collective-permute-start | bytes 1474568 | tf_op jit(solution)/shard_map/ppermute | solution.py:26
  161.3 22.0 %collective-permute-start.9 = (f32[6,5,16,256]{3,2,1,0:T(8,128)S(1)}, f32[6,5,16,256]{3,2,1,0:T(8,128)}, u32[]{:S(2)}, u32[]{:S(2)}) collective-permute-start(f32[6,5,16,256]{3,2,1,0:T(8,128)S(1)} %get-tuple-element.7), channel_id=1, source_target_pairs={{0,1},{1,2},{2,3},{3,4},{4,5},{5,6},{6,7},{8,9},{9,10},{10,11},{11... | collective-permute-start | bytes 1474568 | tf_op jit(solution)/shard_map/ppermute | solution.py:24
  231.8 2.2 copy-start.4
  231.8 2.2 copy-start.5
  231.8 2.2 copy-start.6
  231.8 2.2 copy-start.7
  231.8 2.2 copy-start.8
  231.8 2.2 copy-start.9
  231.8 2.2 copy-start.10
  (3 other events, 4.6 us)
where the time goes:
time: 236 us; the launch traced here: 235 us
  Pallas kernels  162 us (69%)
  starting transfers between devices  28.9 us (12%)
  other arithmetic  26.7 us (11%)
  waiting for transfers between devices  10.8 us (5%)
  local copies, waits for them, and re-layouts  6.27 us (3%)
    pallas_call x6, Pallas kernels, kernel_solve(): pl.pallas_call(body, grid=(fields,), in_specs=[pl.BlockSpec((1, rows, row...  162 us
    ppermute x4, starting transfers between devices, with_halo(): lax.ppermute(tail, axis, [(i, i + 1) for i in range(ends)])  17.2 us
    ppermute x3, waiting for transfers between devices, shards(): lax.ppermute(packed, 'test', [(i, (i + shift) % groups) for i in range(gr...  10.7 us
    ppermute x4, starting transfers between devices, with_halo(): lax.ppermute(head, axis, [(i + 1, i) for i in range(ends)])  7.87 us
  transfers between devices with their start and end apart: 11, of which 2 were waited for; matrix products, arithmetic and copies ran while one was open for 11% of the time, Pallas kernels for 49%

commit v1 on v0

--- a/solution.py
+++ b/solution.py
@@ -44,7 +44,7 @@
         sol[r] = jnp.zeros_like(value)
         return c
 
-    lax.fori_loop(0, rows, init, 0)
+    lax.fori_loop(0, rows, init, 0, unroll=True)
     bufs = (da, db)
     for turn in range(CHEB):
         src = bufs[turn % 2]
@@ -70,14 +70,14 @@
             dst[r] = (keep * here + push * fresh) * m_ref[r + offset]
             return c
 
-        lax.fori_loop(turn + 1, rows - 1 - turn, step, 0)
+        lax.fori_loop(turn + 1, rows - 1 - turn, step, 0, unroll=True)
     final = bufs[CHEB % 2]
 
     def out(r, c):
         o_ref[0, r - CHEB] = sol[r] + final[r]
         return c
 
-    lax.fori_loop(CHEB, rows - CHEB, out, 0)
+    lax.fori_loop(CHEB, rows - CHEB, out, 0, unroll=True)
 
 
 def kernel_solve(right_side, face_stack, mask_full, offset, first, keeps, pushes):

time: 236 us -> 118 us (0.50)
  Pallas kernels: 162 us -> 41.1 us
    pallas_call x6, Pallas kernels: 162 us -> 41.1 us  [kernel_solve(): pl.pallas_call(body, grid=(fields,), in_specs=[pl.BlockSpec((1, rows, row...]
  transfers between devices with their start and end apart: 11 -> 11, of which waited for: 2 -> 3; matrix products, arithmetic and copies ran while one was open for 11% -> 21% of each run, Pallas kernels for 49% -> 25%
where the time goes in v1:
time: 118 us; the launch traced here: 117 us
  Pallas kernels  41.1 us (35%)
  starting transfers between devices  29.4 us (25%)
  other arithmetic  26.7 us (23%)
  waiting for transfers between devices  12.8 us (11%)
  local copies, waits for them, and re-layouts  6.27 us (5%)
    pallas_call x6, Pallas kernels, kernel_solve(): pl.pallas_call(body, grid=(fields,), in_specs=[pl.BlockSpec((1, rows, row...  41.1 us
    ppermute x4, starting transfers between devices, with_halo(): lax.ppermute(tail, axis, [(i, i + 1) for i in range(ends)])  17.5 us
    ppermute x3, waiting for transfers between devices, shards(): lax.ppermute(packed, 'test', [(i, (i + shift) % groups) for i in range(gr...  10.7 us
    ppermute x4, starting transfers between devices, with_halo(): lax.ppermute(head, axis, [(i + 1, i) for i in range(ends)])  8.09 us
    concatenate x3, other arithmetic, with_halo(): jnp.concatenate([lax.ppermute(tail, axis, [(i, i + 1) for i in range(ends...  4.08 us
    ppermute x3, starting transfers between devices, shards(): lax.ppermute(packed, 'test', [(i, (i + shift) % groups) for i in range(gr...  3.81 us
    mul x2, other arithmetic, shards(): return -0.5 * perm[None] * contrib  3.03 us
    slice x4, local copies, waits for them, and re-layouts, with_halo(): lax.slice_in_dim(cells, cells.shape[dim] - width, cells.shape[dim], axis=...  2.94 us
  transfers between devices with their start and end apart: 11, of which 3 were waited for; matrix products, arithmetic and copies ran while one was open for 21% of the time, Pallas kernels for 25%

profile of v1, /device:TPU:11, one launch (start us, length us, event | category | flops | bytes accessed | tf_op | source)
XLA Modules:
  0.0 117.0 jit_solution(3184541610243107838)
XLA Ops:
  6.7 1.7 %broadcast_multiply_fusion.2 = (f32[16,16,256]{2,1,0:T(8,128)}, f32[1,16,16,256]{3,2,1,0:T(8,128)S(1)}, f32[16,16,256]{2,1,0:T(8,128)S(1)}) fusion(f32[16,16,256]{2,1,0:T(8,128)} %param.6), kind=kLoop, calls=%fused_computation.183 | loop fusion | flops 65536 | bytes 1048576 | tf_op jit(solution)/shard_map/mul | solution.py:297
  9.9 4.6 %collective-permute-start = (f32[4,9,16,256]{3,2,1,0:T(8,128)}, f32[4,9,16,256]{3,2,1,0:T(8,128)}, u32[]{:S(2)}, u32[]{:S(2)}) collective-permute-start(f32[4,9,16,256]{3,2,1,0:T(8,128)} %get-tuple-element.16), channel_id=1, source_target_pairs={{0,1},{1,2},{2,3},{3,4},{4,5},{5,6},{6,7},{8,9},{9,10},{10,11},{11... | collective-permute-start | bytes 1769480 | tf_op jit(solution)/shard_map/ppermute | solution.py:24
  14.5 1.9 %collective-permute-start.1 = (f32[4,9,16,256]{3,2,1,0:T(8,128)}, f32[4,9,16,256]{3,2,1,0:T(8,128)}, u32[]{:S(2)}, u32[]{:S(2)}) collective-permute-start(f32[4,9,16,256]{3,2,1,0:T(8,128)} %get-tuple-element.17), channel_id=1, source_target_pairs={{1,0},{2,1},{3,2},{4,3},{5,4},{6,5},{7,6},{9,8},{10,9},{11,10},{12... | collective-permute-start | bytes 1769480 | tf_op jit(solution)/shard_map/ppermute | solution.py:26
  18.3 7.9 %collective-permute-done.5 = f32[1,65552]{1,0:T(1,128)S(1)} collective-permute-done((f32[1,65552]{1,0:T(1,128)S(1)}, f32[1,65552]{1,0:T(1,128)S(1)}, u32[]{:S(2)}, u32[]{:S(2)}) %collective-permute-start.5) | collective-permute-done | bytes 262240 | tf_op jit(solution)/shard_map/ppermute | solution.py:222
  26.2 2.8 %collective-permute-done.6 = f32[1,65552]{1,0:T(1,128)S(1)} collective-permute-done((f32[1,65552]{1,0:T(1,128)S(1)}, f32[1,65552]{1,0:T(1,128)S(1)}, u32[]{:S(2)}, u32[]{:S(2)}) %collective-permute-start.6) | collective-permute-done | bytes 262240 | tf_op jit(solution)/shard_map/ppermute | solution.py:222
  31.0 3.5 %collective-permute-start.7 = (f32[3,9,16,256]{3,2,1,0:T(8,128)}, f32[3,9,16,256]{3,2,1,0:T(8,128)}, u32[]{:S(2)}, u32[]{:S(2)}) collective-permute-start(f32[3,9,16,256]{3,2,1,0:T(8,128)} %get-tuple-element.33), channel_id=1, source_target_pairs={{0,1},{1,2},{2,3},{3,4},{4,5},{5,6},{6,7},{8,9},{9,10},{10,11},{11... | collective-permute-start | bytes 1327112 | tf_op jit(solution)/shard_map/ppermute | solution.py:24
  34.5 2.1 %collective-permute-start.8 = (f32[3,9,16,256]{3,2,1,0:T(8,128)}, f32[3,9,16,256]{3,2,1,0:T(8,128)}, u32[]{:S(2)}, u32[]{:S(2)}) collective-permute-start(f32[3,9,16,256]{3,2,1,0:T(8,128)} %get-tuple-element.34), channel_id=1, source_target_pairs={{1,0},{2,1},{3,2},{4,3},{5,4},{6,5},{7,6},{9,8},{10,9},{11,10},{12... | collective-permute-start | bytes 1327112 | tf_op jit(solution)/shard_map/ppermute | solution.py:26
  36.7 1.8 %broadcast_compare_fusion = pred[3,8,34,16,256]{4,3,2,1,0:T(8,128)(4,1)S(1)} fusion(s32[34,16,256]{2,1,0:T(8,128)S(1)} %iota_add_fusion, s32[3,8]{1,0:T(4,128)S(1)} %get-tuple-element.24), kind=kLoop, calls=%fused_computation.1 | loop fusion | flops 3342336 | bytes 3899488 | tf_op jit(solution)/shard_map/eq | solution.py:275
  39.2 1.4 %select_reduce_fusion = f32[3,34,16,256]{3,2,1,0:T(8,128)S(1)} fusion(f32[3,8]{1,0:T(4,128)S(1)} %get-tuple-element.25, s32[34,16,256]{2,1,0:T(8,128)S(1)} %iota_add_fusion, s32[3,8]{1,0:T(4,128)S(1)} %get-tuple-element.24), kind=kLoop, calls=%fused_computation | loop fusion | flops 9609216 | bytes 2228416 | tf_op jit(solution)/shard_map/reduce_sum | solution.py:276
  40.7 1.5 %pad_maximum_fusion.1 = f32[4,34,16,256]{3,2,1,0:T(8,128)S(1)} fusion(f32[4,9,16,256]{3,2,1,0:T(8,128)} %collective-permute-done.1, f32[1,16,16,256]{3,2,1,0:T(8,128)S(1)} %copy-done.2, f32[2,16,16,256]{3,2,1,0:T(8,128)S(1)} %broadcast_multiply_fusion.1, f32[1,16,16,256]{3,2,1,0:T(8,128)S(1)} %get-tuple-element.48, f32[4,9,16,256]{3,2,1,0:T(8,128)} %collective-permute-done), kind=kLoop, calls=%fused_computation.11 | loop fusion | flops 2228224 | bytes 4456448 | tf_op jit(solution)/shard_map/concatenate | solution.py:22
  43.2 2.3 %shard_map.64 = f32[1,26,16,256]{3,2,1,0:T(8,128)S(1)} custom-call(f32[1,34,16,256]{3,2,1,0:T(8,128)S(1)} %slice_add_fusion.2.b_ref, f32[6,32,16,256]{3,2,1,0:T(8,128)S(1)} %fusion.55.k_ref, f32[34,16,256]{2,1,0:T(8,128)S(1)} %broadcast_in_dim.72.m_ref), custom_call_target="tpu_custom_call" | custom-call | tf_op jit(solution)/shard_map/pallas_call | solution.py:92
  47.2 3.1 %shard_map.65 = f32[2,16,16,256]{3,2,1,0:T(8,128)S(1)} custom-call(f32[2,24,16,256]{3,2,1,0:T(8,128)S(1)} %get-tuple-element.21.b_ref, f32[6,32,16,256]{3,2,1,0:T(8,128)S(1)} %fusion.55.k_ref, f32[34,16,256]{2,1,0:T(8,128)S(1)} %broadcast_in_dim.72.m_ref), custom_call_target="tpu_custom_call" | custom-call | tf_op jit(solution)/shard_map/pallas_call | solution.py:92
  51.1 4.5 %collective-permute-start.2 = (f32[2,5,16,256]{3,2,1,0:T(8,128)}, f32[2,5,16,256]{3,2,1,0:T(8,128)}, u32[]{:S(2)}, u32[]{:S(2)}) collective-permute-start(f32[2,5,16,256]{3,2,1,0:T(8,128)} %get-tuple-element.35), channel_id=1, source_target_pairs={{0,1},{1,2},{2,3},{3,4},{4,5},{5,6},{6,7},{8,9},{9,10},{10,11},{11... | collective-permute-start | bytes 491528 | tf_op jit(solution)/shard_map/ppermute | solution.py:24
  55.6 2.1 %collective-permute-start.3 = (f32[2,5,16,256]{3,2,1,0:T(8,128)S(1)}, f32[2,5,16,256]{3,2,1,0:T(8,128)}, u32[]{:S(2)}, u32[]{:S(2)}) collective-permute-start(f32[2,5,16,256]{3,2,1,0:T(8,128)S(1)} %get-tuple-element.36), channel_id=1, source_target_pairs={{1,0},{2,1},{3,2},{4,3},{5,4},{6,5},{7,6},{9,8},{10,9},{11,10},{12... | collective-permute-start | bytes 491528 | tf_op jit(solution)/shard_map/ppermute | solution.py:26
  60.1 1.5 %maximum_add_fusion.b_ref = f32[3,34,16,256]{3,2,1,0:T(8,128)S(1)} fusion(f32[3,34,16,256]{3,2,1,0:T(8,128)S(1)} %select_reduce_fusion, f32[3,9,16,256]{3,2,1,0:T(8,128)} %collective-permute-done.8, f32[3,16,16,256]{3,2,1,0:T(8,128)S(1)} %bitcast.119, f32[3,9,16,256]{3,2,1,0:T(8,128)} %collective-permute-done.7), kind=kLoop, calls=%fused_computation.18 | loop fusion | flops 1253376 | bytes 5013504 | tf_op jit(solution)/shard_map/add | solution.py:280
  61.6 8.9 %shard_map.67 = f32[3,26,16,256]{3,2,1,0:T(8,128)S(1)} custom-call(f32[3,34,16,256]{3,2,1,0:T(8,128)S(1)} %maximum_add_fusion.b_ref, f32[6,32,16,256]{3,2,1,0:T(8,128)} %copy-done, f32[34,16,256]{2,1,0:T(8,128)S(1)} %broadcast_in_dim.72.m_ref), custom_call_target="tpu_custom_call" | custom-call | tf_op jit(solution)/shard_map/pallas_call | solution.py:92
  71.7 1.5 %add_negate_fusion = f32[3,2,24,16,256]{4,3,2,1,0:T(8,128)S(1)} fusion(f32[3,24,16,256]{3,2,1,0:T(8,128)S(1)} %get-tuple-element.14, f32[2,24,16,256]{3,2,1,0:T(8,128)S(1)} %multiply_bitcast_fusion, f32[3,24,16,256]{3,2,1,0:T(8,128)S(1)} %get-tuple-element.13, f32[2,24,16,256]{3,2,1,0:T(8,128)S(1)} %get-tuple-element.28, ...), kind=kLoop, calls=%fused_computation.10 | loop fusion | flops 7077888 | bytes 14155776 | tf_op jit(solution)/shard_map/neg | solution.py:281
  73.7 11.2 %shard_map.68 = f32[6,16,16,256]{3,2,1,0:T(8,128)S(1)} custom-call(f32[6,24,16,256]{3,2,1,0:T(8,128)S(1)} %bitcast_multiply_fusion.b_ref, f32[6,32,16,256]{3,2,1,0:T(8,128)} %copy-done, f32[34,16,256]{2,1,0:T(8,128)S(1)} %broadcast_in_dim.72.m_ref), custom_call_target="tpu_custom_call" | custom-call | tf_op jit(solution)/shard_map/pallas_call | solution.py:92
  85.3 1.9 %collective-permute-start.10 = (f32[6,5,16,256]{3,2,1,0:T(8,128)S(1)}, f32[6,5,16,256]{3,2,1,0:T(8,128)S(1)}, u32[]{:S(2)}, u32[]{:S(2)}) collective-permute-start(f32[6,5,16,256]{3,2,1,0:T(8,128)S(1)} %get-tuple-element.8), channel_id=1, source_target_pairs={{1,0},{2,1},{3,2},{4,3},{5,4},{6,5},{7,6},{9,8},{10,9},{11,10},{12... | collective-permute-start | bytes 1474568 | tf_op jit(solution)/shard_map/ppermute | solution.py:26
  87.2 4.8 %collective-permute-start.9 = (f32[6,5,16,256]{3,2,1,0:T(8,128)S(1)}, f32[6,5,16,256]{3,2,1,0:T(8,128)}, u32[]{:S(2)}, u32[]{:S(2)}) collective-permute-start(f32[6,5,16,256]{3,2,1,0:T(8,128)S(1)} %get-tuple-element.7), channel_id=1, source_target_pairs={{0,1},{1,2},{2,3},{3,4},{4,5},{5,6},{6,7},{8,9},{9,10},{10,11},{11... | collective-permute-start | bytes 1474568 | tf_op jit(solution)/shard_map/ppermute | solution.py:24
  94.3 3.4 %shard_map.66 = f32[2,18,16,256]{3,2,1,0:T(8,128)S(1)} custom-call(f32[2,26,16,256]{3,2,1,0:T(8,128)S(1)} %pad_maximum_fusion.4.b_ref, f32[6,32,16,256]{3,2,1,0:T(8,128)S(1)} %copy-done.1, f32[34,16,256]{2,1,0:T(8,128)S(1)} %broadcast_in_dim.72.m_ref), custom_call_target="tpu_custom_call" | custom-call | tf_op jit(solution)/shard_map/pallas_call | solution.py:92
  97.8 2.1 %collective-permute-done.10 = f32[6,5,16,256]{3,2,1,0:T(8,128)S(1)} collective-permute-done((f32[6,5,16,256]{3,2,1,0:T(8,128)S(1)}, f32[6,5,16,256]{3,2,1,0:T(8,128)S(1)}, u32[]{:S(2)}, u32[]{:S(2)}) %collective-permute-start.10) | collective-permute-done | bytes 491552 | tf_op jit(solution)/shard_map/ppermute | solution.py:26
  101.2 12.1 %shard_map.69 = f32[6,18,16,256]{3,2,1,0:T(8,128)S(1)} custom-call(f32[6,26,16,256]{3,2,1,0:T(8,128)S(1)} %pad_maximum_fusion.b_ref, f32[6,32,16,256]{3,2,1,0:T(8,128)} %copy-done, f32[34,16,256]{2,1,0:T(8,128)S(1)} %broadcast_in_dim.72.m_ref), custom_call_target="tpu_custom_call" | custom-call | tf_op jit(solution)/shard_map/pallas_call | solution.py:92
  113.5 2.1 %fusion.6 = f32[2,16,16,256]{3,2,1,0:T(8,128)S(1)} fusion(f32[3,2,16,16,256]{4,3,2,1,0:T(8,128)S(1)} %slice.353, f32[3,2,18,16,256]{4,3,2,1,0:T(8,128)S(1)} %bitcast.114, f32[3,16,16,256]{3,2,1,0:T(8,128)S(1)} %get-tuple-element.31, f32[3,16,16,256]{3,2,1,0:T(8,128)S(1)} %get-tuple-element.30, f32[3,16,16,256]{3,2,1,0:T(8,128)S(1)} %get-tuple-element.32, ...), kind=kLoop, calls=%fused_computation.25 | loop fusion | flops 6946816 | bytes 9961472 | tf_op jit(solution)/shard_map/reduce_sum | solution.py:292
  (100 shorter events, 25.3 us)
Async XLA Ops:
  0.0 8.5 %copy-start.11 = (f32[2,16,16,256]{3,2,1,0:T(8,128)S(1)}, f32[2,16,16,256]{3,2,1,0:T(8,128)}, u32[]{:S(2)}) copy-start(f32[2,16,16,256]{3,2,1,0:T(8,128)} %param.7) | copy-start | bytes 1572868
  0.0 8.6 %copy-start.2 = (f32[1,16,16,256]{3,2,1,0:T(8,128)S(1)}, f32[1,16,16,256]{3,2,1,0:T(8,128)}, u32[]{:S(2)}) copy-start(f32[1,16,16,256]{3,2,1,0:T(8,128)} %param.10) | copy-start | bytes 786436
  2.9 15.3 %collective-permute-start.4 = (f32[1,65552]{1,0:T(1,128)S(1)}, f32[1,65552]{1,0:T(1,128)S(1)}, u32[]{:S(2)}, u32[]{:S(2)}) collective-permute-start(f32[1,65552]{1,0:T(1,128)S(1)} %dynamic-update-slice.2), channel_id=1, source_target_pairs={{0,8},{8,16},{16,24},{24,0},{1,9},{9,17},{17,25},{25,1},{2,10},{10... | collective-permute-start | bytes 786632 | tf_op jit(solution)/shard_map/ppermute | solution.py:222
  4.3 21.9 %collective-permute-start.5 = (f32[1,65552]{1,0:T(1,128)S(1)}, f32[1,65552]{1,0:T(1,128)S(1)}, u32[]{:S(2)}, u32[]{:S(2)}) collective-permute-start(f32[1,65552]{1,0:T(1,128)S(1)} %dynamic-update-slice.2), channel_id=1, source_target_pairs={{0,16},{8,24},{16,0},{24,8},{1,17},{9,25},{17,1},{25,9},{2,18},{10... | collective-permute-start | bytes 786632 | tf_op jit(solution)/shard_map/ppermute | solution.py:222
  5.4 23.6 %collective-permute-start.6 = (f32[1,65552]{1,0:T(1,128)S(1)}, f32[1,65552]{1,0:T(1,128)S(1)}, u32[]{:S(2)}, u32[]{:S(2)}) collective-permute-start(f32[1,65552]{1,0:T(1,128)S(1)} %dynamic-update-slice.2), channel_id=1, source_target_pairs={{0,24},{8,0},{16,8},{24,16},{1,25},{9,1},{17,9},{25,17},{2,26},{10... | collective-permute-start | bytes 786632 | tf_op jit(solution)/shard_map/ppermute | solution.py:222
  8.7 8.0 %copy-start.12 = (s32[1,8]{1,0:T(1,128)S(1)}, s32[1,8]{1,0:T(1,128)}, u32[]{:S(2)}) copy-start(s32[1,8]{1,0:T(1,128)} %param.8) | copy-start | bytes 100
  9.9 7.8 %copy-start.3 = (f32[16,16,256]{2,1,0:T(8,128)S(1)}, f32[16,16,256]{2,1,0:T(8,128)}, u32[]{:S(2)}) copy-start(f32[16,16,256]{2,1,0:T(8,128)} %param.11) | copy-start | bytes 786436
  9.9 30.8 %collective-permute-start = (f32[4,9,16,256]{3,2,1,0:T(8,128)}, f32[4,9,16,256]{3,2,1,0:T(8,128)}, u32[]{:S(2)}, u32[]{:S(2)}) collective-permute-start(f32[4,9,16,256]{3,2,1,0:T(8,128)} %get-tuple-element.16), channel_id=1, source_target_pairs={{0,1},{1,2},{2,3},{3,4},{4,5},{5,6},{6,7},{8,9},{9,10},{10,11},{11... | collective-permute-start | bytes 1769480 | tf_op jit(solution)/shard_map/ppermute | solution.py:24
  14.5 26.2 %collective-permute-start.1 = (f32[4,9,16,256]{3,2,1,0:T(8,128)}, f32[4,9,16,256]{3,2,1,0:T(8,128)}, u32[]{:S(2)}, u32[]{:S(2)}) collective-permute-start(f32[4,9,16,256]{3,2,1,0:T(8,128)} %get-tuple-element.17), channel_id=1, source_target_pairs={{1,0},{2,1},{3,2},{4,3},{5,4},{6,5},{7,6},{9,8},{10,9},{11,10},{12... | collective-permute-start | bytes 1769480 | tf_op jit(solution)/shard_map/ppermute | solution.py:26
  17.7 28.3 %copy-start.14 = (f32[24]{0:T(128)}, f32[24]{0:T(128)S(1)}, u32[]{:S(2)}) copy-start(f32[24]{0:T(128)S(1)} %slice.272) | copy-start | bytes 292
  31.0 29.0 %collective-permute-start.7 = (f32[3,9,16,256]{3,2,1,0:T(8,128)}, f32[3,9,16,256]{3,2,1,0:T(8,128)}, u32[]{:S(2)}, u32[]{:S(2)}) collective-permute-start(f32[3,9,16,256]{3,2,1,0:T(8,128)} %get-tuple-element.33), channel_id=1, source_target_pairs={{0,1},{1,2},{2,3},{3,4},{4,5},{5,6},{6,7},{8,9},{9,10},{10,11},{11... | collective-permute-start | bytes 1327112 | tf_op jit(solution)/shard_map/ppermute | solution.py:24
  34.5 25.6 %collective-permute-start.8 = (f32[3,9,16,256]{3,2,1,0:T(8,128)}, f32[3,9,16,256]{3,2,1,0:T(8,128)}, u32[]{:S(2)}, u32[]{:S(2)}) collective-permute-start(f32[3,9,16,256]{3,2,1,0:T(8,128)} %get-tuple-element.34), channel_id=1, source_target_pairs={{1,0},{2,1},{3,2},{4,3},{5,4},{6,5},{7,6},{9,8},{10,9},{11,10},{12... | collective-permute-start | bytes 1327112 | tf_op jit(solution)/shard_map/ppermute | solution.py:26
  42.9 4.3 %copy-start = (f32[6,32,16,256]{3,2,1,0:T(8,128)}, f32[6,32,16,256]{3,2,1,0:T(8,128)S(1)}, u32[]{:S(2)}) copy-start(f32[6,32,16,256]{3,2,1,0:T(8,128)S(1)} %fusion.55.k_ref) | copy-start | bytes 9437188
  51.1 41.7 %collective-permute-start.2 = (f32[2,5,16,256]{3,2,1,0:T(8,128)}, f32[2,5,16,256]{3,2,1,0:T(8,128)}, u32[]{:S(2)}, u32[]{:S(2)}) collective-permute-start(f32[2,5,16,256]{3,2,1,0:T(8,128)} %get-tuple-element.35), channel_id=1, source_target_pairs={{0,1},{1,2},{2,3},{3,4},{4,5},{5,6},{6,7},{8,9},{9,10},{10,11},{11... | collective-permute-start | bytes 491528 | tf_op jit(solution)/shard_map/ppermute | solution.py:24
  55.6 37.2 %collective-permute-start.3 = (f32[2,5,16,256]{3,2,1,0:T(8,128)S(1)}, f32[2,5,16,256]{3,2,1,0:T(8,128)}, u32[]{:S(2)}, u32[]{:S(2)}) collective-permute-start(f32[2,5,16,256]{3,2,1,0:T(8,128)S(1)} %get-tuple-element.36), channel_id=1, source_target_pairs={{1,0},{2,1},{3,2},{4,3},{5,4},{6,5},{7,6},{9,8},{10,9},{11,10},{12... | collective-permute-start | bytes 491528 | tf_op jit(solution)/shard_map/ppermute | solution.py:26
  85.3 14.6 %collective-permute-start.10 = (f32[6,5,16,256]{3,2,1,0:T(8,128)S(1)}, f32[6,5,16,256]{3,2,1,0:T(8,128)S(1)}, u32[]{:S(2)}, u32[]{:S(2)}) collective-permute-start(f32[6,5,16,256]{3,2,1,0:T(8,128)S(1)} %get-tuple-element.8), channel_id=1, source_target_pairs={{1,0},{2,1},{3,2},{4,3},{5,4},{6,5},{7,6},{9,8},{10,9},{11,10},{12... | collective-permute-start | bytes 1474568 | tf_op jit(solution)/shard_map/ppermute | solution.py:26
  87.2 12.7 %collective-permute-start.9 = (f32[6,5,16,256]{3,2,1,0:T(8,128)S(1)}, f32[6,5,16,256]{3,2,1,0:T(8,128)}, u32[]{:S(2)}, u32[]{:S(2)}) collective-permute-start(f32[6,5,16,256]{3,2,1,0:T(8,128)S(1)} %get-tuple-element.7), channel_id=1, source_target_pairs={{0,1},{1,2},{2,3},{3,4},{4,5},{5,6},{6,7},{8,9},{9,10},{10,11},{11... | collective-permute-start | bytes 1474568 | tf_op jit(solution)/shard_map/ppermute | solution.py:24
  113.4 2.2 %copy-start.4 = (f32[16,16,256]{2,1,0:T(8,128)S(1)}, f32[16,16,256]{2,1,0:T(8,128)}, u32[]{:S(2)}) copy-start(f32[16,16,256]{2,1,0:T(8,128)} %get-tuple-element.50) | copy-start | bytes 786436
  113.4 2.2 %copy-start.5 = (f32[16,16,256]{2,1,0:T(8,128)S(1)}, f32[16,16,256]{2,1,0:T(8,128)}, u32[]{:S(2)}) copy-start(f32[16,16,256]{2,1,0:T(8,128)} %get-tuple-element.51) | copy-start | bytes 786436
  113.5 2.2 %copy-start.6 = (f32[16,16,256]{2,1,0:T(8,128)S(1)}, f32[16,16,256]{2,1,0:T(8,128)}, u32[]{:S(2)}) copy-start(f32[16,16,256]{2,1,0:T(8,128)} %get-tuple-element.52) | copy-start | bytes 786436
  113.5 2.2 %copy-start.7 = (f32[16,16,256]{2,1,0:T(8,128)S(1)}, f32[16,16,256]{2,1,0:T(8,128)}, u32[]{:S(2)}) copy-start(f32[16,16,256]{2,1,0:T(8,128)} %get-tuple-element.53) | copy-start | bytes 786436
  113.5 2.2 %copy-start.8 = (f32[16,16,256]{2,1,0:T(8,128)S(1)}, f32[16,16,256]{2,1,0:T(8,128)}, u32[]{:S(2)}) copy-start(f32[16,16,256]{2,1,0:T(8,128)} %get-tuple-element.47) | copy-start | bytes 786436
  113.5 2.2 %copy-start.9 = (f32[16,16,256]{2,1,0:T(8,128)S(1)}, f32[16,16,256]{2,1,0:T(8,128)}, u32[]{:S(2)}) copy-start(f32[16,16,256]{2,1,0:T(8,128)} %get-tuple-element.44) | copy-start | bytes 786436
  113.5 2.2 %copy-start.10 = (f32[16,16,256]{2,1,0:T(8,128)S(1)}, f32[16,16,256]{2,1,0:T(8,128)}, u32[]{:S(2)}) copy-start(f32[16,16,256]{2,1,0:T(8,128)} %get-tuple-element.45) | copy-start | bytes 786436
  (3 other events, 4.6 us)

commit v2 on v1

--- a/solution.py
+++ b/solution.py
@@ -270,8 +270,7 @@
             )
         return solution + direction, halo
 
-    def chain(rech_ext, well_rows, rate_rows):
-        count = rech_ext.shape[0]
+    def begin(rech_ext, well_rows, rate_rows):
         hits = well_rows[:, :, None, None, None] == flat[None, None]
         points = jnp.sum(jnp.where(hits, rate_rows[:, :, None, None, None], 0.0), axis=1)
         own_hits = hits[:, :, reach : reach + slab]
@@ -280,20 +279,22 @@
         state, state_halo = solve(rech_ext + points, reach)
         forcing = -diffuse(rows_of(scaled_ext, state_halo)[None], state[:, None])
         forcing = forcing * rows_of(mask_ext, state_halo - 1)
-        forcing = forcing.reshape(count * cols, slab + 2 * CHEB, rows_y, depth_z)
-        change, _ = solve(forcing, CHEB)
-        weighted = (
-            change.reshape(count, cols, slab, rows_y, depth_z) * observe[:, None]
-        ).reshape(count * cols, slab, rows_y, depth_z)
-        weighted_ext = with_halo(weighted, "cell", 1, CHEB + 1)
-        adjoint, _ = solve(weighted_ext, CHEB + 1)
-        adjoint = adjoint.reshape(count, cols, slab + 2, rows_y, depth_z)
         state = lax.slice_in_dim(state, CHEB, state.shape[1] - CHEB, axis=1)
-        return jnp.sum(pairs(state[:, None], adjoint), axis=0)
-
-    contrib = chain(rech_own, wells, rates)
+        return state, forcing, observe
+
+    parts_of = [begin(rech_own, wells, rates)]
     if tests > tests_here:
-        contrib = contrib + chain(rech_others, wells_others, rates_others)
+        parts_of.append(begin(rech_others, wells_others, rates_others))
+    state, forcing, observe = (jnp.concatenate(group, axis=0) for group in zip(*parts_of))
+    forcing = forcing.reshape(tests * cols, slab + 2 * CHEB, rows_y, depth_z)
+    change, _ = solve(forcing, CHEB)
+    weighted = (
+        change.reshape(tests, cols, slab, rows_y, depth_z) * observe[:, None]
+    ).reshape(tests * cols, slab, rows_y, depth_z)
+    weighted_ext = with_halo(weighted, "cell", 1, CHEB + 1)
+    adjoint, _ = solve(weighted_ext, CHEB + 1)
+    adjoint = adjoint.reshape(tests, cols, slab + 2, rows_y, depth_z)
+    contrib = jnp.sum(pairs(state[:, None], adjoint), axis=0)
     return -0.5 * perm[None] * contrib
 
 

time: 118 us -> 118 us (level)
  starting transfers between devices: 29.4 us -> 24.4 us
  waiting for transfers between devices: 12.8 us -> 16.8 us
    ppermute x4 -> x3, waiting for transfers between devices: 2.06 us -> 10.7 us  [with_halo(): lax.ppermute(head, axis, [(i + 1, i) for i in range(ends)])]
    ppermute x4 -> x3, starting transfers between devices: 17.5 us -> 11.2 us  [with_halo(): lax.ppermute(tail, axis, [(i, i + 1) for i in range(ends)])]
    ppermute x3, waiting for transfers between devices: 10.7 us -> 6.09 us  [shards(): lax.ppermute(packed, 'test', [(i, (i + shift) % groups) for i in range(gr...]
    mul x3, other arithmetic: 0.81 us -> 3.32 us  [the longest x2 2.97 us: begin(): forcing = forcing * rows_of(mask_ext, state_halo - 1)]
    concatenate x3 -> x2, other arithmetic: 4.08 us -> 2.31 us  [with_halo(): jnp.concatenate([lax.ppermute(tail, axis, [(i, i + 1) for i in range(ends...]
    neg x1 -> x0, other arithmetic: 1.53 us -> none  [chain(): forcing = -diffuse(rows_of(scaled_ext, state_halo)[None], state[:, None])]
    reduce_sum x5, other arithmetic: 4.87 us -> 6.17 us  [the longest x1 2.66 us: shards(): contrib = jnp.sum(pairs(state[:, None], adjoint), axis=0)]
    reshape x1 -> x0, other arithmetic: 1.2 us -> none  [chain(): forcing = forcing.reshape(count * cols, slab + 2 * CHEB, rows_y, depth_z)]
  transfers between devices with their start and end apart: 11 -> 9, of which waited for: 3 -> 3; matrix products, arithmetic and copies ran while one was open for 21% -> 16% of each run, Pallas kernels for 25% -> 2%
where the time goes in v2:
time: 118 us; the launch traced here: 116 us
  Pallas kernels  41.9 us (36%)
  other arithmetic  27.2 us (23%)
  starting transfers between devices  24.4 us (21%)
  waiting for transfers between devices  16.8 us (14%)
  local copies, waits for them, and re-layouts  5.69 us (5%)
    pallas_call x4, Pallas kernels, kernel_solve(): pl.pallas_call(body, grid=(fields,), in_specs=[pl.BlockSpec((1, rows, row...  41.9 us
    ppermute x3, starting transfers between devices, with_halo(): lax.ppermute(tail, axis, [(i, i + 1) for i in range(ends)])  11.2 us
    ppermute x3, waiting for transfers between devices, with_halo(): lax.ppermute(head, axis, [(i + 1, i) for i in range(ends)])  10.7 us
    ppermute x3, starting transfers between devices, with_halo(): lax.ppermute(head, axis, [(i + 1, i) for i in range(ends)])  8.45 us
    ppermute x3, waiting for transfers between devices, shards(): lax.ppermute(packed, 'test', [(i, (i + shift) % groups) for i in range(gr...  6.09 us
    ppermute x3, starting transfers between devices, shards(): lax.ppermute(packed, 'test', [(i, (i + shift) % groups) for i in range(gr...  4.71 us
    eq x2, other arithmetic, begin(): hits = well_rows[:, :, None, None, None] == flat[None, None]  3.09 us
    mul x2, other arithmetic, begin(): forcing = forcing * rows_of(mask_ext, state_halo - 1)  2.97 us
  transfers between devices with their start and end apart: 9, of which 3 were waited for; matrix products, arithmetic and copies ran while one was open for 16% of the time, Pallas kernels for 2%

profile of v2, /device:TPU:11, one launch (start us, length us, event | category | flops | bytes accessed | tf_op | source)
XLA Modules:
  0.0 116.4 jit_solution(6421466362748240995)
XLA Ops:
  0.0 1.3 %copy.7 = f32[1,1,256,256]{3,1,2,0:T(1,128)S(1)} copy(f32[1,1,256,256]{3,2,1,0:T(8,128)} %bitcast.98) | data formatting | bytes 524288
  3.1 2.3 %collective-permute-start.3 = (f32[1,65552]{1,0:T(1,128)S(1)}, f32[1,65552]{1,0:T(1,128)S(1)}, u32[]{:S(2)}, u32[]{:S(2)}) collective-permute-start(f32[1,65552]{1,0:T(1,128)S(1)} %dynamic-update-slice.2), channel_id=1, source_target_pairs={{0,16},{8,24},{16,0},{24,8},{1,17},{9,25},{17,1},{25,9},{2,18},{10... | collective-permute-start | bytes 786632 | tf_op jit(solution)/shard_map/ppermute | solution.py:222
  5.4 2.2 %collective-permute-start.2 = (f32[1,65552]{1,0:T(1,128)S(1)}, f32[1,65552]{1,0:T(1,128)S(1)}, u32[]{:S(2)}, u32[]{:S(2)}) collective-permute-start(f32[1,65552]{1,0:T(1,128)S(1)} %dynamic-update-slice.2), channel_id=1, source_target_pairs={{0,8},{8,16},{16,24},{24,0},{1,9},{9,17},{17,25},{25,1},{2,10},{10... | collective-permute-start | bytes 786632 | tf_op jit(solution)/shard_map/ppermute | solution.py:222
  7.6 1.7 %broadcast_multiply_fusion.2 = (f32[16,16,256]{2,1,0:T(8,128)}, f32[1,16,16,256]{3,2,1,0:T(8,128)S(1)}, f32[16,16,256]{2,1,0:T(8,128)S(1)}) fusion(f32[16,16,256]{2,1,0:T(8,128)} %param.6), kind=kLoop, calls=%fused_computation.143 | loop fusion | flops 65536 | bytes 1048576 | tf_op jit(solution)/shard_map/mul | solution.py:298
  10.7 3.4 %collective-permute-start.1 = (f32[4,9,16,256]{3,2,1,0:T(8,128)}, f32[4,9,16,256]{3,2,1,0:T(8,128)S(1)}, u32[]{:S(2)}, u32[]{:S(2)}) collective-permute-start(f32[4,9,16,256]{3,2,1,0:T(8,128)} %get-tuple-element.24), channel_id=1, source_target_pairs={{1,0},{2,1},{3,2},{4,3},{5,4},{6,5},{7,6},{9,8},{10,9},{11,10},{12... | collective-permute-start | bytes 1769480 | tf_op jit(solution)/shard_map/ppermute | solution.py:26
  14.1 3.2 %collective-permute-start = (f32[4,9,16,256]{3,2,1,0:T(8,128)}, f32[4,9,16,256]{3,2,1,0:T(8,128)S(1)}, u32[]{:S(2)}, u32[]{:S(2)}) collective-permute-start(f32[4,9,16,256]{3,2,1,0:T(8,128)} %get-tuple-element.23), channel_id=1, source_target_pairs={{0,1},{1,2},{2,3},{3,4},{4,5},{5,6},{6,7},{8,9},{9,10},{10,11},{11... | collective-permute-start | bytes 1769480 | tf_op jit(solution)/shard_map/ppermute | solution.py:24
  18.7 1.3 %broadcast_compare_fusion.1 = pred[1,8,34,16,256]{4,3,2,1,0:T(8,128)(4,1)S(1)} fusion(s32[34,16,256]{2,1,0:T(8,128)S(1)} %iota_add_fusion, s32[8]{0:T(128)} %bitcast.100), kind=kLoop, calls=%fused_computation.12 | loop fusion | flops 1114112 | bytes 1671200 | tf_op jit(solution)/shard_map/eq | solution.py:274
  22.1 5.6 %collective-permute-done.2 = f32[1,65552]{1,0:T(1,128)S(1)} collective-permute-done((f32[1,65552]{1,0:T(1,128)S(1)}, f32[1,65552]{1,0:T(1,128)S(1)}, u32[]{:S(2)}, u32[]{:S(2)}) %collective-permute-start.2) | collective-permute-done | bytes 262240 | tf_op jit(solution)/shard_map/ppermute | solution.py:222
  29.7 3.1 %collective-permute-start.6 = (f32[3,9,16,256]{3,2,1,0:T(8,128)}, f32[3,9,16,256]{3,2,1,0:T(8,128)}, u32[]{:S(2)}, u32[]{:S(2)}) collective-permute-start(f32[3,9,16,256]{3,2,1,0:T(8,128)} %get-tuple-element.34), channel_id=1, source_target_pairs={{1,0},{2,1},{3,2},{4,3},{5,4},{6,5},{7,6},{9,8},{10,9},{11,10},{12... | collective-permute-start | bytes 1327112 | tf_op jit(solution)/shard_map/ppermute | solution.py:26
  32.8 3.5 %collective-permute-start.5 = (f32[3,9,16,256]{3,2,1,0:T(8,128)}, f32[3,9,16,256]{3,2,1,0:T(8,128)}, u32[]{:S(2)}, u32[]{:S(2)}) collective-permute-start(f32[3,9,16,256]{3,2,1,0:T(8,128)} %get-tuple-element.33), channel_id=1, source_target_pairs={{0,1},{1,2},{2,3},{3,4},{4,5},{5,6},{6,7},{8,9},{9,10},{10,11},{11... | collective-permute-start | bytes 1327112 | tf_op jit(solution)/shard_map/ppermute | solution.py:24
  36.4 1.8 %broadcast_compare_fusion = pred[3,8,34,16,256]{4,3,2,1,0:T(8,128)(4,1)S(1)} fusion(s32[34,16,256]{2,1,0:T(8,128)S(1)} %iota_add_fusion, s32[3,8]{1,0:T(4,128)S(1)} %get-tuple-element.28), kind=kLoop, calls=%fused_computation.1 | loop fusion | flops 3342336 | bytes 3899488 | tf_op jit(solution)/shard_map/eq | solution.py:274
  39.1 1.4 %select_reduce_fusion = f32[3,34,16,256]{3,2,1,0:T(8,128)S(1)} fusion(f32[3,8]{1,0:T(4,128)S(1)} %get-tuple-element.29, s32[34,16,256]{2,1,0:T(8,128)S(1)} %iota_add_fusion, s32[3,8]{1,0:T(4,128)S(1)} %get-tuple-element.28), kind=kLoop, calls=%fused_computation | loop fusion | flops 9609216 | bytes 2228416 | tf_op jit(solution)/shard_map/reduce_sum | solution.py:275
  41.8 2.5 %shard_map.64 = f32[1,26,16,256]{3,2,1,0:T(8,128)S(1)} custom-call(f32[1,34,16,256]{3,2,1,0:T(8,128)S(1)} %slice_add_fusion.2.b_ref, f32[6,32,16,256]{3,2,1,0:T(8,128)S(1)} %fusion.55.k_ref, f32[34,16,256]{2,1,0:T(8,128)S(1)} %broadcast_in_dim.68.m_ref), custom_call_target="tpu_custom_call" | custom-call | tf_op jit(solution)/shard_map/pallas_call | solution.py:92
  46.0 1.4 %negate_multiply_fusion.1 = (f32[1,2,24,16,256]{4,3,2,1,0:T(8,128)S(1)}, f32[2,24,16,256]{3,2,1,0:T(8,128)S(1)}, f32[2,24,16,256]{3,2,1,0:T(8,128)S(1)}, f32[2,2...) fusion(f32[24]{0:T(128)S(1)} %slice.230, ...), kind=kLoop, calls=%fused_computation.91 | loop fusion | flops 5701632 | bytes 10223712 | tf_op jit(solution)/shard_map/mul | solution.py:281
  47.4 1.5 %maximum_add_fusion.b_ref = f32[3,34,16,256]{3,2,1,0:T(8,128)S(1)} fusion(f32[3,34,16,256]{3,2,1,0:T(8,128)S(1)} %select_reduce_fusion, f32[3,9,16,256]{3,2,1,0:T(8,128)} %collective-permute-done.6, f32[3,16,16,256]{3,2,1,0:T(8,128)S(1)} %bitcast.96, f32[3,9,16,256]{3,2,1,0:T(8,128)} %collective-permute-done.5), kind=kLoop, calls=%fused_computation.41 | loop fusion | flops 1253376 | bytes 5013504 | tf_op jit(solution)/shard_map/add | solution.py:279
  49.0 9.1 %shard_map.65 = f32[3,26,16,256]{3,2,1,0:T(8,128)S(1)} custom-call(f32[3,34,16,256]{3,2,1,0:T(8,128)S(1)} %maximum_add_fusion.b_ref, f32[6,32,16,256]{3,2,1,0:T(8,128)} %copy-done, f32[34,16,256]{2,1,0:T(8,128)S(1)} %broadcast_in_dim.68.m_ref), custom_call_target="tpu_custom_call" | custom-call | tf_op jit(solution)/shard_map/pallas_call | solution.py:92
  59.7 1.5 %negate_multiply_fusion = f32[3,2,24,16,256]{4,3,2,1,0:T(8,128)S(1)} fusion(f32[24]{0:T(128)S(1)} %slice.230, f32[3,24,16,256]{3,2,1,0:T(8,128)S(1)} %get-tuple-element.17, f32[2,24,16,256]{3,2,1,0:T(8,128)S(1)} %copy-done.2, f32[3,24,16,256]{3,2,1,0:T(8,128)S(1)} %get-tuple-element.16, f32[2,24,16,256]{3,2,1,0:T(8,128)S(1)} %get-tuple-element.32, ...), kind=kLoop, calls=%fused_computation.10 | loop fusion | flops 7667712 | bytes 14155872 | tf_op jit(solution)/shard_map/mul | solution.py:281
  61.6 14.6 %shard_map.66 = f32[8,16,16,256]{3,2,1,0:T(8,128)S(1)} custom-call(f32[8,24,16,256]{3,2,1,0:T(8,128)S(1)} %bitcast.93, f32[6,32,16,256]{3,2,1,0:T(8,128)} %copy-done, f32[34,16,256]{2,1,0:T(8,128)S(1)} %broadcast_in_dim.68.m_ref), custom_call_target="tpu_custom_call" | custom-call | tf_op jit(solution)/shard_map/pallas_call | solution.py:92
  76.7 1.9 %collective-permute-start.8 = (f32[8,5,16,256]{3,2,1,0:T(8,128)S(1)}, f32[8,5,16,256]{3,2,1,0:T(8,128)S(1)}, u32[]{:S(2)}, u32[]{:S(2)}) collective-permute-start(f32[8,5,16,256]{3,2,1,0:T(8,128)S(1)} %get-tuple-element.8), channel_id=1, source_target_pairs={{1,0},{2,1},{3,2},{4,3},{5,4},{6,5},{7,6},{9,8},{10,9},{11,10},{12... | collective-permute-start | bytes 1966088 | tf_op jit(solution)/shard_map/ppermute | solution.py:26
  78.6 4.5 %collective-permute-start.7 = (f32[8,5,16,256]{3,2,1,0:T(8,128)S(1)}, f32[8,5,16,256]{3,2,1,0:T(8,128)S(1)}, u32[]{:S(2)}, u32[]{:S(2)}) collective-permute-start(f32[8,5,16,256]{3,2,1,0:T(8,128)S(1)} %get-tuple-element.7), channel_id=1, source_target_pairs={{0,1},{1,2},{2,3},{3,4},{4,5},{5,6},{6,7},{8,9},{9,10},{10,11},{11... | collective-permute-start | bytes 1966088 | tf_op jit(solution)/shard_map/ppermute | solution.py:24
  84.3 10.6 %collective-permute-done.8 = f32[8,5,16,256]{3,2,1,0:T(8,128)S(1)} collective-permute-done((f32[8,5,16,256]{3,2,1,0:T(8,128)S(1)}, f32[8,5,16,256]{3,2,1,0:T(8,128)S(1)}, u32[]{:S(2)}, u32[]{:S(2)}) %collective-permute-start.8) | collective-permute-done | bytes 655392 | tf_op jit(solution)/shard_map/ppermute | solution.py:26
  94.9 2.1 %pad_maximum_fusion.b_ref = f32[8,26,16,256]{3,2,1,0:T(8,128)} fusion(f32[8,5,16,256]{3,2,1,0:T(8,128)S(1)} %collective-permute-done.8, f32[8,16,16,256]{3,2,1,0:T(8,128)S(1)} %bitcast_multiply_fusion, f32[8,5,16,256]{3,2,1,0:T(8,128)S(1)} %collective-permute-done.7), kind=kLoop, calls=%fused_computation.8 | loop fusion | flops 1703936 | bytes 6815744 | tf_op jit(solution)/shard_map/concatenate | solution.py:22
  97.0 15.6 %shard_map.67 = f32[8,18,16,256]{3,2,1,0:T(8,128)S(1)} custom-call(f32[8,26,16,256]{3,2,1,0:T(8,128)} %pad_maximum_fusion.b_ref, f32[6,32,16,256]{3,2,1,0:T(8,128)S(1)} %copy-done.1, f32[34,16,256]{2,1,0:T(8,128)S(1)} %broadcast_in_dim.68.m_ref), custom_call_target="tpu_custom_call" | custom-call | tf_op jit(solution)/shard_map/pallas_call | solution.py:92
  112.8 2.7 %fusion.6 = f32[2,16,16,256]{3,2,1,0:T(8,128)S(1)} fusion(f32[4,2,16,16,256]{4,3,2,1,0:T(8,128)S(1)} %slice.281, f32[4,2,18,16,256]{4,3,2,1,0:T(8,128)S(1)} %bitcast.91, f32[4,16,16,256]{3,2,1,0:T(8,128)S(1)} %get-tuple-element.21, f32[4,16,16,256]{3,2,1,0:T(8,128)S(1)} %get-tuple-element.20, f32[4,16,16,256]{3,2,1,0:T(8,128)S(1)} %get-tuple-element.22, ...), kind=kLoop, calls=%fused_computation.19 | loop fusion | flops 9306112 | bytes 13107200 | tf_op jit(solution)/shard_map/reduce_sum | solution.py:297
  (72 shorter events, 16.8 us)
Async XLA Ops:
  0.0 9.5 %copy-start.3 = (f32[1,16,16,256]{3,2,1,0:T(8,128)S(1)}, f32[1,16,16,256]{3,2,1,0:T(8,128)}, u32[]{:S(2)}) copy-start(f32[1,16,16,256]{3,2,1,0:T(8,128)} %param.10) | copy-start | bytes 786436
  0.0 9.4 %copy-start.6 = (f32[2,16,16,256]{3,2,1,0:T(8,128)S(1)}, f32[2,16,16,256]{3,2,1,0:T(8,128)}, u32[]{:S(2)}) copy-start(f32[2,16,16,256]{3,2,1,0:T(8,128)} %param.7) | copy-start | bytes 1572868
  2.9 18.7 %collective-permute-start.4 = (f32[1,65552]{1,0:T(1,128)S(1)}, f32[1,65552]{1,0:T(1,128)S(1)}, u32[]{:S(2)}, u32[]{:S(2)}) collective-permute-start(f32[1,65552]{1,0:T(1,128)S(1)} %dynamic-update-slice.2), channel_id=1, source_target_pairs={{0,24},{8,0},{16,8},{24,16},{1,25},{9,1},{17,9},{25,17},{2,26},{10... | collective-permute-start | bytes 786632 | tf_op jit(solution)/shard_map/ppermute | solution.py:222
  3.1 18.9 %collective-permute-start.3 = (f32[1,65552]{1,0:T(1,128)S(1)}, f32[1,65552]{1,0:T(1,128)S(1)}, u32[]{:S(2)}, u32[]{:S(2)}) collective-permute-start(f32[1,65552]{1,0:T(1,128)S(1)} %dynamic-update-slice.2), channel_id=1, source_target_pairs={{0,16},{8,24},{16,0},{24,8},{1,17},{9,25},{17,1},{25,9},{2,18},{10... | collective-permute-start | bytes 786632 | tf_op jit(solution)/shard_map/ppermute | solution.py:222
  5.4 22.2 %collective-permute-start.2 = (f32[1,65552]{1,0:T(1,128)S(1)}, f32[1,65552]{1,0:T(1,128)S(1)}, u32[]{:S(2)}, u32[]{:S(2)}) collective-permute-start(f32[1,65552]{1,0:T(1,128)S(1)} %dynamic-update-slice.2), channel_id=1, source_target_pairs={{0,8},{8,16},{16,24},{24,0},{1,9},{9,17},{17,25},{25,1},{2,10},{10... | collective-permute-start | bytes 786632 | tf_op jit(solution)/shard_map/ppermute | solution.py:222
  10.7 29.8 %collective-permute-start.1 = (f32[4,9,16,256]{3,2,1,0:T(8,128)}, f32[4,9,16,256]{3,2,1,0:T(8,128)S(1)}, u32[]{:S(2)}, u32[]{:S(2)}) collective-permute-start(f32[4,9,16,256]{3,2,1,0:T(8,128)} %get-tuple-element.24), channel_id=1, source_target_pairs={{1,0},{2,1},{3,2},{4,3},{5,4},{6,5},{7,6},{9,8},{10,9},{11,10},{12... | collective-permute-start | bytes 1769480 | tf_op jit(solution)/shard_map/ppermute | solution.py:26
  14.1 7.4 %copy-start.4 = (f32[16,16,256]{2,1,0:T(8,128)S(1)}, f32[16,16,256]{2,1,0:T(8,128)}, u32[]{:S(2)}) copy-start(f32[16,16,256]{2,1,0:T(8,128)} %param.11) | copy-start | bytes 786436
  14.1 26.4 %collective-permute-start = (f32[4,9,16,256]{3,2,1,0:T(8,128)}, f32[4,9,16,256]{3,2,1,0:T(8,128)S(1)}, u32[]{:S(2)}, u32[]{:S(2)}) collective-permute-start(f32[4,9,16,256]{3,2,1,0:T(8,128)} %get-tuple-element.23), channel_id=1, source_target_pairs={{0,1},{1,2},{2,3},{3,4},{4,5},{5,6},{6,7},{8,9},{9,10},{10,11},{11... | collective-permute-start | bytes 1769480 | tf_op jit(solution)/shard_map/ppermute | solution.py:24
  29.7 17.7 %collective-permute-start.6 = (f32[3,9,16,256]{3,2,1,0:T(8,128)}, f32[3,9,16,256]{3,2,1,0:T(8,128)}, u32[]{:S(2)}, u32[]{:S(2)}) collective-permute-start(f32[3,9,16,256]{3,2,1,0:T(8,128)} %get-tuple-element.34), channel_id=1, source_target_pairs={{1,0},{2,1},{3,2},{4,3},{5,4},{6,5},{7,6},{9,8},{10,9},{11,10},{12... | collective-permute-start | bytes 1327112 | tf_op jit(solution)/shard_map/ppermute | solution.py:26
  32.8 14.6 %collective-permute-start.5 = (f32[3,9,16,256]{3,2,1,0:T(8,128)}, f32[3,9,16,256]{3,2,1,0:T(8,128)}, u32[]{:S(2)}, u32[]{:S(2)}) collective-permute-start(f32[3,9,16,256]{3,2,1,0:T(8,128)} %get-tuple-element.33), channel_id=1, source_target_pairs={{0,1},{1,2},{2,3},{3,4},{4,5},{5,6},{6,7},{8,9},{9,10},{10,11},{11... | collective-permute-start | bytes 1327112 | tf_op jit(solution)/shard_map/ppermute | solution.py:24
  41.6 2.8 %copy-start = (f32[6,32,16,256]{3,2,1,0:T(8,128)}, f32[6,32,16,256]{3,2,1,0:T(8,128)S(1)}, u32[]{:S(2)}) copy-start(f32[6,32,16,256]{3,2,1,0:T(8,128)S(1)} %fusion.55.k_ref) | copy-start | bytes 9437188
  58.6 1.1 copy-start.2
  76.7 18.2 %collective-permute-start.8 = (f32[8,5,16,256]{3,2,1,0:T(8,128)S(1)}, f32[8,5,16,256]{3,2,1,0:T(8,128)S(1)}, u32[]{:S(2)}, u32[]{:S(2)}) collective-permute-start(f32[8,5,16,256]{3,2,1,0:T(8,128)S(1)} %get-tuple-element.8), channel_id=1, source_target_pairs={{1,0},{2,1},{3,2},{4,3},{5,4},{6,5},{7,6},{9,8},{10,9},{11,10},{12... | collective-permute-start | bytes 1966088 | tf_op jit(solution)/shard_map/ppermute | solution.py:26
  78.6 16.3 %collective-permute-start.7 = (f32[8,5,16,256]{3,2,1,0:T(8,128)S(1)}, f32[8,5,16,256]{3,2,1,0:T(8,128)S(1)}, u32[]{:S(2)}, u32[]{:S(2)}) collective-permute-start(f32[8,5,16,256]{3,2,1,0:T(8,128)S(1)} %get-tuple-element.7), channel_id=1, source_target_pairs={{0,1},{1,2},{2,3},{3,4},{4,5},{5,6},{6,7},{8,9},{9,10},{10,11},{11... | collective-permute-start | bytes 1966088 | tf_op jit(solution)/shard_map/ppermute | solution.py:24
  84.3 12.7 %copy-start.1 = (f32[6,32,16,256]{3,2,1,0:T(8,128)S(1)}, f32[6,32,16,256]{3,2,1,0:T(8,128)}, u32[]{:S(2)}) copy-start(f32[6,32,16,256]{3,2,1,0:T(8,128)} %copy-done) | copy-start | bytes 9437188
  112.8 2.7 %copy-start.5 = (f32[16,16,256]{2,1,0:T(8,128)S(1)}, f32[16,16,256]{2,1,0:T(8,128)}, u32[]{:S(2)}) copy-start(f32[16,16,256]{2,1,0:T(8,128)} %get-tuple-element.42) | copy-start | bytes 786436

commit v3 on v2

--- a/solution.py
+++ b/solution.py
@@ -38,10 +38,7 @@
     iz = lax.broadcasted_iota(jnp.int32, (rows_y, depth_z), 1)
 
     def init(r, c):
-        value = b_ref[0, r]
-        res[r] = value
-        da[r] = value * first
-        sol[r] = jnp.zeros_like(value)
+        da[r] = b_ref[0, r] * first
         return c
 
     lax.fori_loop(0, rows, init, 0, unroll=True)
@@ -52,7 +49,7 @@
         keep = keeps[turn]
         push = pushes[turn]
 
-        def step(r, c, src=src, dst=dst, keep=keep, push=push):
+        def step(r, c, turn=turn, src=src, dst=dst, keep=keep, push=push):
             here = src[r]
             face = r - 1 + offset
             total = k_ref[0, face] * (here - src[r + 1])
@@ -64,20 +61,22 @@
             down = jnp.where(iz > 0, pltpu.roll(here, 1, 1), 0.0)
             total = total + k_ref[4, face] * (here - up) + k_ref[5, face] * (here - down)
             image = storage * here + total
-            sol[r] = sol[r] + here
-            fresh = res[r] - image
-            res[r] = fresh
-            dst[r] = (keep * here + push * fresh) * m_ref[r + offset]
+            if turn == 0:
+                summed = here
+                fresh = b_ref[0, r] - image
+            else:
+                summed = sol[r] + here
+                fresh = res[r] - image
+            after = (keep * here + push * fresh) * m_ref[r + offset]
+            if turn == CHEB - 1:
+                o_ref[0, r - CHEB] = summed + after
+            else:
+                sol[r] = summed
+                res[r] = fresh
+                dst[r] = after
             return c
 
         lax.fori_loop(turn + 1, rows - 1 - turn, step, 0, unroll=True)
-    final = bufs[CHEB % 2]
-
-    def out(r, c):
-        o_ref[0, r - CHEB] = sol[r] + final[r]
-        return c
-
-    lax.fori_loop(CHEB, rows - CHEB, out, 0, unroll=True)
 
 
 def kernel_solve(right_side, face_stack, mask_full, offset, first, keeps, pushes):

time: 118 us -> 118 us (level)
  no operation moved by 1% of the time
where the time goes in v3:
time: 118 us; the launch traced here: 116 us
  Pallas kernels  41.9 us (36%)
  other arithmetic  27.2 us (23%)
  starting transfers between devices  24.4 us (21%)
  waiting for transfers between devices  16.8 us (14%)
  local copies, waits for them, and re-layouts  5.69 us (5%)
    pallas_call x4, Pallas kernels, kernel_solve(): pl.pallas_call(body, grid=(fields,), in_specs=[pl.BlockSpec((1, rows, row...  41.9 us
    ppermute x3, starting transfers between devices, with_halo(): lax.ppermute(tail, axis, [(i, i + 1) for i in range(ends)])  11.2 us
    ppermute x3, waiting for transfers between devices, with_halo(): lax.ppermute(head, axis, [(i + 1, i) for i in range(ends)])  10.7 us
    ppermute x3, starting transfers between devices, with_halo(): lax.ppermute(head, axis, [(i + 1, i) for i in range(ends)])  8.45 us
    ppermute x3, waiting for transfers between devices, shards(): lax.ppermute(packed, 'test', [(i, (i + shift) % groups) for i in range(gr...  6.09 us
    ppermute x3, starting transfers between devices, shards(): lax.ppermute(packed, 'test', [(i, (i + shift) % groups) for i in range(gr...  4.71 us
    eq x2, other arithmetic, begin(): hits = well_rows[:, :, None, None, None] == flat[None, None]  3.09 us
    mul x2, other arithmetic, begin(): forcing = forcing * rows_of(mask_ext, state_halo - 1)  2.97 us
  transfers between devices with their start and end apart: 9, of which 3 were waited for; matrix products, arithmetic and copies ran while one was open for 16% of the time, Pallas kernels for 2%

profile of v3, /device:TPU:11, one launch (start us, length us, event | category | flops | bytes accessed | tf_op | source)
XLA Modules:
  0.0 116.4 jit_solution(716626423112220659)
XLA Ops:
  0.0 1.3 %copy.7 = f32[1,1,256,256]{3,1,2,0:T(1,128)S(1)} copy(f32[1,1,256,256]{3,2,1,0:T(8,128)} %bitcast.98) | data formatting | bytes 524288
  3.1 2.3 %collective-permute-start.3 = (f32[1,65552]{1,0:T(1,128)S(1)}, f32[1,65552]{1,0:T(1,128)S(1)}, u32[]{:S(2)}, u32[]{:S(2)}) collective-permute-start(f32[1,65552]{1,0:T(1,128)S(1)} %dynamic-update-slice.2), channel_id=1, source_target_pairs={{0,16},{8,24},{16,0},{24,8},{1,17},{9,25},{17,1},{25,9},{2,18},{10... | collective-permute-start | bytes 786632 | tf_op jit(solution)/shard_map/ppermute | solution.py:221
  5.4 2.2 %collective-permute-start.2 = (f32[1,65552]{1,0:T(1,128)S(1)}, f32[1,65552]{1,0:T(1,128)S(1)}, u32[]{:S(2)}, u32[]{:S(2)}) collective-permute-start(f32[1,65552]{1,0:T(1,128)S(1)} %dynamic-update-slice.2), channel_id=1, source_target_pairs={{0,8},{8,16},{16,24},{24,0},{1,9},{9,17},{17,25},{25,1},{2,10},{10... | collective-permute-start | bytes 786632 | tf_op jit(solution)/shard_map/ppermute | solution.py:221
  7.6 1.7 %broadcast_multiply_fusion.2 = (f32[16,16,256]{2,1,0:T(8,128)}, f32[1,16,16,256]{3,2,1,0:T(8,128)S(1)}, f32[16,16,256]{2,1,0:T(8,128)S(1)}) fusion(f32[16,16,256]{2,1,0:T(8,128)} %param.6), kind=kLoop, calls=%fused_computation.143 | loop fusion | flops 65536 | bytes 1048576 | tf_op jit(solution)/shard_map/mul | solution.py:297
  10.7 3.4 %collective-permute-start.1 = (f32[4,9,16,256]{3,2,1,0:T(8,128)}, f32[4,9,16,256]{3,2,1,0:T(8,128)S(1)}, u32[]{:S(2)}, u32[]{:S(2)}) collective-permute-start(f32[4,9,16,256]{3,2,1,0:T(8,128)} %get-tuple-element.24), channel_id=1, source_target_pairs={{1,0},{2,1},{3,2},{4,3},{5,4},{6,5},{7,6},{9,8},{10,9},{11,10},{12... | collective-permute-start | bytes 1769480 | tf_op jit(solution)/shard_map/ppermute | solution.py:26
  14.1 3.2 %collective-permute-start = (f32[4,9,16,256]{3,2,1,0:T(8,128)}, f32[4,9,16,256]{3,2,1,0:T(8,128)S(1)}, u32[]{:S(2)}, u32[]{:S(2)}) collective-permute-start(f32[4,9,16,256]{3,2,1,0:T(8,128)} %get-tuple-element.23), channel_id=1, source_target_pairs={{0,1},{1,2},{2,3},{3,4},{4,5},{5,6},{6,7},{8,9},{9,10},{10,11},{11... | collective-permute-start | bytes 1769480 | tf_op jit(solution)/shard_map/ppermute | solution.py:24
  18.7 1.3 %broadcast_compare_fusion.1 = pred[1,8,34,16,256]{4,3,2,1,0:T(8,128)(4,1)S(1)} fusion(s32[34,16,256]{2,1,0:T(8,128)S(1)} %iota_add_fusion, s32[8]{0:T(128)} %bitcast.100), kind=kLoop, calls=%fused_computation.12 | loop fusion | flops 1114112 | bytes 1671200 | tf_op jit(solution)/shard_map/eq | solution.py:273
  22.1 5.6 %collective-permute-done.2 = f32[1,65552]{1,0:T(1,128)S(1)} collective-permute-done((f32[1,65552]{1,0:T(1,128)S(1)}, f32[1,65552]{1,0:T(1,128)S(1)}, u32[]{:S(2)}, u32[]{:S(2)}) %collective-permute-start.2) | collective-permute-done | bytes 262240 | tf_op jit(solution)/shard_map/ppermute | solution.py:221
  29.7 3.1 %collective-permute-start.6 = (f32[3,9,16,256]{3,2,1,0:T(8,128)}, f32[3,9,16,256]{3,2,1,0:T(8,128)}, u32[]{:S(2)}, u32[]{:S(2)}) collective-permute-start(f32[3,9,16,256]{3,2,1,0:T(8,128)} %get-tuple-element.34), channel_id=1, source_target_pairs={{1,0},{2,1},{3,2},{4,3},{5,4},{6,5},{7,6},{9,8},{10,9},{11,10},{12... | collective-permute-start | bytes 1327112 | tf_op jit(solution)/shard_map/ppermute | solution.py:26
  32.8 3.5 %collective-permute-start.5 = (f32[3,9,16,256]{3,2,1,0:T(8,128)}, f32[3,9,16,256]{3,2,1,0:T(8,128)}, u32[]{:S(2)}, u32[]{:S(2)}) collective-permute-start(f32[3,9,16,256]{3,2,1,0:T(8,128)} %get-tuple-element.33), channel_id=1, source_target_pairs={{0,1},{1,2},{2,3},{3,4},{4,5},{5,6},{6,7},{8,9},{9,10},{10,11},{11... | collective-permute-start | bytes 1327112 | tf_op jit(solution)/shard_map/ppermute | solution.py:24
  36.4 1.8 %broadcast_compare_fusion = pred[3,8,34,16,256]{4,3,2,1,0:T(8,128)(4,1)S(1)} fusion(s32[34,16,256]{2,1,0:T(8,128)S(1)} %iota_add_fusion, s32[3,8]{1,0:T(4,128)S(1)} %get-tuple-element.28), kind=kLoop, calls=%fused_computation.1 | loop fusion | flops 3342336 | bytes 3899488 | tf_op jit(solution)/shard_map/eq | solution.py:273
  39.1 1.4 %select_reduce_fusion = f32[3,34,16,256]{3,2,1,0:T(8,128)S(1)} fusion(f32[3,8]{1,0:T(4,128)S(1)} %get-tuple-element.29, s32[34,16,256]{2,1,0:T(8,128)S(1)} %iota_add_fusion, s32[3,8]{1,0:T(4,128)S(1)} %get-tuple-element.28), kind=kLoop, calls=%fused_computation | loop fusion | flops 9609216 | bytes 2228416 | tf_op jit(solution)/shard_map/reduce_sum | solution.py:274
  41.8 2.5 %shard_map.64 = f32[1,26,16,256]{3,2,1,0:T(8,128)S(1)} custom-call(f32[1,34,16,256]{3,2,1,0:T(8,128)S(1)} %slice_add_fusion.2.b_ref, f32[6,32,16,256]{3,2,1,0:T(8,128)S(1)} %fusion.55.k_ref, f32[34,16,256]{2,1,0:T(8,128)S(1)} %broadcast_in_dim.68.m_ref), custom_call_target="tpu_custom_call" | custom-call | tf_op jit(solution)/shard_map/pallas_call | solution.py:91
  46.0 1.4 %negate_multiply_fusion.1 = (f32[1,2,24,16,256]{4,3,2,1,0:T(8,128)S(1)}, f32[2,24,16,256]{3,2,1,0:T(8,128)S(1)}, f32[2,24,16,256]{3,2,1,0:T(8,128)S(1)}, f32[2,2...) fusion(f32[24]{0:T(128)S(1)} %slice.230, ...), kind=kLoop, calls=%fused_computation.91 | loop fusion | flops 5701632 | bytes 10223712 | tf_op jit(solution)/shard_map/mul | solution.py:280
  47.4 1.5 %maximum_add_fusion.b_ref = f32[3,34,16,256]{3,2,1,0:T(8,128)S(1)} fusion(f32[3,34,16,256]{3,2,1,0:T(8,128)S(1)} %select_reduce_fusion, f32[3,9,16,256]{3,2,1,0:T(8,128)} %collective-permute-done.6, f32[3,16,16,256]{3,2,1,0:T(8,128)S(1)} %bitcast.96, f32[3,9,16,256]{3,2,1,0:T(8,128)} %collective-permute-done.5), kind=kLoop, calls=%fused_computation.41 | loop fusion | flops 1253376 | bytes 5013504 | tf_op jit(solution)/shard_map/add | solution.py:278
  49.0 9.2 %shard_map.65 = f32[3,26,16,256]{3,2,1,0:T(8,128)S(1)} custom-call(f32[3,34,16,256]{3,2,1,0:T(8,128)S(1)} %maximum_add_fusion.b_ref, f32[6,32,16,256]{3,2,1,0:T(8,128)} %copy-done, f32[34,16,256]{2,1,0:T(8,128)S(1)} %broadcast_in_dim.68.m_ref), custom_call_target="tpu_custom_call" | custom-call | tf_op jit(solution)/shard_map/pallas_call | solution.py:91
  59.8 1.5 %negate_multiply_fusion = f32[3,2,24,16,256]{4,3,2,1,0:T(8,128)S(1)} fusion(f32[24]{0:T(128)S(1)} %slice.230, f32[3,24,16,256]{3,2,1,0:T(8,128)S(1)} %get-tuple-element.17, f32[2,24,16,256]{3,2,1,0:T(8,128)S(1)} %copy-done.2, f32[3,24,16,256]{3,2,1,0:T(8,128)S(1)} %get-tuple-element.16, f32[2,24,16,256]{3,2,1,0:T(8,128)S(1)} %get-tuple-element.32, ...), kind=kLoop, calls=%fused_computation.10 | loop fusion | flops 7667712 | bytes 14155872 | tf_op jit(solution)/shard_map/mul | solution.py:280
  61.7 14.6 %shard_map.66 = f32[8,16,16,256]{3,2,1,0:T(8,128)S(1)} custom-call(f32[8,24,16,256]{3,2,1,0:T(8,128)S(1)} %bitcast.93, f32[6,32,16,256]{3,2,1,0:T(8,128)} %copy-done, f32[34,16,256]{2,1,0:T(8,128)S(1)} %broadcast_in_dim.68.m_ref), custom_call_target="tpu_custom_call" | custom-call | tf_op jit(solution)/shard_map/pallas_call | solution.py:91
  76.8 1.9 %collective-permute-start.8 = (f32[8,5,16,256]{3,2,1,0:T(8,128)S(1)}, f32[8,5,16,256]{3,2,1,0:T(8,128)S(1)}, u32[]{:S(2)}, u32[]{:S(2)}) collective-permute-start(f32[8,5,16,256]{3,2,1,0:T(8,128)S(1)} %get-tuple-element.8), channel_id=1, source_target_pairs={{1,0},{2,1},{3,2},{4,3},{5,4},{6,5},{7,6},{9,8},{10,9},{11,10},{12... | collective-permute-start | bytes 1966088 | tf_op jit(solution)/shard_map/ppermute | solution.py:26
  78.7 4.5 %collective-permute-start.7 = (f32[8,5,16,256]{3,2,1,0:T(8,128)S(1)}, f32[8,5,16,256]{3,2,1,0:T(8,128)S(1)}, u32[]{:S(2)}, u32[]{:S(2)}) collective-permute-start(f32[8,5,16,256]{3,2,1,0:T(8,128)S(1)} %get-tuple-element.7), channel_id=1, source_target_pairs={{0,1},{1,2},{2,3},{3,4},{4,5},{5,6},{6,7},{8,9},{9,10},{10,11},{11... | collective-permute-start | bytes 1966088 | tf_op jit(solution)/shard_map/ppermute | solution.py:24
  84.3 10.6 %collective-permute-done.8 = f32[8,5,16,256]{3,2,1,0:T(8,128)S(1)} collective-permute-done((f32[8,5,16,256]{3,2,1,0:T(8,128)S(1)}, f32[8,5,16,256]{3,2,1,0:T(8,128)S(1)}, u32[]{:S(2)}, u32[]{:S(2)}) %collective-permute-start.8) | collective-permute-done | bytes 655392 | tf_op jit(solution)/shard_map/ppermute | solution.py:26
  95.0 2.1 %pad_maximum_fusion.b_ref = f32[8,26,16,256]{3,2,1,0:T(8,128)} fusion(f32[8,5,16,256]{3,2,1,0:T(8,128)S(1)} %collective-permute-done.8, f32[8,16,16,256]{3,2,1,0:T(8,128)S(1)} %bitcast_multiply_fusion, f32[8,5,16,256]{3,2,1,0:T(8,128)S(1)} %collective-permute-done.7), kind=kLoop, calls=%fused_computation.8 | loop fusion | flops 1703936 | bytes 6815744 | tf_op jit(solution)/shard_map/concatenate | solution.py:22
  97.0 15.6 %shard_map.67 = f32[8,18,16,256]{3,2,1,0:T(8,128)S(1)} custom-call(f32[8,26,16,256]{3,2,1,0:T(8,128)} %pad_maximum_fusion.b_ref, f32[6,32,16,256]{3,2,1,0:T(8,128)S(1)} %copy-done.1, f32[34,16,256]{2,1,0:T(8,128)S(1)} %broadcast_in_dim.68.m_ref), custom_call_target="tpu_custom_call" | custom-call | tf_op jit(solution)/shard_map/pallas_call | solution.py:91
  112.8 2.7 %fusion.6 = f32[2,16,16,256]{3,2,1,0:T(8,128)S(1)} fusion(f32[4,2,16,16,256]{4,3,2,1,0:T(8,128)S(1)} %slice.281, f32[4,2,18,16,256]{4,3,2,1,0:T(8,128)S(1)} %bitcast.91, f32[4,16,16,256]{3,2,1,0:T(8,128)S(1)} %get-tuple-element.21, f32[4,16,16,256]{3,2,1,0:T(8,128)S(1)} %get-tuple-element.20, f32[4,16,16,256]{3,2,1,0:T(8,128)S(1)} %get-tuple-element.22, ...), kind=kLoop, calls=%fused_computation.19 | loop fusion | flops 9306112 | bytes 13107200 | tf_op jit(solution)/shard_map/reduce_sum | solution.py:296
  (72 shorter events, 16.8 us)
Async XLA Ops:
  0.0 9.5 %copy-start.3 = (f32[1,16,16,256]{3,2,1,0:T(8,128)S(1)}, f32[1,16,16,256]{3,2,1,0:T(8,128)}, u32[]{:S(2)}) copy-start(f32[1,16,16,256]{3,2,1,0:T(8,128)} %param.10) | copy-start | bytes 786436
  0.0 9.4 %copy-start.6 = (f32[2,16,16,256]{3,2,1,0:T(8,128)S(1)}, f32[2,16,16,256]{3,2,1,0:T(8,128)}, u32[]{:S(2)}) copy-start(f32[2,16,16,256]{3,2,1,0:T(8,128)} %param.7) | copy-start | bytes 1572868
  2.9 18.7 %collective-permute-start.4 = (f32[1,65552]{1,0:T(1,128)S(1)}, f32[1,65552]{1,0:T(1,128)S(1)}, u32[]{:S(2)}, u32[]{:S(2)}) collective-permute-start(f32[1,65552]{1,0:T(1,128)S(1)} %dynamic-update-slice.2), channel_id=1, source_target_pairs={{0,24},{8,0},{16,8},{24,16},{1,25},{9,1},{17,9},{25,17},{2,26},{10... | collective-permute-start | bytes 786632 | tf_op jit(solution)/shard_map/ppermute | solution.py:221
  3.1 18.9 %collective-permute-start.3 = (f32[1,65552]{1,0:T(1,128)S(1)}, f32[1,65552]{1,0:T(1,128)S(1)}, u32[]{:S(2)}, u32[]{:S(2)}) collective-permute-start(f32[1,65552]{1,0:T(1,128)S(1)} %dynamic-update-slice.2), channel_id=1, source_target_pairs={{0,16},{8,24},{16,0},{24,8},{1,17},{9,25},{17,1},{25,9},{2,18},{10... | collective-permute-start | bytes 786632 | tf_op jit(solution)/shard_map/ppermute | solution.py:221
  5.4 22.2 %collective-permute-start.2 = (f32[1,65552]{1,0:T(1,128)S(1)}, f32[1,65552]{1,0:T(1,128)S(1)}, u32[]{:S(2)}, u32[]{:S(2)}) collective-permute-start(f32[1,65552]{1,0:T(1,128)S(1)} %dynamic-update-slice.2), channel_id=1, source_target_pairs={{0,8},{8,16},{16,24},{24,0},{1,9},{9,17},{17,25},{25,1},{2,10},{10... | collective-permute-start | bytes 786632 | tf_op jit(solution)/shard_map/ppermute | solution.py:221
  10.7 29.8 %collective-permute-start.1 = (f32[4,9,16,256]{3,2,1,0:T(8,128)}, f32[4,9,16,256]{3,2,1,0:T(8,128)S(1)}, u32[]{:S(2)}, u32[]{:S(2)}) collective-permute-start(f32[4,9,16,256]{3,2,1,0:T(8,128)} %get-tuple-element.24), channel_id=1, source_target_pairs={{1,0},{2,1},{3,2},{4,3},{5,4},{6,5},{7,6},{9,8},{10,9},{11,10},{12... | collective-permute-start | bytes 1769480 | tf_op jit(solution)/shard_map/ppermute | solution.py:26
  14.1 7.4 %copy-start.4 = (f32[16,16,256]{2,1,0:T(8,128)S(1)}, f32[16,16,256]{2,1,0:T(8,128)}, u32[]{:S(2)}) copy-start(f32[16,16,256]{2,1,0:T(8,128)} %param.11) | copy-start | bytes 786436
  14.1 26.4 %collective-permute-start = (f32[4,9,16,256]{3,2,1,0:T(8,128)}, f32[4,9,16,256]{3,2,1,0:T(8,128)S(1)}, u32[]{:S(2)}, u32[]{:S(2)}) collective-permute-start(f32[4,9,16,256]{3,2,1,0:T(8,128)} %get-tuple-element.23), channel_id=1, source_target_pairs={{0,1},{1,2},{2,3},{3,4},{4,5},{5,6},{6,7},{8,9},{9,10},{10,11},{11... | collective-permute-start | bytes 1769480 | tf_op jit(solution)/shard_map/ppermute | solution.py:24
  29.7 17.7 %collective-permute-start.6 = (f32[3,9,16,256]{3,2,1,0:T(8,128)}, f32[3,9,16,256]{3,2,1,0:T(8,128)}, u32[]{:S(2)}, u32[]{:S(2)}) collective-permute-start(f32[3,9,16,256]{3,2,1,0:T(8,128)} %get-tuple-element.34), channel_id=1, source_target_pairs={{1,0},{2,1},{3,2},{4,3},{5,4},{6,5},{7,6},{9,8},{10,9},{11,10},{12... | collective-permute-start | bytes 1327112 | tf_op jit(solution)/shard_map/ppermute | solution.py:26
  32.8 14.6 %collective-permute-start.5 = (f32[3,9,16,256]{3,2,1,0:T(8,128)}, f32[3,9,16,256]{3,2,1,0:T(8,128)}, u32[]{:S(2)}, u32[]{:S(2)}) collective-permute-start(f32[3,9,16,256]{3,2,1,0:T(8,128)} %get-tuple-element.33), channel_id=1, source_target_pairs={{0,1},{1,2},{2,3},{3,4},{4,5},{5,6},{6,7},{8,9},{9,10},{10,11},{11... | collective-permute-start | bytes 1327112 | tf_op jit(solution)/shard_map/ppermute | solution.py:24
  41.6 2.8 %copy-start = (f32[6,32,16,256]{3,2,1,0:T(8,128)}, f32[6,32,16,256]{3,2,1,0:T(8,128)S(1)}, u32[]{:S(2)}) copy-start(f32[6,32,16,256]{3,2,1,0:T(8,128)S(1)} %fusion.55.k_ref) | copy-start | bytes 9437188
  58.6 1.1 copy-start.2
  76.8 18.2 %collective-permute-start.8 = (f32[8,5,16,256]{3,2,1,0:T(8,128)S(1)}, f32[8,5,16,256]{3,2,1,0:T(8,128)S(1)}, u32[]{:S(2)}, u32[]{:S(2)}) collective-permute-start(f32[8,5,16,256]{3,2,1,0:T(8,128)S(1)} %get-tuple-element.8), channel_id=1, source_target_pairs={{1,0},{2,1},{3,2},{4,3},{5,4},{6,5},{7,6},{9,8},{10,9},{11,10},{12... | collective-permute-start | bytes 1966088 | tf_op jit(solution)/shard_map/ppermute | solution.py:26
  78.7 16.3 %collective-permute-start.7 = (f32[8,5,16,256]{3,2,1,0:T(8,128)S(1)}, f32[8,5,16,256]{3,2,1,0:T(8,128)S(1)}, u32[]{:S(2)}, u32[]{:S(2)}) collective-permute-start(f32[8,5,16,256]{3,2,1,0:T(8,128)S(1)} %get-tuple-element.7), channel_id=1, source_target_pairs={{0,1},{1,2},{2,3},{3,4},{4,5},{5,6},{6,7},{8,9},{9,10},{10,11},{11... | collective-permute-start | bytes 1966088 | tf_op jit(solution)/shard_map/ppermute | solution.py:24
  84.3 12.7 %copy-start.1 = (f32[6,32,16,256]{3,2,1,0:T(8,128)S(1)}, f32[6,32,16,256]{3,2,1,0:T(8,128)}, u32[]{:S(2)}) copy-start(f32[6,32,16,256]{3,2,1,0:T(8,128)} %copy-done) | copy-start | bytes 9437188
  112.8 2.7 %copy-start.5 = (f32[16,16,256]{2,1,0:T(8,128)S(1)}, f32[16,16,256]{2,1,0:T(8,128)}, u32[]{:S(2)}) copy-start(f32[16,16,256]{2,1,0:T(8,128)} %get-tuple-element.42) | copy-start | bytes 786436

commit v4 on v3

--- a/solution.py
+++ b/solution.py
@@ -34,8 +34,6 @@
 
 def solve_kernel(b_ref, k_ref, m_ref, o_ref, sol, res, da, db, *, offset, first, keeps, pushes):
     rows, rows_y, depth_z = sol.shape
-    iy = lax.broadcasted_iota(jnp.int32, (rows_y, depth_z), 0)
-    iz = lax.broadcasted_iota(jnp.int32, (rows_y, depth_z), 1)
 
     def init(r, c):
         da[r] = b_ref[0, r] * first
@@ -52,15 +50,12 @@
         def step(r, c, turn=turn, src=src, dst=dst, keep=keep, push=push):
             here = src[r]
             face = r - 1 + offset
-            total = k_ref[0, face] * (here - src[r + 1])
-            total = total + k_ref[1, face] * (here - src[r - 1])
-            up = jnp.where(iy < rows_y - 1, pltpu.roll(here, rows_y - 1, 0), 0.0)
-            down = jnp.where(iy > 0, pltpu.roll(here, 1, 0), 0.0)
-            total = total + k_ref[2, face] * (here - up) + k_ref[3, face] * (here - down)
-            up = jnp.where(iz < depth_z - 1, pltpu.roll(here, depth_z - 1, 1), 0.0)
-            down = jnp.where(iz > 0, pltpu.roll(here, 1, 1), 0.0)
-            total = total + k_ref[4, face] * (here - up) + k_ref[5, face] * (here - down)
-            image = storage * here + total
+            image = k_ref[6, face] * here - k_ref[0, face] * src[r + 1]
+            image = image - k_ref[1, face] * src[r - 1]
+            image = image - k_ref[2, face] * pltpu.roll(here, rows_y - 1, 0)
+            image = image - k_ref[3, face] * pltpu.roll(here, 1, 0)
+            image = image - k_ref[4, face] * pltpu.roll(here, depth_z - 1, 1)
+            image = image - k_ref[5, face] * pltpu.roll(here, 1, 1)
             if turn == 0:
                 summed = here
                 fresh = b_ref[0, r] - image
@@ -243,7 +238,22 @@
     def rows_of(field, halo):
         return lax.slice_in_dim(field, reach - halo, reach + slab + halo, axis=field.ndim - 3)
 
-    face_stack = jnp.stack(perm_faces)
+    iy = lax.broadcasted_iota(jnp.int32, (rows_y, depth_z), 0)
+    iz = lax.broadcasted_iota(jnp.int32, (rows_y, depth_z), 1)
+    face_stack = jnp.stack(
+        [
+            perm_faces[0],
+            perm_faces[1],
+            jnp.where(iy < rows_y - 1, perm_faces[2], 0.0),
+            jnp.where(iy > 0, perm_faces[3], 0.0),
+            jnp.where(iz < depth_z - 1, perm_faces[4], 0.0),
+            jnp.where(iz > 0, perm_faces[5], 0.0),
+            storage + (
+                perm_faces[0] + perm_faces[1] + perm_faces[2]
+                + perm_faces[3] + perm_faces[4] + perm_faces[5]
+            ),
+        ]
+    )
     mask_full = jnp.broadcast_to(mask_ext, (rows_ext, rows_y, depth_z))
 
     def solve(right_side, halo):

time: 118 us -> 112 us (0.949)
  Pallas kernels: 41.9 us -> 34.3 us
    pallas_call x4, Pallas kernels: 41.9 us -> 34.3 us  [kernel_solve(): pl.pallas_call(body, grid=(fields,), in_specs=[pl.BlockSpec((1, rows, row...]
  transfers between devices with their start and end apart: 9 -> 9, of which waited for: 3 -> 3; matrix products, arithmetic and copies ran while one was open for 16% -> 18% of each run, Pallas kernels for 2% -> 2%
where the time goes in v4:
time: 112 us; the launch traced here: 110 us
  Pallas kernels  34.3 us (31%)
  other arithmetic  27.4 us (24%)
  starting transfers between devices  24.3 us (22%)
  waiting for transfers between devices  16.8 us (15%)
  local copies, waits for them, and re-layouts  6.42 us (6%)
    pallas_call x4, Pallas kernels, kernel_solve(): pl.pallas_call(body, grid=(fields,), in_specs=[pl.BlockSpec((1, rows, row...  34.3 us
    ppermute x3, starting transfers between devices, with_halo(): lax.ppermute(tail, axis, [(i, i + 1) for i in range(ends)])  11.1 us
    ppermute x3, waiting for transfers between devices, with_halo(): lax.ppermute(head, axis, [(i + 1, i) for i in range(ends)])  10.7 us
    ppermute x3, starting transfers between devices, with_halo(): lax.ppermute(head, axis, [(i + 1, i) for i in range(ends)])  8.45 us
    ppermute x3, waiting for transfers between devices, shards(): lax.ppermute(packed, 'test', [(i, (i + shift) % groups) for i in range(gr...  6.14 us
    ppermute x3, starting transfers between devices, shards(): lax.ppermute(packed, 'test', [(i, (i + shift) % groups) for i in range(gr...  4.71 us
    eq x2, other arithmetic, begin(): hits = well_rows[:, :, None, None, None] == flat[None, None]  3.09 us
    mul x2, other arithmetic, begin(): forcing = forcing * rows_of(mask_ext, state_halo - 1)  2.7 us
  transfers between devices with their start and end apart: 9, of which 3 were waited for; matrix products, arithmetic and copies ran while one was open for 18% of the time, Pallas kernels for 2%

profile of v4, /device:TPU:11, one launch (start us, length us, event | category | flops | bytes accessed | tf_op | source)
XLA Modules:
  0.0 109.8 jit_solution(9682906789923196839)
XLA Ops:
  0.0 1.3 %copy.7 = f32[1,1,256,256]{3,1,2,0:T(1,128)S(1)} copy(f32[1,1,256,256]{3,2,1,0:T(8,128)} %bitcast.114) | data formatting | bytes 524288
  3.1 2.3 %collective-permute-start.3 = (f32[1,65552]{1,0:T(1,128)S(1)}, f32[1,65552]{1,0:T(1,128)S(1)}, u32[]{:S(2)}, u32[]{:S(2)}) collective-permute-start(f32[1,65552]{1,0:T(1,128)S(1)} %dynamic-update-slice.2), channel_id=1, source_target_pairs={{0,16},{8,24},{16,0},{24,8},{1,17},{9,25},{17,1},{25,9},{2,18},{10... | collective-permute-start | bytes 786632 | tf_op jit(solution)/shard_map/ppermute | solution.py:216
  5.4 2.2 %collective-permute-start.2 = (f32[1,65552]{1,0:T(1,128)S(1)}, f32[1,65552]{1,0:T(1,128)S(1)}, u32[]{:S(2)}, u32[]{:S(2)}) collective-permute-start(f32[1,65552]{1,0:T(1,128)S(1)} %dynamic-update-slice.2), channel_id=1, source_target_pairs={{0,8},{8,16},{16,24},{24,0},{1,9},{9,17},{17,25},{25,1},{2,10},{10... | collective-permute-start | bytes 786632 | tf_op jit(solution)/shard_map/ppermute | solution.py:216
  7.6 1.7 %broadcast_multiply_fusion.2 = (f32[16,16,256]{2,1,0:T(8,128)}, f32[1,16,16,256]{3,2,1,0:T(8,128)S(1)}, f32[16,16,256]{2,1,0:T(8,128)S(1)}) fusion(f32[16,16,256]{2,1,0:T(8,128)} %param.6), kind=kLoop, calls=%fused_computation.145 | loop fusion | flops 65536 | bytes 1048576 | tf_op jit(solution)/shard_map/mul | solution.py:307
  10.7 3.4 %collective-permute-start.1 = (f32[4,9,16,256]{3,2,1,0:T(8,128)}, f32[4,9,16,256]{3,2,1,0:T(8,128)S(1)}, u32[]{:S(2)}, u32[]{:S(2)}) collective-permute-start(f32[4,9,16,256]{3,2,1,0:T(8,128)} %get-tuple-element.24), channel_id=1, source_target_pairs={{1,0},{2,1},{3,2},{4,3},{5,4},{6,5},{7,6},{9,8},{10,9},{11,10},{12... | collective-permute-start | bytes 1769480 | tf_op jit(solution)/shard_map/ppermute | solution.py:26
  14.1 3.0 %collective-permute-start = (f32[4,9,16,256]{3,2,1,0:T(8,128)}, f32[4,9,16,256]{3,2,1,0:T(8,128)S(1)}, u32[]{:S(2)}, u32[]{:S(2)}) collective-permute-start(f32[4,9,16,256]{3,2,1,0:T(8,128)} %get-tuple-element.23), channel_id=1, source_target_pairs={{0,1},{1,2},{2,3},{3,4},{4,5},{5,6},{6,7},{8,9},{9,10},{10,11},{11... | collective-permute-start | bytes 1769480 | tf_op jit(solution)/shard_map/ppermute | solution.py:24
  18.6 1.3 %broadcast_compare_fusion.1 = pred[1,8,34,16,256]{4,3,2,1,0:T(8,128)(4,1)S(1)} fusion(s32[34,16,256]{2,1,0:T(8,128)S(1)} %iota_add_fusion, s32[8]{0:T(128)} %bitcast.116), kind=kLoop, calls=%fused_computation.12 | loop fusion | flops 1114112 | bytes 1671200 | tf_op jit(solution)/shard_map/eq | solution.py:283
  19.9 1.2 %select_reduce_fusion.1 = f32[34,16,256]{2,1,0:T(8,128)S(1)} fusion(f32[8]{0:T(128)} %bitcast.118, s32[34,16,256]{2,1,0:T(8,128)S(1)} %iota_add_fusion, s32[8]{0:T(128)} %bitcast.117), kind=kLoop, calls=%fused_computation.3 | loop fusion | flops 3203072 | bytes 1114176 | tf_op jit(solution)/shard_map/reduce_sum | solution.py:284
  22.1 5.6 %collective-permute-done.2 = f32[1,65552]{1,0:T(1,128)S(1)} collective-permute-done((f32[1,65552]{1,0:T(1,128)S(1)}, f32[1,65552]{1,0:T(1,128)S(1)}, u32[]{:S(2)}, u32[]{:S(2)}) %collective-permute-start.2) | collective-permute-done | bytes 262240 | tf_op jit(solution)/shard_map/ppermute | solution.py:216
  29.7 3.1 %collective-permute-start.6 = (f32[3,9,16,256]{3,2,1,0:T(8,128)}, f32[3,9,16,256]{3,2,1,0:T(8,128)}, u32[]{:S(2)}, u32[]{:S(2)}) collective-permute-start(f32[3,9,16,256]{3,2,1,0:T(8,128)} %get-tuple-element.34), channel_id=1, source_target_pairs={{1,0},{2,1},{3,2},{4,3},{5,4},{6,5},{7,6},{9,8},{10,9},{11,10},{12... | collective-permute-start | bytes 1327112 | tf_op jit(solution)/shard_map/ppermute | solution.py:26
  32.8 3.5 %collective-permute-start.5 = (f32[3,9,16,256]{3,2,1,0:T(8,128)}, f32[3,9,16,256]{3,2,1,0:T(8,128)}, u32[]{:S(2)}, u32[]{:S(2)}) collective-permute-start(f32[3,9,16,256]{3,2,1,0:T(8,128)} %get-tuple-element.33), channel_id=1, source_target_pairs={{0,1},{1,2},{2,3},{3,4},{4,5},{5,6},{6,7},{8,9},{9,10},{10,11},{11... | collective-permute-start | bytes 1327112 | tf_op jit(solution)/shard_map/ppermute | solution.py:24
  36.4 1.8 %broadcast_compare_fusion = pred[3,8,34,16,256]{4,3,2,1,0:T(8,128)(4,1)S(1)} fusion(s32[34,16,256]{2,1,0:T(8,128)S(1)} %iota_add_fusion, s32[3,8]{1,0:T(4,128)S(1)} %get-tuple-element.28), kind=kLoop, calls=%fused_computation.1 | loop fusion | flops 3342336 | bytes 3899488 | tf_op jit(solution)/shard_map/eq | solution.py:283
  39.1 1.4 %select_reduce_fusion = f32[3,34,16,256]{3,2,1,0:T(8,128)S(1)} fusion(f32[3,8]{1,0:T(4,128)S(1)} %get-tuple-element.29, s32[34,16,256]{2,1,0:T(8,128)S(1)} %iota_add_fusion, s32[3,8]{1,0:T(4,128)S(1)} %get-tuple-element.28), kind=kLoop, calls=%fused_computation | loop fusion | flops 9609216 | bytes 2228416 | tf_op jit(solution)/shard_map/reduce_sum | solution.py:284
  42.4 2.1 %shard_map.64 = f32[1,26,16,256]{3,2,1,0:T(8,128)S(1)} custom-call(f32[1,34,16,256]{3,2,1,0:T(8,128)S(1)} %slice_add_fusion.2.b_ref, f32[7,32,16,256]{3,2,1,0:T(8,128)S(1)} %bitcast_dynamic-update-slice_fusion.k_ref, f32[34,16,256]{2,1,0:T(8,128)S(1)} %broadcast_in_dim.93.m_ref), custom_call_target="tpu_custom_call" | custom-call | tf_op jit(solution)/shard_map/pallas_call | solution.py:86
  47.9 1.5 %maximum_add_fusion.b_ref = f32[3,34,16,256]{3,2,1,0:T(8,128)S(1)} fusion(f32[3,34,16,256]{3,2,1,0:T(8,128)S(1)} %select_reduce_fusion, f32[3,9,16,256]{3,2,1,0:T(8,128)} %collective-permute-done.6, f32[3,16,16,256]{3,2,1,0:T(8,128)S(1)} %bitcast.112, f32[3,9,16,256]{3,2,1,0:T(8,128)} %collective-permute-done.5), kind=kLoop, calls=%fused_computation.41 | loop fusion | flops 1253376 | bytes 5013504 | tf_op jit(solution)/shard_map/add | solution.py:288
  49.4 7.6 %shard_map.65 = f32[3,26,16,256]{3,2,1,0:T(8,128)S(1)} custom-call(f32[3,34,16,256]{3,2,1,0:T(8,128)S(1)} %maximum_add_fusion.b_ref, f32[7,32,16,256]{3,2,1,0:T(8,128)} %copy-done, f32[34,16,256]{2,1,0:T(8,128)S(1)} %broadcast_in_dim.93.m_ref), custom_call_target="tpu_custom_call" | custom-call | tf_op jit(solution)/shard_map/pallas_call | solution.py:86
  58.7 1.6 %negate_multiply_fusion = f32[3,2,24,16,256]{4,3,2,1,0:T(8,128)S(1)} fusion(f32[24]{0:T(128)S(1)} %slice.236, f32[3,24,16,256]{3,2,1,0:T(8,128)S(1)} %get-tuple-element.17, f32[2,24,16,256]{3,2,1,0:T(8,128)S(1)} %copy-done.1, f32[3,24,16,256]{3,2,1,0:T(8,128)S(1)} %get-tuple-element.16, f32[2,24,16,256]{3,2,1,0:T(8,128)S(1)} %get-tuple-element.32, ...), kind=kLoop, calls=%fused_computation.10 | loop fusion | flops 7667712 | bytes 14155872 | tf_op jit(solution)/shard_map/mul | solution.py:290
  60.6 11.8 %shard_map.66 = f32[8,16,16,256]{3,2,1,0:T(8,128)S(1)} custom-call(f32[8,24,16,256]{3,2,1,0:T(8,128)S(1)} %bitcast.109, f32[7,32,16,256]{3,2,1,0:T(8,128)} %copy-done, f32[34,16,256]{2,1,0:T(8,128)S(1)} %broadcast_in_dim.93.m_ref), custom_call_target="tpu_custom_call" | custom-call | tf_op jit(solution)/shard_map/pallas_call | solution.py:86
  72.9 1.9 %collective-permute-start.8 = (f32[8,5,16,256]{3,2,1,0:T(8,128)S(1)}, f32[8,5,16,256]{3,2,1,0:T(8,128)S(1)}, u32[]{:S(2)}, u32[]{:S(2)}) collective-permute-start(f32[8,5,16,256]{3,2,1,0:T(8,128)S(1)} %get-tuple-element.8), channel_id=1, source_target_pairs={{1,0},{2,1},{3,2},{4,3},{5,4},{6,5},{7,6},{9,8},{10,9},{11,10},{12... | collective-permute-start | bytes 1966088 | tf_op jit(solution)/shard_map/ppermute | solution.py:26
  74.8 4.5 %collective-permute-start.7 = (f32[8,5,16,256]{3,2,1,0:T(8,128)S(1)}, f32[8,5,16,256]{3,2,1,0:T(8,128)S(1)}, u32[]{:S(2)}, u32[]{:S(2)}) collective-permute-start(f32[8,5,16,256]{3,2,1,0:T(8,128)S(1)} %get-tuple-element.7), channel_id=1, source_target_pairs={{0,1},{1,2},{2,3},{3,4},{4,5},{5,6},{6,7},{8,9},{9,10},{10,11},{11... | collective-permute-start | bytes 1966088 | tf_op jit(solution)/shard_map/ppermute | solution.py:24
  80.4 10.6 %collective-permute-done.8 = f32[8,5,16,256]{3,2,1,0:T(8,128)S(1)} collective-permute-done((f32[8,5,16,256]{3,2,1,0:T(8,128)S(1)}, f32[8,5,16,256]{3,2,1,0:T(8,128)S(1)}, u32[]{:S(2)}, u32[]{:S(2)}) %collective-permute-start.8) | collective-permute-done | bytes 655392 | tf_op jit(solution)/shard_map/ppermute | solution.py:26
  91.1 2.1 %pad_maximum_fusion.b_ref = f32[8,26,16,256]{3,2,1,0:T(8,128)} fusion(f32[8,5,16,256]{3,2,1,0:T(8,128)S(1)} %collective-permute-done.8, f32[8,16,16,256]{3,2,1,0:T(8,128)S(1)} %bitcast_multiply_fusion, f32[8,5,16,256]{3,2,1,0:T(8,128)S(1)} %collective-permute-done.7), kind=kLoop, calls=%fused_computation.8 | loop fusion | flops 1703936 | bytes 6815744 | tf_op jit(solution)/shard_map/concatenate | solution.py:22
  93.2 12.8 %shard_map.67 = f32[8,18,16,256]{3,2,1,0:T(8,128)S(1)} custom-call(f32[8,26,16,256]{3,2,1,0:T(8,128)} %pad_maximum_fusion.b_ref, f32[7,32,16,256]{3,2,1,0:T(8,128)} %copy-done, f32[34,16,256]{2,1,0:T(8,128)S(1)} %broadcast_in_dim.93.m_ref), custom_call_target="tpu_custom_call" | custom-call | tf_op jit(solution)/shard_map/pallas_call | solution.py:86
  106.2 2.7 %fusion.6 = f32[2,16,16,256]{3,2,1,0:T(8,128)S(1)} fusion(f32[4,2,16,16,256]{4,3,2,1,0:T(8,128)S(1)} %slice.287, f32[4,2,18,16,256]{4,3,2,1,0:T(8,128)S(1)} %bitcast.107, f32[4,16,16,256]{3,2,1,0:T(8,128)S(1)} %get-tuple-element.21, f32[4,16,16,256]{3,2,1,0:T(8,128)S(1)} %get-tuple-element.20, f32[4,16,16,256]{3,2,1,0:T(8,128)S(1)} %get-tuple-element.22, ...), kind=kLoop, calls=%fused_computation.19 | loop fusion | flops 9306112 | bytes 13107200 | tf_op jit(solution)/shard_map/reduce_sum | solution.py:306
  (77 shorter events, 17.9 us)
Async XLA Ops:
  0.0 9.5 %copy-start.2 = (f32[1,16,16,256]{3,2,1,0:T(8,128)S(1)}, f32[1,16,16,256]{3,2,1,0:T(8,128)}, u32[]{:S(2)}) copy-start(f32[1,16,16,256]{3,2,1,0:T(8,128)} %param.10) | copy-start | bytes 786436
  0.0 9.4 %copy-start.6 = (f32[2,16,16,256]{3,2,1,0:T(8,128)S(1)}, f32[2,16,16,256]{3,2,1,0:T(8,128)}, u32[]{:S(2)}) copy-start(f32[2,16,16,256]{3,2,1,0:T(8,128)} %param.7) | copy-start | bytes 1572868
  2.9 18.6 %collective-permute-start.4 = (f32[1,65552]{1,0:T(1,128)S(1)}, f32[1,65552]{1,0:T(1,128)S(1)}, u32[]{:S(2)}, u32[]{:S(2)}) collective-permute-start(f32[1,65552]{1,0:T(1,128)S(1)} %dynamic-update-slice.2), channel_id=1, source_target_pairs={{0,24},{8,0},{16,8},{24,16},{1,25},{9,1},{17,9},{25,17},{2,26},{10... | collective-permute-start | bytes 786632 | tf_op jit(solution)/shard_map/ppermute | solution.py:216
  3.1 18.9 %collective-permute-start.3 = (f32[1,65552]{1,0:T(1,128)S(1)}, f32[1,65552]{1,0:T(1,128)S(1)}, u32[]{:S(2)}, u32[]{:S(2)}) collective-permute-start(f32[1,65552]{1,0:T(1,128)S(1)} %dynamic-update-slice.2), channel_id=1, source_target_pairs={{0,16},{8,24},{16,0},{24,8},{1,17},{9,25},{17,1},{25,9},{2,18},{10... | collective-permute-start | bytes 786632 | tf_op jit(solution)/shard_map/ppermute | solution.py:216
  5.4 22.2 %collective-permute-start.2 = (f32[1,65552]{1,0:T(1,128)S(1)}, f32[1,65552]{1,0:T(1,128)S(1)}, u32[]{:S(2)}, u32[]{:S(2)}) collective-permute-start(f32[1,65552]{1,0:T(1,128)S(1)} %dynamic-update-slice.2), channel_id=1, source_target_pairs={{0,8},{8,16},{16,24},{24,0},{1,9},{9,17},{17,25},{25,1},{2,10},{10... | collective-permute-start | bytes 786632 | tf_op jit(solution)/shard_map/ppermute | solution.py:216
  10.7 29.8 %collective-permute-start.1 = (f32[4,9,16,256]{3,2,1,0:T(8,128)}, f32[4,9,16,256]{3,2,1,0:T(8,128)S(1)}, u32[]{:S(2)}, u32[]{:S(2)}) collective-permute-start(f32[4,9,16,256]{3,2,1,0:T(8,128)} %get-tuple-element.24), channel_id=1, source_target_pairs={{1,0},{2,1},{3,2},{4,3},{5,4},{6,5},{7,6},{9,8},{10,9},{11,10},{12... | collective-permute-start | bytes 1769480 | tf_op jit(solution)/shard_map/ppermute | solution.py:26
  14.1 26.4 %collective-permute-start = (f32[4,9,16,256]{3,2,1,0:T(8,128)}, f32[4,9,16,256]{3,2,1,0:T(8,128)S(1)}, u32[]{:S(2)}, u32[]{:S(2)}) collective-permute-start(f32[4,9,16,256]{3,2,1,0:T(8,128)} %get-tuple-element.23), channel_id=1, source_target_pairs={{0,1},{1,2},{2,3},{3,4},{4,5},{5,6},{6,7},{8,9},{9,10},{10,11},{11... | collective-permute-start | bytes 1769480 | tf_op jit(solution)/shard_map/ppermute | solution.py:24
  17.7 3.8 %copy-start.4 = (f32[16,16,256]{2,1,0:T(8,128)S(1)}, f32[16,16,256]{2,1,0:T(8,128)}, u32[]{:S(2)}) copy-start(f32[16,16,256]{2,1,0:T(8,128)} %param.11) | copy-start | bytes 786436
  29.7 18.2 %collective-permute-start.6 = (f32[3,9,16,256]{3,2,1,0:T(8,128)}, f32[3,9,16,256]{3,2,1,0:T(8,128)}, u32[]{:S(2)}, u32[]{:S(2)}) collective-permute-start(f32[3,9,16,256]{3,2,1,0:T(8,128)} %get-tuple-element.34), channel_id=1, source_target_pairs={{1,0},{2,1},{3,2},{4,3},{5,4},{6,5},{7,6},{9,8},{10,9},{11,10},{12... | collective-permute-start | bytes 1327112 | tf_op jit(solution)/shard_map/ppermute | solution.py:26
  32.8 15.0 %collective-permute-start.5 = (f32[3,9,16,256]{3,2,1,0:T(8,128)}, f32[3,9,16,256]{3,2,1,0:T(8,128)}, u32[]{:S(2)}, u32[]{:S(2)}) collective-permute-start(f32[3,9,16,256]{3,2,1,0:T(8,128)} %get-tuple-element.33), channel_id=1, source_target_pairs={{0,1},{1,2},{2,3},{3,4},{4,5},{5,6},{6,7},{8,9},{9,10},{10,11},{11... | collective-permute-start | bytes 1327112 | tf_op jit(solution)/shard_map/ppermute | solution.py:24
  42.1 2.3 %copy-start = (f32[7,32,16,256]{3,2,1,0:T(8,128)}, f32[7,32,16,256]{3,2,1,0:T(8,128)S(1)}, u32[]{:S(2)}) copy-start(f32[7,32,16,256]{3,2,1,0:T(8,128)S(1)} %bitcast_dynamic-update-slice_fusion.k_ref) | copy-start | bytes 11010052
  57.5 1.1 %copy-start.1 = (f32[2,24,16,256]{3,2,1,0:T(8,128)S(1)}, f32[2,24,16,256]{3,2,1,0:T(8,128)}, u32[]{:S(2)}) copy-start(f32[2,24,16,256]{3,2,1,0:T(8,128)} %multiply_bitcast_fusion) | copy-start | bytes 2359300
  72.7 6.6 %copy-start.3 = (f32[1,18,16,256]{3,2,1,0:T(8,128)S(1)}, f32[1,18,16,256]{3,2,1,0:T(8,128)}, u32[]{:S(2)}) copy-start(f32[1,18,16,256]{3,2,1,0:T(8,128)} %slice.266) | copy-start | bytes 884740
  72.9 18.2 %collective-permute-start.8 = (f32[8,5,16,256]{3,2,1,0:T(8,128)S(1)}, f32[8,5,16,256]{3,2,1,0:T(8,128)S(1)}, u32[]{:S(2)}, u32[]{:S(2)}) collective-permute-start(f32[8,5,16,256]{3,2,1,0:T(8,128)S(1)} %get-tuple-element.8), channel_id=1, source_target_pairs={{1,0},{2,1},{3,2},{4,3},{5,4},{6,5},{7,6},{9,8},{10,9},{11,10},{12... | collective-permute-start | bytes 1966088 | tf_op jit(solution)/shard_map/ppermute | solution.py:26
  74.8 16.3 %collective-permute-start.7 = (f32[8,5,16,256]{3,2,1,0:T(8,128)S(1)}, f32[8,5,16,256]{3,2,1,0:T(8,128)S(1)}, u32[]{:S(2)}, u32[]{:S(2)}) collective-permute-start(f32[8,5,16,256]{3,2,1,0:T(8,128)S(1)} %get-tuple-element.7), channel_id=1, source_target_pairs={{0,1},{1,2},{2,3},{3,4},{4,5},{5,6},{6,7},{8,9},{9,10},{10,11},{11... | collective-permute-start | bytes 1966088 | tf_op jit(solution)/shard_map/ppermute | solution.py:24
  106.2 2.7 %copy-start.5 = (f32[16,16,256]{2,1,0:T(8,128)S(1)}, f32[16,16,256]{2,1,0:T(8,128)}, u32[]{:S(2)}) copy-start(f32[16,16,256]{2,1,0:T(8,128)} %get-tuple-element.42) | copy-start | bytes 786436

commit v5 on v4

--- a/solution.py
+++ b/solution.py
@@ -7,6 +7,7 @@
 from jax.experimental import pallas as pl
 from jax.experimental.pallas import tpu as pltpu
 from jax.sharding import PartitionSpec as P
+
 
 CHEB = 4
 
@@ -107,7 +108,7 @@
     rho = 1.0 / sigma
     keeps = []
     pushes = []
-    for turn in range(count):
+    for _ in range(count):
         after = 1.0 / (2.0 * sigma - rho)
         keeps.append(after * rho)
         pushes.append(2.0 * after / spread)
@@ -157,16 +158,6 @@
         0.5 * (weight + weight_up_z),
         0.5 * (weight + weight_down_z),
     )
-
-
-def apply_faces(face, field_ext):
-    field = field_ext[..., 1:-1, :, :]
-    total = face[0] * (field - field_ext[..., 2:, :, :])
-    total = total + face[1] * (field - field_ext[..., :-2, :, :])
-    for back, up, down in ((2, face[2], face[3]), (1, face[4], face[5])):
-        field_up, field_down = neighbours(field, back)
-        total = total + up * (field - field_up) + down * (field - field_down)
-    return total
 
 
 def pairs(left_ext, right_ext):
@@ -183,10 +174,6 @@
             + (left - left_down) * (right - right_down)
         )
     return total
-
-
-def inner(field):
-    return field[..., 1:-1, :, :]
 
 
 def shards(log_perm, panel, wells, rates, recharge, gauge):
@@ -264,21 +251,6 @@
         )
         return result.reshape(lead + result.shape[-3:]), halo - CHEB
 
-    def solve_xla(right_side, halo):
-        solution = jnp.zeros_like(right_side)
-        residual = right_side
-        direction = right_side * first
-        for turn in range(CHEB):
-            face = tuple(part[reach - halo : reach + slab + halo - 2] for part in perm_faces)
-            image = storage * inner(direction) + apply_faces(face, direction)
-            solution = inner(solution) + inner(direction)
-            residual = inner(residual) - image
-            halo -= 1
-            direction = (keeps[turn] * inner(direction) + pushes[turn] * residual) * rows_of(
-                mask_ext, halo
-            )
-        return solution + direction, halo
-
     def begin(rech_ext, well_rows, rate_rows):
         hits = well_rows[:, :, None, None, None] == flat[None, None]
         points = jnp.sum(jnp.where(hits, rate_rows[:, :, None, None, None], 0.0), axis=1)
@@ -296,12 +268,25 @@
         parts_of.append(begin(rech_others, wells_others, rates_others))
     state, forcing, observe = (jnp.concatenate(group, axis=0) for group in zip(*parts_of))
     forcing = forcing.reshape(tests * cols, slab + 2 * CHEB, rows_y, depth_z)
-    change, _ = solve(forcing, CHEB)
-    weighted = (
-        change.reshape(tests, cols, slab, rows_y, depth_z) * observe[:, None]
-    ).reshape(tests * cols, slab, rows_y, depth_z)
-    weighted_ext = with_halo(weighted, "cell", 1, CHEB + 1)
-    adjoint, _ = solve(weighted_ext, CHEB + 1)
+    fields = tests * cols
+    observe_fields = jnp.broadcast_to(
+        observe[:, None], (tests, cols, slab, rows_y, depth_z)
+    ).reshape(fields, slab, rows_y, depth_z)
+    half = fields // 2
+    spans = [(0, half), (half, fields)] if half else [(0, fields)]
+    halos = []
+    ahead = forcing[spans[0][0] : spans[0][1]]
+    for index, (lo, hi) in enumerate(spans):
+        change, _ = solve(ahead, CHEB)
+        weighted = change * observe_fields[lo:hi]
+        if index + 1 < len(spans):
+            nxt = spans[index + 1]
+            weighted, ahead = lax.optimization_barrier((weighted, forcing[nxt[0] : nxt[1]]))
+        halos.append(with_halo(weighted, "cell", 1, CHEB + 1))
+    adjoints = []
+    for part in halos:
+        adjoints.append(solve(part, CHEB + 1)[0])
+    adjoint = jnp.concatenate(adjoints, axis=0)
     adjoint = adjoint.reshape(tests, cols, slab + 2, rows_y, depth_z)
     contrib = jnp.sum(pairs(state[:, None], adjoint), axis=0)
     return -0.5 * perm[None] * contrib

time: 112 us -> 111 us (level)
  waiting for transfers between devices: 16.8 us -> 7.84 us
  starting transfers between devices: 24.3 us -> 30.7 us
  Pallas kernels: 34.3 us -> 38.7 us
  other arithmetic: 27.4 us -> 23.9 us
  local copies, waits for them, and re-layouts: 6.42 us -> 7.7 us
    ppermute x3 -> x4, waiting for transfers between devices: 10.7 us -> 0.01 us  [with_halo(): lax.ppermute(head, axis, [(i + 1, i) for i in range(ends)])]
    ppermute x3 -> x4, starting transfers between devices: 11.1 us -> 15.6 us  [with_halo(): lax.ppermute(tail, axis, [(i, i + 1) for i in range(ends)])]
    pallas_call x4 -> x6, Pallas kernels: 34.3 us -> 38.7 us  [kernel_solve(): pl.pallas_call(body, grid=(fields,), in_specs=[pl.BlockSpec((1, rows, row...]
    ppermute x3 -> x4, starting transfers between devices: 8.45 us -> 10.4 us  [with_halo(): lax.ppermute(head, axis, [(i + 1, i) for i in range(ends)])]
    concatenate x2 -> x3, other arithmetic: 2.36 us -> 0.53 us  [with_halo(): jnp.concatenate([lax.ppermute(tail, axis, [(i, i + 1) for i in range(ends...]
    ppermute x3, waiting for transfers between devices: 6.14 us -> 7.82 us  [shards(): lax.ppermute(packed, 'test', [(i, (i + shift) % groups) for i in range(gr...]
    unnamed x18 -> x14, local copies, waits for them, and re-layouts: 1.88 us -> 3.37 us
  transfers between devices with their start and end apart: 9 -> 11, of which waited for: 3 -> 2; matrix products, arithmetic and copies ran while one was open for 18% -> 16% of each run, Pallas kernels for 2% -> 9%
where the time goes in v5:
time: 111 us; the launch traced here: 109 us
  Pallas kernels  38.7 us (35%)
  starting transfers between devices  30.7 us (28%)
  other arithmetic  23.9 us (22%)
  waiting for transfers between devices  7.84 us (7%)
  local copies, waits for them, and re-layouts  7.7 us (7%)
    pallas_call x6, Pallas kernels, kernel_solve(): pl.pallas_call(body, grid=(fields,), in_specs=[pl.BlockSpec((1, rows, row...  38.7 us
    ppermute x4, starting transfers between devices, with_halo(): lax.ppermute(tail, axis, [(i, i + 1) for i in range(ends)])  15.6 us
    ppermute x4, starting transfers between devices, with_halo(): lax.ppermute(head, axis, [(i + 1, i) for i in range(ends)])  10.4 us
    ppermute x3, waiting for transfers between devices, shards(): lax.ppermute(packed, 'test', [(i, (i + shift) % groups) for i in range(gr...  7.82 us
    ppermute x3, starting transfers between devices, shards(): lax.ppermute(packed, 'test', [(i, (i + shift) % groups) for i in range(gr...  4.67 us
    unnamed x14, local copies, waits for them, and re-layouts  3.37 us
    mul x2, other arithmetic, begin(): forcing = forcing * rows_of(mask_ext, state_halo - 1)  3 us
    reduce_sum x1, other arithmetic, shards(): contrib = jnp.sum(pairs(state[:, None], adjoint), axis=0)  2.72 us
  transfers between devices with their start and end apart: 11, of which 2 were waited for; matrix products, arithmetic and copies ran while one was open for 16% of the time, Pallas kernels for 9%

profile of v5, /device:TPU:11, one launch (start us, length us, event | category | flops | bytes accessed | tf_op | source)
XLA Modules:
  0.0 109.5 jit_solution(12289864195508012717)
XLA Ops:
  5.3 2.3 %collective-permute-start.3 = (f32[1,65552]{1,0:T(1,128)}, f32[1,65552]{1,0:T(1,128)S(1)}, u32[]{:S(2)}, u32[]{:S(2)}) collective-permute-start(f32[1,65552]{1,0:T(1,128)} %dynamic-update-slice.2), channel_id=1, source_target_pairs={{0,16},{8,24},{16,0},{24,8},{1,17},{9,25},{17,1},{25,9},{2,18},{10... | collective-permute-start | bytes 786632 | tf_op jit(solution)/shard_map/ppermute | solution.py:203
  7.6 2.2 %collective-permute-start.2 = (f32[1,65552]{1,0:T(1,128)}, f32[1,65552]{1,0:T(1,128)S(1)}, u32[]{:S(2)}, u32[]{:S(2)}) collective-permute-start(f32[1,65552]{1,0:T(1,128)} %dynamic-update-slice.2), channel_id=1, source_target_pairs={{0,8},{8,16},{16,24},{24,0},{1,9},{9,17},{17,25},{25,1},{2,10},{10... | collective-permute-start | bytes 786632 | tf_op jit(solution)/shard_map/ppermute | solution.py:203
  12.2 3.4 %collective-permute-start.1 = (f32[4,9,16,256]{3,2,1,0:T(8,128)}, f32[4,9,16,256]{3,2,1,0:T(8,128)S(1)}, u32[]{:S(2)}, u32[]{:S(2)}) collective-permute-start(f32[4,9,16,256]{3,2,1,0:T(8,128)} %get-tuple-element.32), channel_id=1, source_target_pairs={{1,0},{2,1},{3,2},{4,3},{5,4},{6,5},{7,6},{9,8},{10,9},{11,10},{12... | collective-permute-start | bytes 1769480 | tf_op jit(solution)/shard_map/ppermute | solution.py:27
  15.6 3.0 %collective-permute-start = (f32[4,9,16,256]{3,2,1,0:T(8,128)}, f32[4,9,16,256]{3,2,1,0:T(8,128)S(1)}, u32[]{:S(2)}, u32[]{:S(2)}) collective-permute-start(f32[4,9,16,256]{3,2,1,0:T(8,128)} %get-tuple-element.31), channel_id=1, source_target_pairs={{0,1},{1,2},{2,3},{3,4},{4,5},{5,6},{6,7},{8,9},{9,10},{10,11},{11... | collective-permute-start | bytes 1769480 | tf_op jit(solution)/shard_map/ppermute | solution.py:25
  22.4 2.2 %collective-permute-done.3 = f32[1,65552]{1,0:T(1,128)S(1)} collective-permute-done((f32[1,65552]{1,0:T(1,128)}, f32[1,65552]{1,0:T(1,128)S(1)}, u32[]{:S(2)}, u32[]{:S(2)}) %collective-permute-start.3) | collective-permute-done | bytes 262240 | tf_op jit(solution)/shard_map/ppermute | solution.py:203
  24.5 5.6 %collective-permute-done.2 = f32[1,65552]{1,0:T(1,128)S(1)} collective-permute-done((f32[1,65552]{1,0:T(1,128)}, f32[1,65552]{1,0:T(1,128)S(1)}, u32[]{:S(2)}, u32[]{:S(2)}) %collective-permute-start.2) | collective-permute-done | bytes 262240 | tf_op jit(solution)/shard_map/ppermute | solution.py:203
  32.2 3.1 %collective-permute-start.6 = (f32[3,9,16,256]{3,2,1,0:T(8,128)}, f32[3,9,16,256]{3,2,1,0:T(8,128)}, u32[]{:S(2)}, u32[]{:S(2)}) collective-permute-start(f32[3,9,16,256]{3,2,1,0:T(8,128)} %get-tuple-element.44), channel_id=1, source_target_pairs={{1,0},{2,1},{3,2},{4,3},{5,4},{6,5},{7,6},{9,8},{10,9},{11,10},{12... | collective-permute-start | bytes 1327112 | tf_op jit(solution)/shard_map/ppermute | solution.py:27
  35.3 3.5 %collective-permute-start.5 = (f32[3,9,16,256]{3,2,1,0:T(8,128)}, f32[3,9,16,256]{3,2,1,0:T(8,128)}, u32[]{:S(2)}, u32[]{:S(2)}) collective-permute-start(f32[3,9,16,256]{3,2,1,0:T(8,128)} %get-tuple-element.43), channel_id=1, source_target_pairs={{0,1},{1,2},{2,3},{3,4},{4,5},{5,6},{6,7},{8,9},{9,10},{10,11},{11... | collective-permute-start | bytes 1327112 | tf_op jit(solution)/shard_map/ppermute | solution.py:25
  38.9 1.8 %broadcast_compare_fusion = pred[3,8,34,16,256]{4,3,2,1,0:T(8,128)(4,1)S(1)} fusion(s32[34,16,256]{2,1,0:T(8,128)S(1)} %iota_add_fusion, s32[3,8]{1,0:T(4,128)S(1)} %get-tuple-element.36), kind=kLoop, calls=%fused_computation.1 | loop fusion | flops 3342336 | bytes 3899488 | tf_op jit(solution)/shard_map/eq | solution.py:255
  41.6 1.4 %select_reduce_fusion = f32[3,34,16,256]{3,2,1,0:T(8,128)S(1)} fusion(f32[3,8]{1,0:T(4,128)S(1)} %get-tuple-element.37, s32[34,16,256]{2,1,0:T(8,128)S(1)} %iota_add_fusion, s32[3,8]{1,0:T(4,128)S(1)} %get-tuple-element.36), kind=kLoop, calls=%fused_computation | loop fusion | flops 9609216 | bytes 2228416 | tf_op jit(solution)/shard_map/reduce_sum | solution.py:256
  44.9 2.0 %shard_map.64 = f32[1,26,16,256]{3,2,1,0:T(8,128)S(1)} custom-call(f32[1,34,16,256]{3,2,1,0:T(8,128)S(1)} %slice_add_fusion.2.b_ref, f32[7,32,16,256]{3,2,1,0:T(8,128)S(1)} %bitcast_dynamic-update-slice_fusion.k_ref, f32[34,16,256]{2,1,0:T(8,128)S(1)} %broadcast_in_dim.100.m_ref), custom_call_target="tpu_custom_call" | custom-call | tf_op jit(solution)/shard_map/pallas_call | solution.py:87
  47.6 1.4 %negate_multiply_fusion.1 = (f32[1,2,24,16,256]{4,3,2,1,0:T(8,128)S(1)}, f32[2,24,16,256]{3,2,1,0:T(8,128)S(1)}, f32[2,24,16,256]{3,2,1,0:T(8,128)S(1)}, f32[2,2...) fusion(f32[24]{0:T(128)S(1)} %slice.270, ...), kind=kLoop, calls=%fused_computation.93 | loop fusion | flops 5701632 | bytes 10223712 | tf_op jit(solution)/shard_map/mul | solution.py:262
  49.0 1.5 %maximum_add_fusion.b_ref = f32[3,34,16,256]{3,2,1,0:T(8,128)S(1)} fusion(f32[3,34,16,256]{3,2,1,0:T(8,128)S(1)} %select_reduce_fusion, f32[3,9,16,256]{3,2,1,0:T(8,128)} %collective-permute-done.6, f32[3,16,16,256]{3,2,1,0:T(8,128)S(1)} %bitcast.116, f32[3,9,16,256]{3,2,1,0:T(8,128)} %collective-permute-done.5), kind=kLoop, calls=%fused_computation.41 | loop fusion | flops 1253376 | bytes 5013504 | tf_op jit(solution)/shard_map/add | solution.py:260
  50.6 7.6 %shard_map.65 = f32[3,26,16,256]{3,2,1,0:T(8,128)S(1)} custom-call(f32[3,34,16,256]{3,2,1,0:T(8,128)S(1)} %maximum_add_fusion.b_ref, f32[7,32,16,256]{3,2,1,0:T(8,128)} %copy-done, f32[34,16,256]{2,1,0:T(8,128)S(1)} %broadcast_in_dim.100.m_ref), custom_call_target="tpu_custom_call" | custom-call | tf_op jit(solution)/shard_map/pallas_call | solution.py:87
  59.5 1.6 %negate_multiply_fusion = f32[3,2,24,16,256]{4,3,2,1,0:T(8,128)S(1)} fusion(f32[24]{0:T(128)S(1)} %slice.270, f32[3,24,16,256]{3,2,1,0:T(8,128)S(1)} %get-tuple-element.21, f32[2,24,16,256]{3,2,1,0:T(8,128)S(1)} %multiply_bitcast_fusion, f32[3,24,16,256]{3,2,1,0:T(8,128)S(1)} %get-tuple-element.20, f32[2,24,16,256]{3,2,1,0:T(8,128)S(1)} %get-tuple-element.42, ...), kind=kLoop, calls=%fused_computation.9 | loop fusion | flops 7667712 | bytes 14155872 | tf_op jit(solution)/shard_map/mul | solution.py:262
  61.4 6.9 %shard_map.66 = f32[4,16,16,256]{3,2,1,0:T(8,128)S(1)} custom-call(f32[4,24,16,256]{3,2,1,0:T(8,128)S(1)} %bitcast.112, f32[7,32,16,256]{3,2,1,0:T(8,128)} %copy-done, f32[34,16,256]{2,1,0:T(8,128)S(1)} %broadcast_in_dim.100.m_ref), custom_call_target="tpu_custom_call" | custom-call | tf_op jit(solution)/shard_map/pallas_call | solution.py:87
  68.5 6.9 %shard_map.68 = f32[4,16,16,256]{3,2,1,0:T(8,128)S(1)} custom-call(f32[4,24,16,256]{3,2,1,0:T(8,128)S(1)} %bitcast.111, f32[7,32,16,256]{3,2,1,0:T(8,128)} %copy-done, f32[34,16,256]{2,1,0:T(8,128)S(1)} %broadcast_in_dim.100.m_ref), custom_call_target="tpu_custom_call" | custom-call | tf_op jit(solution)/shard_map/pallas_call | solution.py:87
  75.7 1.9 %collective-permute-start.10 = (f32[4,5,16,256]{3,2,1,0:T(8,128)S(1)}, f32[4,5,16,256]{3,2,1,0:T(8,128)S(1)}, u32[]{:S(2)}, u32[]{:S(2)}) collective-permute-start(f32[4,5,16,256]{3,2,1,0:T(8,128)S(1)} %get-tuple-element.30), channel_id=1, source_target_pairs={{1,0},{2,1},{3,2},{4,3},{5,4},{6,5},{7,6},{9,8},{10,9},{11,10},{12... | collective-permute-start | bytes 983048 | tf_op jit(solution)/shard_map/ppermute | solution.py:27
  77.6 4.5 %collective-permute-start.9 = (f32[4,5,16,256]{3,2,1,0:T(8,128)S(1)}, f32[4,5,16,256]{3,2,1,0:T(8,128)S(1)}, u32[]{:S(2)}, u32[]{:S(2)}) collective-permute-start(f32[4,5,16,256]{3,2,1,0:T(8,128)S(1)} %get-tuple-element.29), channel_id=1, source_target_pairs={{0,1},{1,2},{2,3},{3,4},{4,5},{5,6},{6,7},{8,9},{9,10},{10,11},{11... | collective-permute-start | bytes 983048 | tf_op jit(solution)/shard_map/ppermute | solution.py:25
  82.2 1.9 %collective-permute-start.8 = (f32[4,5,16,256]{3,2,1,0:T(8,128)S(1)}, f32[4,5,16,256]{3,2,1,0:T(8,128)S(1)}, u32[]{:S(2)}, u32[]{:S(2)}) collective-permute-start(f32[4,5,16,256]{3,2,1,0:T(8,128)S(1)} %get-tuple-element.28), channel_id=1, source_target_pairs={{1,0},{2,1},{3,2},{4,3},{5,4},{6,5},{7,6},{9,8},{10,9},{11,10},{12... | collective-permute-start | bytes 983048 | tf_op jit(solution)/shard_map/ppermute | solution.py:27
  84.2 4.5 %collective-permute-start.7 = (f32[4,5,16,256]{3,2,1,0:T(8,128)S(1)}, f32[4,5,16,256]{3,2,1,0:T(8,128)S(1)}, u32[]{:S(2)}, u32[]{:S(2)}) collective-permute-start(f32[4,5,16,256]{3,2,1,0:T(8,128)S(1)} %get-tuple-element.27), channel_id=1, source_target_pairs={{0,1},{1,2},{2,3},{3,4},{4,5},{5,6},{6,7},{8,9},{9,10},{10,11},{11... | collective-permute-start | bytes 983048 | tf_op jit(solution)/shard_map/ppermute | solution.py:25
  90.0 7.7 %shard_map.69 = f32[4,18,16,256]{3,2,1,0:T(8,128)S(1)} custom-call(f32[4,26,16,256]{3,2,1,0:T(8,128)S(1)} %pad_maximum_fusion.3.b_ref, f32[7,32,16,256]{3,2,1,0:T(8,128)} %copy-done, f32[34,16,256]{2,1,0:T(8,128)S(1)} %broadcast_in_dim.100.m_ref), custom_call_target="tpu_custom_call" | custom-call | tf_op jit(solution)/shard_map/pallas_call | solution.py:87
  97.9 7.5 %shard_map.67 = f32[4,18,16,256]{3,2,1,0:T(8,128)S(1)} custom-call(f32[4,26,16,256]{3,2,1,0:T(8,128)S(1)} %pad_maximum_fusion.2.b_ref, f32[7,32,16,256]{3,2,1,0:T(8,128)} %copy-done, f32[34,16,256]{2,1,0:T(8,128)S(1)} %broadcast_in_dim.100.m_ref), custom_call_target="tpu_custom_call" | custom-call | tf_op jit(solution)/shard_map/pallas_call | solution.py:87
  105.9 2.7 %fusion.6 = f32[2,16,16,256]{3,2,1,0:T(8,128)S(1)} fusion(f32[4,2,16,16,256]{4,3,2,1,0:T(8,128)S(1)} %slice.333, f32[4,2,18,16,256]{4,3,2,1,0:T(8,128)S(1)} %bitcast.114, f32[4,16,16,256]{3,2,1,0:T(8,128)S(1)} %get-tuple-element.25, f32[4,16,16,256]{3,2,1,0:T(8,128)S(1)} %get-tuple-element.24, f32[4,16,16,256]{3,2,1,0:T(8,128)S(1)} %get-tuple-element.26, ...), kind=kLoop, calls=%fused_computation.18 | loop fusion | flops 9306112 | bytes 13107200 | tf_op jit(solution)/shard_map/reduce_sum | solution.py:291
  (83 shorter events, 21.4 us)
Async XLA Ops:
  0.0 10.9 %copy-start.1 = (f32[1,16,16,256]{3,2,1,0:T(8,128)S(1)}, f32[1,16,16,256]{3,2,1,0:T(8,128)}, u32[]{:S(2)}) copy-start(f32[1,16,16,256]{3,2,1,0:T(8,128)} %param.10) | copy-start | bytes 786436
  0.0 10.8 %copy-start.3 = (f32[2,16,16,256]{3,2,1,0:T(8,128)S(1)}, f32[2,16,16,256]{3,2,1,0:T(8,128)}, u32[]{:S(2)}) copy-start(f32[2,16,16,256]{3,2,1,0:T(8,128)} %param.7) | copy-start | bytes 1572868
  5.1 17.2 %collective-permute-start.4 = (f32[1,65552]{1,0:T(1,128)}, f32[1,65552]{1,0:T(1,128)S(1)}, u32[]{:S(2)}, u32[]{:S(2)}) collective-permute-start(f32[1,65552]{1,0:T(1,128)} %dynamic-update-slice.2), channel_id=1, source_target_pairs={{0,24},{8,0},{16,8},{24,16},{1,25},{9,1},{17,9},{25,17},{2,26},{10... | collective-permute-start | bytes 786632 | tf_op jit(solution)/shard_map/ppermute | solution.py:203
  5.3 19.2 %collective-permute-start.3 = (f32[1,65552]{1,0:T(1,128)}, f32[1,65552]{1,0:T(1,128)S(1)}, u32[]{:S(2)}, u32[]{:S(2)}) collective-permute-start(f32[1,65552]{1,0:T(1,128)} %dynamic-update-slice.2), channel_id=1, source_target_pairs={{0,16},{8,24},{16,0},{24,8},{1,17},{9,25},{17,1},{25,9},{2,18},{10... | collective-permute-start | bytes 786632 | tf_op jit(solution)/shard_map/ppermute | solution.py:203
  7.6 22.6 %collective-permute-start.2 = (f32[1,65552]{1,0:T(1,128)}, f32[1,65552]{1,0:T(1,128)S(1)}, u32[]{:S(2)}, u32[]{:S(2)}) collective-permute-start(f32[1,65552]{1,0:T(1,128)} %dynamic-update-slice.2), channel_id=1, source_target_pairs={{0,8},{8,16},{16,24},{24,0},{1,9},{9,17},{17,25},{25,1},{2,10},{10... | collective-permute-start | bytes 786632 | tf_op jit(solution)/shard_map/ppermute | solution.py:203
  11.0 9.2 %copy-start.4 = (s32[1,8]{1,0:T(1,128)S(1)}, s32[1,8]{1,0:T(1,128)}, u32[]{:S(2)}) copy-start(s32[1,8]{1,0:T(1,128)} %param.8) | copy-start | bytes 100
  12.2 30.8 %collective-permute-start.1 = (f32[4,9,16,256]{3,2,1,0:T(8,128)}, f32[4,9,16,256]{3,2,1,0:T(8,128)S(1)}, u32[]{:S(2)}, u32[]{:S(2)}) collective-permute-start(f32[4,9,16,256]{3,2,1,0:T(8,128)} %get-tuple-element.32), channel_id=1, source_target_pairs={{1,0},{2,1},{3,2},{4,3},{5,4},{6,5},{7,6},{9,8},{10,9},{11,10},{12... | collective-permute-start | bytes 1769480 | tf_op jit(solution)/shard_map/ppermute | solution.py:27
  15.6 27.4 %collective-permute-start = (f32[4,9,16,256]{3,2,1,0:T(8,128)}, f32[4,9,16,256]{3,2,1,0:T(8,128)S(1)}, u32[]{:S(2)}, u32[]{:S(2)}) collective-permute-start(f32[4,9,16,256]{3,2,1,0:T(8,128)} %get-tuple-element.31), channel_id=1, source_target_pairs={{0,1},{1,2},{2,3},{3,4},{4,5},{5,6},{6,7},{8,9},{9,10},{10,11},{11... | collective-permute-start | bytes 1769480 | tf_op jit(solution)/shard_map/ppermute | solution.py:25
  19.2 3.1 %copy-start.2 = (f32[16,16,256]{2,1,0:T(8,128)S(1)}, f32[16,16,256]{2,1,0:T(8,128)}, u32[]{:S(2)}) copy-start(f32[16,16,256]{2,1,0:T(8,128)} %param.11) | copy-start | bytes 786436
  32.2 16.8 %collective-permute-start.6 = (f32[3,9,16,256]{3,2,1,0:T(8,128)}, f32[3,9,16,256]{3,2,1,0:T(8,128)}, u32[]{:S(2)}, u32[]{:S(2)}) collective-permute-start(f32[3,9,16,256]{3,2,1,0:T(8,128)} %get-tuple-element.44), channel_id=1, source_target_pairs={{1,0},{2,1},{3,2},{4,3},{5,4},{6,5},{7,6},{9,8},{10,9},{11,10},{12... | collective-permute-start | bytes 1327112 | tf_op jit(solution)/shard_map/ppermute | solution.py:27
  35.3 13.7 %collective-permute-start.5 = (f32[3,9,16,256]{3,2,1,0:T(8,128)}, f32[3,9,16,256]{3,2,1,0:T(8,128)}, u32[]{:S(2)}, u32[]{:S(2)}) collective-permute-start(f32[3,9,16,256]{3,2,1,0:T(8,128)} %get-tuple-element.43), channel_id=1, source_target_pairs={{0,1},{1,2},{2,3},{3,4},{4,5},{5,6},{6,7},{8,9},{9,10},{10,11},{11... | collective-permute-start | bytes 1327112 | tf_op jit(solution)/shard_map/ppermute | solution.py:25
  44.6 2.3 %copy-start = (f32[7,32,16,256]{3,2,1,0:T(8,128)}, f32[7,32,16,256]{3,2,1,0:T(8,128)S(1)}, u32[]{:S(2)}) copy-start(f32[7,32,16,256]{3,2,1,0:T(8,128)S(1)} %bitcast_dynamic-update-slice_fusion.k_ref) | copy-start | bytes 11010052
  75.7 14.1 %collective-permute-start.10 = (f32[4,5,16,256]{3,2,1,0:T(8,128)S(1)}, f32[4,5,16,256]{3,2,1,0:T(8,128)S(1)}, u32[]{:S(2)}, u32[]{:S(2)}) collective-permute-start(f32[4,5,16,256]{3,2,1,0:T(8,128)S(1)} %get-tuple-element.30), channel_id=1, source_target_pairs={{1,0},{2,1},{3,2},{4,3},{5,4},{6,5},{7,6},{9,8},{10,9},{11,10},{12... | collective-permute-start | bytes 983048 | tf_op jit(solution)/shard_map/ppermute | solution.py:27
  77.6 12.2 %collective-permute-start.9 = (f32[4,5,16,256]{3,2,1,0:T(8,128)S(1)}, f32[4,5,16,256]{3,2,1,0:T(8,128)S(1)}, u32[]{:S(2)}, u32[]{:S(2)}) collective-permute-start(f32[4,5,16,256]{3,2,1,0:T(8,128)S(1)} %get-tuple-element.29), channel_id=1, source_target_pairs={{0,1},{1,2},{2,3},{3,4},{4,5},{5,6},{6,7},{8,9},{9,10},{10,11},{11... | collective-permute-start | bytes 983048 | tf_op jit(solution)/shard_map/ppermute | solution.py:25
  82.2 15.5 %collective-permute-start.8 = (f32[4,5,16,256]{3,2,1,0:T(8,128)S(1)}, f32[4,5,16,256]{3,2,1,0:T(8,128)S(1)}, u32[]{:S(2)}, u32[]{:S(2)}) collective-permute-start(f32[4,5,16,256]{3,2,1,0:T(8,128)S(1)} %get-tuple-element.28), channel_id=1, source_target_pairs={{1,0},{2,1},{3,2},{4,3},{5,4},{6,5},{7,6},{9,8},{10,9},{11,10},{12... | collective-permute-start | bytes 983048 | tf_op jit(solution)/shard_map/ppermute | solution.py:27
  84.2 13.6 %collective-permute-start.7 = (f32[4,5,16,256]{3,2,1,0:T(8,128)S(1)}, f32[4,5,16,256]{3,2,1,0:T(8,128)S(1)}, u32[]{:S(2)}, u32[]{:S(2)}) collective-permute-start(f32[4,5,16,256]{3,2,1,0:T(8,128)S(1)} %get-tuple-element.27), channel_id=1, source_target_pairs={{0,1},{1,2},{2,3},{3,4},{4,5},{5,6},{6,7},{8,9},{9,10},{10,11},{11... | collective-permute-start | bytes 983048 | tf_op jit(solution)/shard_map/ppermute | solution.py:25

commit v6 on v5

--- a/solution.py
+++ b/solution.py
@@ -34,10 +34,10 @@
 
 
 def solve_kernel(b_ref, k_ref, m_ref, o_ref, sol, res, da, db, *, offset, first, keeps, pushes):
-    rows, rows_y, depth_z = sol.shape
+    block, rows, rows_y, depth_z = sol.shape
 
     def init(r, c):
-        da[r] = b_ref[0, r] * first
+        da[:, r] = b_ref[:, r] * first
         return c
 
     lax.fori_loop(0, rows, init, 0, unroll=True)
@@ -49,27 +49,30 @@
         push = pushes[turn]
 
         def step(r, c, turn=turn, src=src, dst=dst, keep=keep, push=push):
-            here = src[r]
             face = r - 1 + offset
-            image = k_ref[6, face] * here - k_ref[0, face] * src[r + 1]
-            image = image - k_ref[1, face] * src[r - 1]
-            image = image - k_ref[2, face] * pltpu.roll(here, rows_y - 1, 0)
-            image = image - k_ref[3, face] * pltpu.roll(here, 1, 0)
-            image = image - k_ref[4, face] * pltpu.roll(here, depth_z - 1, 1)
-            image = image - k_ref[5, face] * pltpu.roll(here, 1, 1)
-            if turn == 0:
-                summed = here
-                fresh = b_ref[0, r] - image
-            else:
-                summed = sol[r] + here
-                fresh = res[r] - image
-            after = (keep * here + push * fresh) * m_ref[r + offset]
-            if turn == CHEB - 1:
-                o_ref[0, r - CHEB] = summed + after
-            else:
-                sol[r] = summed
-                res[r] = fresh
-                dst[r] = after
+            coeff = [k_ref[j, face] for j in range(7)]
+            gate = m_ref[r + offset]
+            for f in range(block):
+                here = src[f, r]
+                image = coeff[6] * here - coeff[0] * src[f, r + 1]
+                image = image - coeff[1] * src[f, r - 1]
+                image = image - coeff[2] * pltpu.roll(here, rows_y - 1, 0)
+                image = image - coeff[3] * pltpu.roll(here, 1, 0)
+                image = image - coeff[4] * pltpu.roll(here, depth_z - 1, 1)
+                image = image - coeff[5] * pltpu.roll(here, 1, 1)
+                if turn == 0:
+                    summed = here
+                    fresh = b_ref[f, r] - image
+                else:
+                    summed = sol[f, r] + here
+                    fresh = res[f, r] - image
+                after = (keep * here + push * fresh) * gate
+                if turn == CHEB - 1:
+                    o_ref[f, r - CHEB] = summed + after
+                else:
+                    sol[f, r] = summed
+                    res[f, r] = fresh
+                    dst[f, r] = after
             return c
 
         lax.fori_loop(turn + 1, rows - 1 - turn, step, 0, unroll=True)
@@ -77,6 +80,7 @@
 
 def kernel_solve(right_side, face_stack, mask_full, offset, first, keeps, pushes):
     fields, rows, rows_y, depth_z = right_side.shape
+    block = 2 if fields % 2 == 0 else 1
     body = functools.partial(
         solve_kernel,
         offset=offset,
@@ -86,15 +90,17 @@
     )
     return pl.pallas_call(
         body,
-        grid=(fields,),
+        grid=(fields // block,),
         in_specs=[
-            pl.BlockSpec((1, rows, rows_y, depth_z), lambda f: (f, 0, 0, 0)),
+            pl.BlockSpec((block, rows, rows_y, depth_z), lambda f: (f, 0, 0, 0)),
             pl.BlockSpec(face_stack.shape, lambda f: (0, 0, 0, 0)),
             pl.BlockSpec(mask_full.shape, lambda f: (0, 0, 0)),
         ],
-        out_specs=pl.BlockSpec((1, rows - 2 * CHEB, rows_y, depth_z), lambda f: (f, 0, 0, 0)),
+        out_specs=pl.BlockSpec((block, rows - 2 * CHEB, rows_y, depth_z), lambda f: (f, 0, 0, 0)),
         out_shape=jax.ShapeDtypeStruct((fields, rows - 2 * CHEB, rows_y, depth_z), jnp.float32),
-        scratch_shapes=[pltpu.VMEM((rows, rows_y, depth_z), jnp.float32) for _ in range(4)],
+        scratch_shapes=[
+            pltpu.VMEM((block, rows, rows_y, depth_z), jnp.float32) for _ in range(4)
+        ],
         compiler_params=pltpu.CompilerParams(vmem_limit_bytes=48 * 1024 * 1024),
         interpret=INTERPRET,
     )(right_side, face_stack, mask_full)

time: 111 us -> 110 us (level)
  no operation moved by 1% of the time
where the time goes in v6:
time: 110 us; the launch traced here: 109 us
  Pallas kernels  38 us (35%)
  starting transfers between devices  30.7 us (28%)
  other arithmetic  23.9 us (22%)
  waiting for transfers between devices  7.84 us (7%)
  local copies, waits for them, and re-layouts  7.7 us (7%)
    pallas_call x6, Pallas kernels, kernel_solve(): pl.pallas_call(body, grid=(fields // block,), in_specs=[pl.BlockSpec((blo...  38 us
    ppermute x4, starting transfers between devices, with_halo(): lax.ppermute(tail, axis, [(i, i + 1) for i in range(ends)])  15.6 us
    ppermute x4, starting transfers between devices, with_halo(): lax.ppermute(head, axis, [(i + 1, i) for i in range(ends)])  10.4 us
    ppermute x3, waiting for transfers between devices, shards(): lax.ppermute(packed, 'test', [(i, (i + shift) % groups) for i in range(gr...  7.82 us
    ppermute x3, starting transfers between devices, shards(): lax.ppermute(packed, 'test', [(i, (i + shift) % groups) for i in range(gr...  4.67 us
    unnamed x14, local copies, waits for them, and re-layouts  3.37 us
    mul x2, other arithmetic, begin(): forcing = forcing * rows_of(mask_ext, state_halo - 1)  3 us
    reduce_sum x1, other arithmetic, shards(): contrib = jnp.sum(pairs(state[:, None], adjoint), axis=0)  2.72 us
  transfers between devices with their start and end apart: 11, of which 2 were waited for; matrix products, arithmetic and copies ran while one was open for 16% of the time, Pallas kernels for 9%

profile of v6, /device:TPU:11, one launch (start us, length us, event | category | flops | bytes accessed | tf_op | source)
XLA Modules:
  0.0 108.8 jit_solution(11357155437741961074)
XLA Ops:
  5.3 2.3 %collective-permute-start.3 = (f32[1,65552]{1,0:T(1,128)}, f32[1,65552]{1,0:T(1,128)S(1)}, u32[]{:S(2)}, u32[]{:S(2)}) collective-permute-start(f32[1,65552]{1,0:T(1,128)} %dynamic-update-slice.2), channel_id=1, source_target_pairs={{0,16},{8,24},{16,0},{24,8},{1,17},{9,25},{17,1},{25,9},{2,18},{10... | collective-permute-start | bytes 786632 | tf_op jit(solution)/shard_map/ppermute | solution.py:209
  7.6 2.2 %collective-permute-start.2 = (f32[1,65552]{1,0:T(1,128)}, f32[1,65552]{1,0:T(1,128)S(1)}, u32[]{:S(2)}, u32[]{:S(2)}) collective-permute-start(f32[1,65552]{1,0:T(1,128)} %dynamic-update-slice.2), channel_id=1, source_target_pairs={{0,8},{8,16},{16,24},{24,0},{1,9},{9,17},{17,25},{25,1},{2,10},{10... | collective-permute-start | bytes 786632 | tf_op jit(solution)/shard_map/ppermute | solution.py:209
  12.2 3.4 %collective-permute-start.1 = (f32[4,9,16,256]{3,2,1,0:T(8,128)}, f32[4,9,16,256]{3,2,1,0:T(8,128)S(1)}, u32[]{:S(2)}, u32[]{:S(2)}) collective-permute-start(f32[4,9,16,256]{3,2,1,0:T(8,128)} %get-tuple-element.32), channel_id=1, source_target_pairs={{1,0},{2,1},{3,2},{4,3},{5,4},{6,5},{7,6},{9,8},{10,9},{11,10},{12... | collective-permute-start | bytes 1769480 | tf_op jit(solution)/shard_map/ppermute | solution.py:27
  15.6 3.0 %collective-permute-start = (f32[4,9,16,256]{3,2,1,0:T(8,128)}, f32[4,9,16,256]{3,2,1,0:T(8,128)S(1)}, u32[]{:S(2)}, u32[]{:S(2)}) collective-permute-start(f32[4,9,16,256]{3,2,1,0:T(8,128)} %get-tuple-element.31), channel_id=1, source_target_pairs={{0,1},{1,2},{2,3},{3,4},{4,5},{5,6},{6,7},{8,9},{9,10},{10,11},{11... | collective-permute-start | bytes 1769480 | tf_op jit(solution)/shard_map/ppermute | solution.py:25
  22.4 2.2 %collective-permute-done.3 = f32[1,65552]{1,0:T(1,128)S(1)} collective-permute-done((f32[1,65552]{1,0:T(1,128)}, f32[1,65552]{1,0:T(1,128)S(1)}, u32[]{:S(2)}, u32[]{:S(2)}) %collective-permute-start.3) | collective-permute-done | bytes 262240 | tf_op jit(solution)/shard_map/ppermute | solution.py:209
  24.5 5.6 %collective-permute-done.2 = f32[1,65552]{1,0:T(1,128)S(1)} collective-permute-done((f32[1,65552]{1,0:T(1,128)}, f32[1,65552]{1,0:T(1,128)S(1)}, u32[]{:S(2)}, u32[]{:S(2)}) %collective-permute-start.2) | collective-permute-done | bytes 262240 | tf_op jit(solution)/shard_map/ppermute | solution.py:209
  32.2 3.1 %collective-permute-start.6 = (f32[3,9,16,256]{3,2,1,0:T(8,128)}, f32[3,9,16,256]{3,2,1,0:T(8,128)}, u32[]{:S(2)}, u32[]{:S(2)}) collective-permute-start(f32[3,9,16,256]{3,2,1,0:T(8,128)} %get-tuple-element.44), channel_id=1, source_target_pairs={{1,0},{2,1},{3,2},{4,3},{5,4},{6,5},{7,6},{9,8},{10,9},{11,10},{12... | collective-permute-start | bytes 1327112 | tf_op jit(solution)/shard_map/ppermute | solution.py:27
  35.3 3.5 %collective-permute-start.5 = (f32[3,9,16,256]{3,2,1,0:T(8,128)}, f32[3,9,16,256]{3,2,1,0:T(8,128)}, u32[]{:S(2)}, u32[]{:S(2)}) collective-permute-start(f32[3,9,16,256]{3,2,1,0:T(8,128)} %get-tuple-element.43), channel_id=1, source_target_pairs={{0,1},{1,2},{2,3},{3,4},{4,5},{5,6},{6,7},{8,9},{9,10},{10,11},{11... | collective-permute-start | bytes 1327112 | tf_op jit(solution)/shard_map/ppermute | solution.py:25
  38.9 1.8 %broadcast_compare_fusion = pred[3,8,34,16,256]{4,3,2,1,0:T(8,128)(4,1)S(1)} fusion(s32[34,16,256]{2,1,0:T(8,128)S(1)} %iota_add_fusion, s32[3,8]{1,0:T(4,128)S(1)} %get-tuple-element.36), kind=kLoop, calls=%fused_computation.1 | loop fusion | flops 3342336 | bytes 3899488 | tf_op jit(solution)/shard_map/eq | solution.py:261
  41.6 1.4 %select_reduce_fusion = f32[3,34,16,256]{3,2,1,0:T(8,128)S(1)} fusion(f32[3,8]{1,0:T(4,128)S(1)} %get-tuple-element.37, s32[34,16,256]{2,1,0:T(8,128)S(1)} %iota_add_fusion, s32[3,8]{1,0:T(4,128)S(1)} %get-tuple-element.36), kind=kLoop, calls=%fused_computation | loop fusion | flops 9609216 | bytes 2228416 | tf_op jit(solution)/shard_map/reduce_sum | solution.py:262
  44.9 2.0 %shard_map.64 = f32[1,26,16,256]{3,2,1,0:T(8,128)S(1)} custom-call(f32[1,34,16,256]{3,2,1,0:T(8,128)S(1)} %slice_add_fusion.2.b_ref, f32[7,32,16,256]{3,2,1,0:T(8,128)S(1)} %bitcast_dynamic-update-slice_fusion.k_ref, f32[34,16,256]{2,1,0:T(8,128)S(1)} %broadcast_in_dim.100.m_ref), custom_call_target="tpu_custom_call" | custom-call | tf_op jit(solution)/shard_map/pallas_call | solution.py:91
  47.6 1.4 %negate_multiply_fusion.1 = (f32[1,2,24,16,256]{4,3,2,1,0:T(8,128)S(1)}, f32[2,24,16,256]{3,2,1,0:T(8,128)S(1)}, f32[2,24,16,256]{3,2,1,0:T(8,128)S(1)}, f32[2,2...) fusion(f32[24]{0:T(128)S(1)} %slice.270, ...), kind=kLoop, calls=%fused_computation.93 | loop fusion | flops 5701632 | bytes 10223712 | tf_op jit(solution)/shard_map/mul | solution.py:268
  49.0 1.5 %maximum_add_fusion.b_ref = f32[3,34,16,256]{3,2,1,0:T(8,128)S(1)} fusion(f32[3,34,16,256]{3,2,1,0:T(8,128)S(1)} %select_reduce_fusion, f32[3,9,16,256]{3,2,1,0:T(8,128)} %collective-permute-done.6, f32[3,16,16,256]{3,2,1,0:T(8,128)S(1)} %bitcast.116, f32[3,9,16,256]{3,2,1,0:T(8,128)} %collective-permute-done.5), kind=kLoop, calls=%fused_computation.41 | loop fusion | flops 1253376 | bytes 5013504 | tf_op jit(solution)/shard_map/add | solution.py:266
  50.6 7.6 %shard_map.65 = f32[3,26,16,256]{3,2,1,0:T(8,128)S(1)} custom-call(f32[3,34,16,256]{3,2,1,0:T(8,128)S(1)} %maximum_add_fusion.b_ref, f32[7,32,16,256]{3,2,1,0:T(8,128)} %copy-done, f32[34,16,256]{2,1,0:T(8,128)S(1)} %broadcast_in_dim.100.m_ref), custom_call_target="tpu_custom_call" | custom-call | tf_op jit(solution)/shard_map/pallas_call | solution.py:91
  59.5 1.6 %negate_multiply_fusion = f32[3,2,24,16,256]{4,3,2,1,0:T(8,128)S(1)} fusion(f32[24]{0:T(128)S(1)} %slice.270, f32[3,24,16,256]{3,2,1,0:T(8,128)S(1)} %get-tuple-element.21, f32[2,24,16,256]{3,2,1,0:T(8,128)S(1)} %multiply_bitcast_fusion, f32[3,24,16,256]{3,2,1,0:T(8,128)S(1)} %get-tuple-element.20, f32[2,24,16,256]{3,2,1,0:T(8,128)S(1)} %get-tuple-element.42, ...), kind=kLoop, calls=%fused_computation.9 | loop fusion | flops 7667712 | bytes 14155872 | tf_op jit(solution)/shard_map/mul | solution.py:268
  61.4 6.8 %shard_map.66 = f32[4,16,16,256]{3,2,1,0:T(8,128)S(1)} custom-call(f32[4,24,16,256]{3,2,1,0:T(8,128)S(1)} %bitcast.112, f32[7,32,16,256]{3,2,1,0:T(8,128)} %copy-done, f32[34,16,256]{2,1,0:T(8,128)S(1)} %broadcast_in_dim.100.m_ref), custom_call_target="tpu_custom_call" | custom-call | tf_op jit(solution)/shard_map/pallas_call | solution.py:91
  68.4 6.8 %shard_map.68 = f32[4,16,16,256]{3,2,1,0:T(8,128)S(1)} custom-call(f32[4,24,16,256]{3,2,1,0:T(8,128)S(1)} %bitcast.111, f32[7,32,16,256]{3,2,1,0:T(8,128)} %copy-done, f32[34,16,256]{2,1,0:T(8,128)S(1)} %broadcast_in_dim.100.m_ref), custom_call_target="tpu_custom_call" | custom-call | tf_op jit(solution)/shard_map/pallas_call | solution.py:91
  75.4 1.9 %collective-permute-start.10 = (f32[4,5,16,256]{3,2,1,0:T(8,128)S(1)}, f32[4,5,16,256]{3,2,1,0:T(8,128)S(1)}, u32[]{:S(2)}, u32[]{:S(2)}) collective-permute-start(f32[4,5,16,256]{3,2,1,0:T(8,128)S(1)} %get-tuple-element.30), channel_id=1, source_target_pairs={{1,0},{2,1},{3,2},{4,3},{5,4},{6,5},{7,6},{9,8},{10,9},{11,10},{12... | collective-permute-start | bytes 983048 | tf_op jit(solution)/shard_map/ppermute | solution.py:27
  77.3 4.5 %collective-permute-start.9 = (f32[4,5,16,256]{3,2,1,0:T(8,128)S(1)}, f32[4,5,16,256]{3,2,1,0:T(8,128)S(1)}, u32[]{:S(2)}, u32[]{:S(2)}) collective-permute-start(f32[4,5,16,256]{3,2,1,0:T(8,128)S(1)} %get-tuple-element.29), channel_id=1, source_target_pairs={{0,1},{1,2},{2,3},{3,4},{4,5},{5,6},{6,7},{8,9},{9,10},{10,11},{11... | collective-permute-start | bytes 983048 | tf_op jit(solution)/shard_map/ppermute | solution.py:25
  81.9 1.9 %collective-permute-start.8 = (f32[4,5,16,256]{3,2,1,0:T(8,128)S(1)}, f32[4,5,16,256]{3,2,1,0:T(8,128)S(1)}, u32[]{:S(2)}, u32[]{:S(2)}) collective-permute-start(f32[4,5,16,256]{3,2,1,0:T(8,128)S(1)} %get-tuple-element.28), channel_id=1, source_target_pairs={{1,0},{2,1},{3,2},{4,3},{5,4},{6,5},{7,6},{9,8},{10,9},{11,10},{12... | collective-permute-start | bytes 983048 | tf_op jit(solution)/shard_map/ppermute | solution.py:27
  83.9 4.5 %collective-permute-start.7 = (f32[4,5,16,256]{3,2,1,0:T(8,128)S(1)}, f32[4,5,16,256]{3,2,1,0:T(8,128)S(1)}, u32[]{:S(2)}, u32[]{:S(2)}) collective-permute-start(f32[4,5,16,256]{3,2,1,0:T(8,128)S(1)} %get-tuple-element.27), channel_id=1, source_target_pairs={{0,1},{1,2},{2,3},{3,4},{4,5},{5,6},{6,7},{8,9},{9,10},{10,11},{11... | collective-permute-start | bytes 983048 | tf_op jit(solution)/shard_map/ppermute | solution.py:25
  89.7 7.6 %shard_map.69 = f32[4,18,16,256]{3,2,1,0:T(8,128)S(1)} custom-call(f32[4,26,16,256]{3,2,1,0:T(8,128)S(1)} %pad_maximum_fusion.3.b_ref, f32[7,32,16,256]{3,2,1,0:T(8,128)} %copy-done, f32[34,16,256]{2,1,0:T(8,128)S(1)} %broadcast_in_dim.100.m_ref), custom_call_target="tpu_custom_call" | custom-call | tf_op jit(solution)/shard_map/pallas_call | solution.py:91
  97.4 7.3 %shard_map.67 = f32[4,18,16,256]{3,2,1,0:T(8,128)S(1)} custom-call(f32[4,26,16,256]{3,2,1,0:T(8,128)S(1)} %pad_maximum_fusion.2.b_ref, f32[7,32,16,256]{3,2,1,0:T(8,128)} %copy-done, f32[34,16,256]{2,1,0:T(8,128)S(1)} %broadcast_in_dim.100.m_ref), custom_call_target="tpu_custom_call" | custom-call | tf_op jit(solution)/shard_map/pallas_call | solution.py:91
  105.2 2.7 %fusion.6 = f32[2,16,16,256]{3,2,1,0:T(8,128)S(1)} fusion(f32[4,2,16,16,256]{4,3,2,1,0:T(8,128)S(1)} %slice.333, f32[4,2,18,16,256]{4,3,2,1,0:T(8,128)S(1)} %bitcast.114, f32[4,16,16,256]{3,2,1,0:T(8,128)S(1)} %get-tuple-element.25, f32[4,16,16,256]{3,2,1,0:T(8,128)S(1)} %get-tuple-element.24, f32[4,16,16,256]{3,2,1,0:T(8,128)S(1)} %get-tuple-element.26, ...), kind=kLoop, calls=%fused_computation.18 | loop fusion | flops 9306112 | bytes 13107200 | tf_op jit(solution)/shard_map/reduce_sum | solution.py:297
  (83 shorter events, 21.4 us)
Async XLA Ops:
  0.0 10.9 %copy-start.1 = (f32[1,16,16,256]{3,2,1,0:T(8,128)S(1)}, f32[1,16,16,256]{3,2,1,0:T(8,128)}, u32[]{:S(2)}) copy-start(f32[1,16,16,256]{3,2,1,0:T(8,128)} %param.10) | copy-start | bytes 786436
  0.0 10.8 %copy-start.3 = (f32[2,16,16,256]{3,2,1,0:T(8,128)S(1)}, f32[2,16,16,256]{3,2,1,0:T(8,128)}, u32[]{:S(2)}) copy-start(f32[2,16,16,256]{3,2,1,0:T(8,128)} %param.7) | copy-start | bytes 1572868
  5.1 17.2 %collective-permute-start.4 = (f32[1,65552]{1,0:T(1,128)}, f32[1,65552]{1,0:T(1,128)S(1)}, u32[]{:S(2)}, u32[]{:S(2)}) collective-permute-start(f32[1,65552]{1,0:T(1,128)} %dynamic-update-slice.2), channel_id=1, source_target_pairs={{0,24},{8,0},{16,8},{24,16},{1,25},{9,1},{17,9},{25,17},{2,26},{10... | collective-permute-start | bytes 786632 | tf_op jit(solution)/shard_map/ppermute | solution.py:209
  5.3 19.2 %collective-permute-start.3 = (f32[1,65552]{1,0:T(1,128)}, f32[1,65552]{1,0:T(1,128)S(1)}, u32[]{:S(2)}, u32[]{:S(2)}) collective-permute-start(f32[1,65552]{1,0:T(1,128)} %dynamic-update-slice.2), channel_id=1, source_target_pairs={{0,16},{8,24},{16,0},{24,8},{1,17},{9,25},{17,1},{25,9},{2,18},{10... | collective-permute-start | bytes 786632 | tf_op jit(solution)/shard_map/ppermute | solution.py:209
  7.6 22.6 %collective-permute-start.2 = (f32[1,65552]{1,0:T(1,128)}, f32[1,65552]{1,0:T(1,128)S(1)}, u32[]{:S(2)}, u32[]{:S(2)}) collective-permute-start(f32[1,65552]{1,0:T(1,128)} %dynamic-update-slice.2), channel_id=1, source_target_pairs={{0,8},{8,16},{16,24},{24,0},{1,9},{9,17},{17,25},{25,1},{2,10},{10... | collective-permute-start | bytes 786632 | tf_op jit(solution)/shard_map/ppermute | solution.py:209
  11.0 9.2 %copy-start.4 = (s32[1,8]{1,0:T(1,128)S(1)}, s32[1,8]{1,0:T(1,128)}, u32[]{:S(2)}) copy-start(s32[1,8]{1,0:T(1,128)} %param.8) | copy-start | bytes 100
  12.2 30.8 %collective-permute-start.1 = (f32[4,9,16,256]{3,2,1,0:T(8,128)}, f32[4,9,16,256]{3,2,1,0:T(8,128)S(1)}, u32[]{:S(2)}, u32[]{:S(2)}) collective-permute-start(f32[4,9,16,256]{3,2,1,0:T(8,128)} %get-tuple-element.32), channel_id=1, source_target_pairs={{1,0},{2,1},{3,2},{4,3},{5,4},{6,5},{7,6},{9,8},{10,9},{11,10},{12... | collective-permute-start | bytes 1769480 | tf_op jit(solution)/shard_map/ppermute | solution.py:27
  15.6 27.4 %collective-permute-start = (f32[4,9,16,256]{3,2,1,0:T(8,128)}, f32[4,9,16,256]{3,2,1,0:T(8,128)S(1)}, u32[]{:S(2)}, u32[]{:S(2)}) collective-permute-start(f32[4,9,16,256]{3,2,1,0:T(8,128)} %get-tuple-element.31), channel_id=1, source_target_pairs={{0,1},{1,2},{2,3},{3,4},{4,5},{5,6},{6,7},{8,9},{9,10},{10,11},{11... | collective-permute-start | bytes 1769480 | tf_op jit(solution)/shard_map/ppermute | solution.py:25
  19.2 3.1 %copy-start.2 = (f32[16,16,256]{2,1,0:T(8,128)S(1)}, f32[16,16,256]{2,1,0:T(8,128)}, u32[]{:S(2)}) copy-start(f32[16,16,256]{2,1,0:T(8,128)} %param.11) | copy-start | bytes 786436
  32.2 16.8 %collective-permute-start.6 = (f32[3,9,16,256]{3,2,1,0:T(8,128)}, f32[3,9,16,256]{3,2,1,0:T(8,128)}, u32[]{:S(2)}, u32[]{:S(2)}) collective-permute-start(f32[3,9,16,256]{3,2,1,0:T(8,128)} %get-tuple-element.44), channel_id=1, source_target_pairs={{1,0},{2,1},{3,2},{4,3},{5,4},{6,5},{7,6},{9,8},{10,9},{11,10},{12... | collective-permute-start | bytes 1327112 | tf_op jit(solution)/shard_map/ppermute | solution.py:27
  35.3 13.7 %collective-permute-start.5 = (f32[3,9,16,256]{3,2,1,0:T(8,128)}, f32[3,9,16,256]{3,2,1,0:T(8,128)}, u32[]{:S(2)}, u32[]{:S(2)}) collective-permute-start(f32[3,9,16,256]{3,2,1,0:T(8,128)} %get-tuple-element.43), channel_id=1, source_target_pairs={{0,1},{1,2},{2,3},{3,4},{4,5},{5,6},{6,7},{8,9},{9,10},{10,11},{11... | collective-permute-start | bytes 1327112 | tf_op jit(solution)/shard_map/ppermute | solution.py:25
  44.6 2.3 %copy-start = (f32[7,32,16,256]{3,2,1,0:T(8,128)}, f32[7,32,16,256]{3,2,1,0:T(8,128)S(1)}, u32[]{:S(2)}) copy-start(f32[7,32,16,256]{3,2,1,0:T(8,128)S(1)} %bitcast_dynamic-update-slice_fusion.k_ref) | copy-start | bytes 11010052
  75.4 14.1 %collective-permute-start.10 = (f32[4,5,16,256]{3,2,1,0:T(8,128)S(1)}, f32[4,5,16,256]{3,2,1,0:T(8,128)S(1)}, u32[]{:S(2)}, u32[]{:S(2)}) collective-permute-start(f32[4,5,16,256]{3,2,1,0:T(8,128)S(1)} %get-tuple-element.30), channel_id=1, source_target_pairs={{1,0},{2,1},{3,2},{4,3},{5,4},{6,5},{7,6},{9,8},{10,9},{11,10},{12... | collective-permute-start | bytes 983048 | tf_op jit(solution)/shard_map/ppermute | solution.py:27
  77.3 12.2 %collective-permute-start.9 = (f32[4,5,16,256]{3,2,1,0:T(8,128)S(1)}, f32[4,5,16,256]{3,2,1,0:T(8,128)S(1)}, u32[]{:S(2)}, u32[]{:S(2)}) collective-permute-start(f32[4,5,16,256]{3,2,1,0:T(8,128)S(1)} %get-tuple-element.29), channel_id=1, source_target_pairs={{0,1},{1,2},{2,3},{3,4},{4,5},{5,6},{6,7},{8,9},{9,10},{10,11},{11... | collective-permute-start | bytes 983048 | tf_op jit(solution)/shard_map/ppermute | solution.py:25
  81.9 15.3 %collective-permute-start.8 = (f32[4,5,16,256]{3,2,1,0:T(8,128)S(1)}, f32[4,5,16,256]{3,2,1,0:T(8,128)S(1)}, u32[]{:S(2)}, u32[]{:S(2)}) collective-permute-start(f32[4,5,16,256]{3,2,1,0:T(8,128)S(1)} %get-tuple-element.28), channel_id=1, source_target_pairs={{1,0},{2,1},{3,2},{4,3},{5,4},{6,5},{7,6},{9,8},{10,9},{11,10},{12... | collective-permute-start | bytes 983048 | tf_op jit(solution)/shard_map/ppermute | solution.py:27
  83.9 13.4 %collective-permute-start.7 = (f32[4,5,16,256]{3,2,1,0:T(8,128)S(1)}, f32[4,5,16,256]{3,2,1,0:T(8,128)S(1)}, u32[]{:S(2)}, u32[]{:S(2)}) collective-permute-start(f32[4,5,16,256]{3,2,1,0:T(8,128)S(1)} %get-tuple-element.27), channel_id=1, source_target_pairs={{0,1},{1,2},{2,3},{3,4},{4,5},{5,6},{6,7},{8,9},{9,10},{10,11},{11... | collective-permute-start | bytes 983048 | tf_op jit(solution)/shard_map/ppermute | solution.py:25

commit v7 on v6

--- a/solution.py
+++ b/solution.py
@@ -51,7 +51,6 @@
         def step(r, c, turn=turn, src=src, dst=dst, keep=keep, push=push):
             face = r - 1 + offset
             coeff = [k_ref[j, face] for j in range(7)]
-            gate = m_ref[r + offset]
             for f in range(block):
                 here = src[f, r]
                 image = coeff[6] * here - coeff[0] * src[f, r + 1]
@@ -66,7 +65,7 @@
                 else:
                     summed = sol[f, r] + here
                     fresh = res[f, r] - image
-                after = (keep * here + push * fresh) * gate
+                after = keep * here + push * fresh
                 if turn == CHEB - 1:
                     o_ref[f, r - CHEB] = summed + after
                 else:
@@ -246,7 +245,7 @@
                 + perm_faces[3] + perm_faces[4] + perm_faces[5]
             ),
         ]
-    )
+    ) * mask_ext[None, 1:-1]
     mask_full = jnp.broadcast_to(mask_ext, (rows_ext, rows_y, depth_z))
 
     def solve(right_side, halo):

time: 110 us -> 109 us (level)
  Pallas kernels: 38 us -> 36.5 us
    pallas_call x6, Pallas kernels: 38 us -> 36.5 us  [kernel_solve(): pl.pallas_call(body, grid=(fields // block,), in_specs=[pl.BlockSpec((blo...]
  transfers between devices with their start and end apart: 11 -> 11, of which waited for: 2 -> 2; matrix products, arithmetic and copies ran while one was open for 16% -> 17% of each run, Pallas kernels for 9% -> 8%
where the time goes in v7:
time: 109 us; the launch traced here: 108 us
  Pallas kernels  36.5 us (33%)
  starting transfers between devices  30.7 us (28%)
  other arithmetic  24.7 us (23%)
  local copies, waits for them, and re-layouts  7.77 us (7%)
  waiting for transfers between devices  7.77 us (7%)
    pallas_call x6, Pallas kernels, kernel_solve(): pl.pallas_call(body, grid=(fields // block,), in_specs=[pl.BlockSpec((blo...  36.5 us
    ppermute x4, starting transfers between devices, with_halo(): lax.ppermute(tail, axis, [(i, i + 1) for i in range(ends)])  15.6 us
    ppermute x4, starting transfers between devices, with_halo(): lax.ppermute(head, axis, [(i + 1, i) for i in range(ends)])  10.4 us
    ppermute x3, waiting for transfers between devices, shards(): lax.ppermute(packed, 'test', [(i, (i + shift) % groups) for i in range(gr...  7.75 us
    ppermute x3, starting transfers between devices, shards(): lax.ppermute(packed, 'test', [(i, (i + shift) % groups) for i in range(gr...  4.67 us
    unnamed x14, local copies, waits for them, and re-layouts  3.37 us
    mul x2, other arithmetic, begin(): forcing = forcing * rows_of(mask_ext, state_halo - 1)  3 us
    reduce_sum x1, other arithmetic, shards(): contrib = jnp.sum(pairs(state[:, None], adjoint), axis=0)  2.72 us
  transfers between devices with their start and end apart: 11, of which 2 were waited for; matrix products, arithmetic and copies ran while one was open for 17% of the time, Pallas kernels for 8%

profile of v7, /device:TPU:11, one launch (start us, length us, event | category | flops | bytes accessed | tf_op | source)
XLA Modules:
  0.0 108.0 jit_solution(8005136612863064675)
XLA Ops:
  5.3 2.3 %collective-permute-start.3 = (f32[1,65552]{1,0:T(1,128)}, f32[1,65552]{1,0:T(1,128)S(1)}, u32[]{:S(2)}, u32[]{:S(2)}) collective-permute-start(f32[1,65552]{1,0:T(1,128)} %dynamic-update-slice.2), channel_id=1, source_target_pairs={{0,16},{8,24},{16,0},{24,8},{1,17},{9,25},{17,1},{25,9},{2,18},{10... | collective-permute-start | bytes 786632 | tf_op jit(solution)/shard_map/ppermute | solution.py:208
  7.6 2.2 %collective-permute-start.2 = (f32[1,65552]{1,0:T(1,128)}, f32[1,65552]{1,0:T(1,128)S(1)}, u32[]{:S(2)}, u32[]{:S(2)}) collective-permute-start(f32[1,65552]{1,0:T(1,128)} %dynamic-update-slice.2), channel_id=1, source_target_pairs={{0,8},{8,16},{16,24},{24,0},{1,9},{9,17},{17,25},{25,1},{2,10},{10... | collective-permute-start | bytes 786632 | tf_op jit(solution)/shard_map/ppermute | solution.py:208
  12.2 3.4 %collective-permute-start.1 = (f32[4,9,16,256]{3,2,1,0:T(8,128)}, f32[4,9,16,256]{3,2,1,0:T(8,128)S(1)}, u32[]{:S(2)}, u32[]{:S(2)}) collective-permute-start(f32[4,9,16,256]{3,2,1,0:T(8,128)} %get-tuple-element.32), channel_id=1, source_target_pairs={{1,0},{2,1},{3,2},{4,3},{5,4},{6,5},{7,6},{9,8},{10,9},{11,10},{12... | collective-permute-start | bytes 1769480 | tf_op jit(solution)/shard_map/ppermute | solution.py:27
  15.6 3.0 %collective-permute-start = (f32[4,9,16,256]{3,2,1,0:T(8,128)}, f32[4,9,16,256]{3,2,1,0:T(8,128)S(1)}, u32[]{:S(2)}, u32[]{:S(2)}) collective-permute-start(f32[4,9,16,256]{3,2,1,0:T(8,128)} %get-tuple-element.31), channel_id=1, source_target_pairs={{0,1},{1,2},{2,3},{3,4},{4,5},{5,6},{6,7},{8,9},{9,10},{10,11},{11... | collective-permute-start | bytes 1769480 | tf_op jit(solution)/shard_map/ppermute | solution.py:25
  22.4 2.1 %collective-permute-done.3 = f32[1,65552]{1,0:T(1,128)S(1)} collective-permute-done((f32[1,65552]{1,0:T(1,128)}, f32[1,65552]{1,0:T(1,128)S(1)}, u32[]{:S(2)}, u32[]{:S(2)}) %collective-permute-start.3) | collective-permute-done | bytes 262240 | tf_op jit(solution)/shard_map/ppermute | solution.py:208
  24.5 5.6 %collective-permute-done.2 = f32[1,65552]{1,0:T(1,128)S(1)} collective-permute-done((f32[1,65552]{1,0:T(1,128)}, f32[1,65552]{1,0:T(1,128)S(1)}, u32[]{:S(2)}, u32[]{:S(2)}) %collective-permute-start.2) | collective-permute-done | bytes 262240 | tf_op jit(solution)/shard_map/ppermute | solution.py:208
  32.2 3.1 %collective-permute-start.6 = (f32[3,9,16,256]{3,2,1,0:T(8,128)}, f32[3,9,16,256]{3,2,1,0:T(8,128)}, u32[]{:S(2)}, u32[]{:S(2)}) collective-permute-start(f32[3,9,16,256]{3,2,1,0:T(8,128)} %get-tuple-element.44), channel_id=1, source_target_pairs={{1,0},{2,1},{3,2},{4,3},{5,4},{6,5},{7,6},{9,8},{10,9},{11,10},{12... | collective-permute-start | bytes 1327112 | tf_op jit(solution)/shard_map/ppermute | solution.py:27
  35.3 3.5 %collective-permute-start.5 = (f32[3,9,16,256]{3,2,1,0:T(8,128)}, f32[3,9,16,256]{3,2,1,0:T(8,128)}, u32[]{:S(2)}, u32[]{:S(2)}) collective-permute-start(f32[3,9,16,256]{3,2,1,0:T(8,128)} %get-tuple-element.43), channel_id=1, source_target_pairs={{0,1},{1,2},{2,3},{3,4},{4,5},{5,6},{6,7},{8,9},{9,10},{10,11},{11... | collective-permute-start | bytes 1327112 | tf_op jit(solution)/shard_map/ppermute | solution.py:25
  38.9 1.8 %broadcast_compare_fusion = pred[3,8,34,16,256]{4,3,2,1,0:T(8,128)(4,1)S(1)} fusion(s32[34,16,256]{2,1,0:T(8,128)S(1)} %iota_add_fusion, s32[3,8]{1,0:T(4,128)S(1)} %get-tuple-element.36), kind=kLoop, calls=%fused_computation.1 | loop fusion | flops 3342336 | bytes 3899488 | tf_op jit(solution)/shard_map/eq | solution.py:260
  41.6 1.4 %select_reduce_fusion = f32[3,34,16,256]{3,2,1,0:T(8,128)S(1)} fusion(f32[3,8]{1,0:T(4,128)S(1)} %get-tuple-element.37, s32[34,16,256]{2,1,0:T(8,128)S(1)} %iota_add_fusion, s32[3,8]{1,0:T(4,128)S(1)} %get-tuple-element.36), kind=kLoop, calls=%fused_computation | loop fusion | flops 9609216 | bytes 2228416 | tf_op jit(solution)/shard_map/reduce_sum | solution.py:261
  45.6 1.9 %shard_map.64 = f32[1,26,16,256]{3,2,1,0:T(8,128)S(1)} custom-call(f32[1,34,16,256]{3,2,1,0:T(8,128)S(1)} %slice_add_fusion.2.b_ref, f32[7,32,16,256]{3,2,1,0:T(8,128)S(1)} %broadcast_multiply_fusion.k_ref, f32[34,16,256]{2,1,0:T(8,128)S(1)} %broadcast_in_dim.101.m_ref), custom_call_target="tpu_custom_call" | custom-call | tf_op jit(solution)/shard_map/pallas_call | solution.py:90
  48.2 1.4 %negate_multiply_fusion.1 = (f32[1,2,24,16,256]{4,3,2,1,0:T(8,128)S(1)}, f32[2,24,16,256]{3,2,1,0:T(8,128)S(1)}, f32[2,24,16,256]{3,2,1,0:T(8,128)S(1)}, f32[2,2...) fusion(f32[24]{0:T(128)S(1)} %slice.275, ...), kind=kLoop, calls=%fused_computation.94 | loop fusion | flops 5701632 | bytes 10223712 | tf_op jit(solution)/shard_map/mul | solution.py:267
  49.6 1.5 %maximum_add_fusion.b_ref = f32[3,34,16,256]{3,2,1,0:T(8,128)S(1)} fusion(f32[3,34,16,256]{3,2,1,0:T(8,128)S(1)} %select_reduce_fusion, f32[3,9,16,256]{3,2,1,0:T(8,128)} %collective-permute-done.6, f32[3,16,16,256]{3,2,1,0:T(8,128)S(1)} %bitcast.116, f32[3,9,16,256]{3,2,1,0:T(8,128)} %collective-permute-done.5), kind=kLoop, calls=%fused_computation.42 | loop fusion | flops 1253376 | bytes 5013504 | tf_op jit(solution)/shard_map/add | solution.py:265
  51.2 7.2 %shard_map.65 = f32[3,26,16,256]{3,2,1,0:T(8,128)S(1)} custom-call(f32[3,34,16,256]{3,2,1,0:T(8,128)S(1)} %maximum_add_fusion.b_ref, f32[7,32,16,256]{3,2,1,0:T(8,128)} %copy-done, f32[34,16,256]{2,1,0:T(8,128)S(1)} %broadcast_in_dim.101.m_ref), custom_call_target="tpu_custom_call" | custom-call | tf_op jit(solution)/shard_map/pallas_call | solution.py:90
  59.7 1.6 %negate_multiply_fusion = f32[3,2,24,16,256]{4,3,2,1,0:T(8,128)S(1)} fusion(f32[24]{0:T(128)S(1)} %slice.275, f32[3,24,16,256]{3,2,1,0:T(8,128)S(1)} %get-tuple-element.21, f32[2,24,16,256]{3,2,1,0:T(8,128)S(1)} %multiply_bitcast_fusion, f32[3,24,16,256]{3,2,1,0:T(8,128)S(1)} %get-tuple-element.20, f32[2,24,16,256]{3,2,1,0:T(8,128)S(1)} %get-tuple-element.42, ...), kind=kLoop, calls=%fused_computation.9 | loop fusion | flops 7667712 | bytes 14155872 | tf_op jit(solution)/shard_map/mul | solution.py:267
  61.7 6.5 %shard_map.66 = f32[4,16,16,256]{3,2,1,0:T(8,128)S(1)} custom-call(f32[4,24,16,256]{3,2,1,0:T(8,128)S(1)} %bitcast.112, f32[7,32,16,256]{3,2,1,0:T(8,128)} %copy-done, f32[34,16,256]{2,1,0:T(8,128)S(1)} %broadcast_in_dim.101.m_ref), custom_call_target="tpu_custom_call" | custom-call | tf_op jit(solution)/shard_map/pallas_call | solution.py:90
  68.4 6.5 %shard_map.68 = f32[4,16,16,256]{3,2,1,0:T(8,128)S(1)} custom-call(f32[4,24,16,256]{3,2,1,0:T(8,128)S(1)} %bitcast.111, f32[7,32,16,256]{3,2,1,0:T(8,128)} %copy-done, f32[34,16,256]{2,1,0:T(8,128)S(1)} %broadcast_in_dim.101.m_ref), custom_call_target="tpu_custom_call" | custom-call | tf_op jit(solution)/shard_map/pallas_call | solution.py:90
  75.1 1.9 %collective-permute-start.10 = (f32[4,5,16,256]{3,2,1,0:T(8,128)S(1)}, f32[4,5,16,256]{3,2,1,0:T(8,128)S(1)}, u32[]{:S(2)}, u32[]{:S(2)}) collective-permute-start(f32[4,5,16,256]{3,2,1,0:T(8,128)S(1)} %get-tuple-element.30), channel_id=1, source_target_pairs={{1,0},{2,1},{3,2},{4,3},{5,4},{6,5},{7,6},{9,8},{10,9},{11,10},{12... | collective-permute-start | bytes 983048 | tf_op jit(solution)/shard_map/ppermute | solution.py:27
  77.1 4.5 %collective-permute-start.9 = (f32[4,5,16,256]{3,2,1,0:T(8,128)S(1)}, f32[4,5,16,256]{3,2,1,0:T(8,128)S(1)}, u32[]{:S(2)}, u32[]{:S(2)}) collective-permute-start(f32[4,5,16,256]{3,2,1,0:T(8,128)S(1)} %get-tuple-element.29), channel_id=1, source_target_pairs={{0,1},{1,2},{2,3},{3,4},{4,5},{5,6},{6,7},{8,9},{9,10},{10,11},{11... | collective-permute-start | bytes 983048 | tf_op jit(solution)/shard_map/ppermute | solution.py:25
  81.7 1.9 %collective-permute-start.8 = (f32[4,5,16,256]{3,2,1,0:T(8,128)S(1)}, f32[4,5,16,256]{3,2,1,0:T(8,128)S(1)}, u32[]{:S(2)}, u32[]{:S(2)}) collective-permute-start(f32[4,5,16,256]{3,2,1,0:T(8,128)S(1)} %get-tuple-element.28), channel_id=1, source_target_pairs={{1,0},{2,1},{3,2},{4,3},{5,4},{6,5},{7,6},{9,8},{10,9},{11,10},{12... | collective-permute-start | bytes 983048 | tf_op jit(solution)/shard_map/ppermute | solution.py:27
  83.6 4.5 %collective-permute-start.7 = (f32[4,5,16,256]{3,2,1,0:T(8,128)S(1)}, f32[4,5,16,256]{3,2,1,0:T(8,128)S(1)}, u32[]{:S(2)}, u32[]{:S(2)}) collective-permute-start(f32[4,5,16,256]{3,2,1,0:T(8,128)S(1)} %get-tuple-element.27), channel_id=1, source_target_pairs={{0,1},{1,2},{2,3},{3,4},{4,5},{5,6},{6,7},{8,9},{9,10},{10,11},{11... | collective-permute-start | bytes 983048 | tf_op jit(solution)/shard_map/ppermute | solution.py:25
  89.4 7.3 %shard_map.69 = f32[4,18,16,256]{3,2,1,0:T(8,128)S(1)} custom-call(f32[4,26,16,256]{3,2,1,0:T(8,128)S(1)} %pad_maximum_fusion.3.b_ref, f32[7,32,16,256]{3,2,1,0:T(8,128)} %copy-done, f32[34,16,256]{2,1,0:T(8,128)S(1)} %broadcast_in_dim.101.m_ref), custom_call_target="tpu_custom_call" | custom-call | tf_op jit(solution)/shard_map/pallas_call | solution.py:90
  96.9 7.0 %shard_map.67 = f32[4,18,16,256]{3,2,1,0:T(8,128)S(1)} custom-call(f32[4,26,16,256]{3,2,1,0:T(8,128)S(1)} %pad_maximum_fusion.2.b_ref, f32[7,32,16,256]{3,2,1,0:T(8,128)} %copy-done, f32[34,16,256]{2,1,0:T(8,128)S(1)} %broadcast_in_dim.101.m_ref), custom_call_target="tpu_custom_call" | custom-call | tf_op jit(solution)/shard_map/pallas_call | solution.py:90
  104.4 2.7 %fusion.6 = f32[2,16,16,256]{3,2,1,0:T(8,128)S(1)} fusion(f32[4,2,16,16,256]{4,3,2,1,0:T(8,128)S(1)} %slice.338, f32[4,2,18,16,256]{4,3,2,1,0:T(8,128)S(1)} %bitcast.114, f32[4,16,16,256]{3,2,1,0:T(8,128)S(1)} %get-tuple-element.25, f32[4,16,16,256]{3,2,1,0:T(8,128)S(1)} %get-tuple-element.24, f32[4,16,16,256]{3,2,1,0:T(8,128)S(1)} %get-tuple-element.26, ...), kind=kLoop, calls=%fused_computation.18 | loop fusion | flops 9306112 | bytes 13107200 | tf_op jit(solution)/shard_map/reduce_sum | solution.py:296
  (85 shorter events, 22.2 us)
Async XLA Ops:
  0.0 10.9 %copy-start.1 = (f32[1,16,16,256]{3,2,1,0:T(8,128)S(1)}, f32[1,16,16,256]{3,2,1,0:T(8,128)}, u32[]{:S(2)}) copy-start(f32[1,16,16,256]{3,2,1,0:T(8,128)} %param.10) | copy-start | bytes 786436
  0.0 10.8 %copy-start.3 = (f32[2,16,16,256]{3,2,1,0:T(8,128)S(1)}, f32[2,16,16,256]{3,2,1,0:T(8,128)}, u32[]{:S(2)}) copy-start(f32[2,16,16,256]{3,2,1,0:T(8,128)} %param.7) | copy-start | bytes 1572868
  5.1 17.3 %collective-permute-start.4 = (f32[1,65552]{1,0:T(1,128)}, f32[1,65552]{1,0:T(1,128)S(1)}, u32[]{:S(2)}, u32[]{:S(2)}) collective-permute-start(f32[1,65552]{1,0:T(1,128)} %dynamic-update-slice.2), channel_id=1, source_target_pairs={{0,24},{8,0},{16,8},{24,16},{1,25},{9,1},{17,9},{25,17},{2,26},{10... | collective-permute-start | bytes 786632 | tf_op jit(solution)/shard_map/ppermute | solution.py:208
  5.3 19.2 %collective-permute-start.3 = (f32[1,65552]{1,0:T(1,128)}, f32[1,65552]{1,0:T(1,128)S(1)}, u32[]{:S(2)}, u32[]{:S(2)}) collective-permute-start(f32[1,65552]{1,0:T(1,128)} %dynamic-update-slice.2), channel_id=1, source_target_pairs={{0,16},{8,24},{16,0},{24,8},{1,17},{9,25},{17,1},{25,9},{2,18},{10... | collective-permute-start | bytes 786632 | tf_op jit(solution)/shard_map/ppermute | solution.py:208
  7.6 22.6 %collective-permute-start.2 = (f32[1,65552]{1,0:T(1,128)}, f32[1,65552]{1,0:T(1,128)S(1)}, u32[]{:S(2)}, u32[]{:S(2)}) collective-permute-start(f32[1,65552]{1,0:T(1,128)} %dynamic-update-slice.2), channel_id=1, source_target_pairs={{0,8},{8,16},{16,24},{24,0},{1,9},{9,17},{17,25},{25,1},{2,10},{10... | collective-permute-start | bytes 786632 | tf_op jit(solution)/shard_map/ppermute | solution.py:208
  11.0 9.2 %copy-start.4 = (s32[1,8]{1,0:T(1,128)S(1)}, s32[1,8]{1,0:T(1,128)}, u32[]{:S(2)}) copy-start(s32[1,8]{1,0:T(1,128)} %param.8) | copy-start | bytes 100
  12.2 30.8 %collective-permute-start.1 = (f32[4,9,16,256]{3,2,1,0:T(8,128)}, f32[4,9,16,256]{3,2,1,0:T(8,128)S(1)}, u32[]{:S(2)}, u32[]{:S(2)}) collective-permute-start(f32[4,9,16,256]{3,2,1,0:T(8,128)} %get-tuple-element.32), channel_id=1, source_target_pairs={{1,0},{2,1},{3,2},{4,3},{5,4},{6,5},{7,6},{9,8},{10,9},{11,10},{12... | collective-permute-start | bytes 1769480 | tf_op jit(solution)/shard_map/ppermute | solution.py:27
  15.6 27.4 %collective-permute-start = (f32[4,9,16,256]{3,2,1,0:T(8,128)}, f32[4,9,16,256]{3,2,1,0:T(8,128)S(1)}, u32[]{:S(2)}, u32[]{:S(2)}) collective-permute-start(f32[4,9,16,256]{3,2,1,0:T(8,128)} %get-tuple-element.31), channel_id=1, source_target_pairs={{0,1},{1,2},{2,3},{3,4},{4,5},{5,6},{6,7},{8,9},{9,10},{10,11},{11... | collective-permute-start | bytes 1769480 | tf_op jit(solution)/shard_map/ppermute | solution.py:25
  19.2 3.2 %copy-start.2 = (f32[16,16,256]{2,1,0:T(8,128)S(1)}, f32[16,16,256]{2,1,0:T(8,128)}, u32[]{:S(2)}) copy-start(f32[16,16,256]{2,1,0:T(8,128)} %param.11) | copy-start | bytes 786436
  32.2 17.4 %collective-permute-start.6 = (f32[3,9,16,256]{3,2,1,0:T(8,128)}, f32[3,9,16,256]{3,2,1,0:T(8,128)}, u32[]{:S(2)}, u32[]{:S(2)}) collective-permute-start(f32[3,9,16,256]{3,2,1,0:T(8,128)} %get-tuple-element.44), channel_id=1, source_target_pairs={{1,0},{2,1},{3,2},{4,3},{5,4},{6,5},{7,6},{9,8},{10,9},{11,10},{12... | collective-permute-start | bytes 1327112 | tf_op jit(solution)/shard_map/ppermute | solution.py:27
  35.3 14.3 %collective-permute-start.5 = (f32[3,9,16,256]{3,2,1,0:T(8,128)}, f32[3,9,16,256]{3,2,1,0:T(8,128)}, u32[]{:S(2)}, u32[]{:S(2)}) collective-permute-start(f32[3,9,16,256]{3,2,1,0:T(8,128)} %get-tuple-element.43), channel_id=1, source_target_pairs={{0,1},{1,2},{2,3},{3,4},{4,5},{5,6},{6,7},{8,9},{9,10},{10,11},{11... | collective-permute-start | bytes 1327112 | tf_op jit(solution)/shard_map/ppermute | solution.py:25
  45.5 2.0 %copy-start = (f32[7,32,16,256]{3,2,1,0:T(8,128)}, f32[7,32,16,256]{3,2,1,0:T(8,128)S(1)}, u32[]{:S(2)}) copy-start(f32[7,32,16,256]{3,2,1,0:T(8,128)S(1)} %broadcast_multiply_fusion.k_ref) | copy-start | bytes 11010052
  75.1 14.1 %collective-permute-start.10 = (f32[4,5,16,256]{3,2,1,0:T(8,128)S(1)}, f32[4,5,16,256]{3,2,1,0:T(8,128)S(1)}, u32[]{:S(2)}, u32[]{:S(2)}) collective-permute-start(f32[4,5,16,256]{3,2,1,0:T(8,128)S(1)} %get-tuple-element.30), channel_id=1, source_target_pairs={{1,0},{2,1},{3,2},{4,3},{5,4},{6,5},{7,6},{9,8},{10,9},{11,10},{12... | collective-permute-start | bytes 983048 | tf_op jit(solution)/shard_map/ppermute | solution.py:27
  77.1 12.2 %collective-permute-start.9 = (f32[4,5,16,256]{3,2,1,0:T(8,128)S(1)}, f32[4,5,16,256]{3,2,1,0:T(8,128)S(1)}, u32[]{:S(2)}, u32[]{:S(2)}) collective-permute-start(f32[4,5,16,256]{3,2,1,0:T(8,128)S(1)} %get-tuple-element.29), channel_id=1, source_target_pairs={{0,1},{1,2},{2,3},{3,4},{4,5},{5,6},{6,7},{8,9},{9,10},{10,11},{11... | collective-permute-start | bytes 983048 | tf_op jit(solution)/shard_map/ppermute | solution.py:25
  81.7 15.0 %collective-permute-start.8 = (f32[4,5,16,256]{3,2,1,0:T(8,128)S(1)}, f32[4,5,16,256]{3,2,1,0:T(8,128)S(1)}, u32[]{:S(2)}, u32[]{:S(2)}) collective-permute-start(f32[4,5,16,256]{3,2,1,0:T(8,128)S(1)} %get-tuple-element.28), channel_id=1, source_target_pairs={{1,0},{2,1},{3,2},{4,3},{5,4},{6,5},{7,6},{9,8},{10,9},{11,10},{12... | collective-permute-start | bytes 983048 | tf_op jit(solution)/shard_map/ppermute | solution.py:27
  83.6 13.1 %collective-permute-start.7 = (f32[4,5,16,256]{3,2,1,0:T(8,128)S(1)}, f32[4,5,16,256]{3,2,1,0:T(8,128)S(1)}, u32[]{:S(2)}, u32[]{:S(2)}) collective-permute-start(f32[4,5,16,256]{3,2,1,0:T(8,128)S(1)} %get-tuple-element.27), channel_id=1, source_target_pairs={{0,1},{1,2},{2,3},{3,4},{4,5},{5,6},{6,7},{8,9},{9,10},{10,11},{11... | collective-permute-start | bytes 983048 | tf_op jit(solution)/shard_map/ppermute | solution.py:25

commit v8 on v7

--- a/solution.py
+++ b/solution.py
@@ -33,7 +33,7 @@
 INTERPRET = False
 
 
-def solve_kernel(b_ref, k_ref, m_ref, o_ref, sol, res, da, db, *, offset, first, keeps, pushes):
+def solve_kernel(b_ref, k_ref, o_ref, sol, res, da, db, *, offset, first, keeps, pushes):
     block, rows, rows_y, depth_z = sol.shape
 
     def init(r, c):
@@ -77,7 +77,7 @@
         lax.fori_loop(turn + 1, rows - 1 - turn, step, 0, unroll=True)
 
 
-def kernel_solve(right_side, face_stack, mask_full, offset, first, keeps, pushes):
+def kernel_solve(right_side, face_stack, offset, first, keeps, pushes):
     fields, rows, rows_y, depth_z = right_side.shape
     block = 2 if fields % 2 == 0 else 1
     body = functools.partial(
@@ -93,7 +93,6 @@
         in_specs=[
             pl.BlockSpec((block, rows, rows_y, depth_z), lambda f: (f, 0, 0, 0)),
             pl.BlockSpec(face_stack.shape, lambda f: (0, 0, 0, 0)),
-            pl.BlockSpec(mask_full.shape, lambda f: (0, 0, 0)),
         ],
         out_specs=pl.BlockSpec((block, rows - 2 * CHEB, rows_y, depth_z), lambda f: (f, 0, 0, 0)),
         out_shape=jax.ShapeDtypeStruct((fields, rows - 2 * CHEB, rows_y, depth_z), jnp.float32),
@@ -102,7 +101,7 @@
         ],
         compiler_params=pltpu.CompilerParams(vmem_limit_bytes=48 * 1024 * 1024),
         interpret=INTERPRET,
-    )(right_side, face_stack, mask_full)
+    )(right_side, face_stack)
 
 
 def cheb_table(count):
@@ -246,13 +245,12 @@
             ),
         ]
     ) * mask_ext[None, 1:-1]
-    mask_full = jnp.broadcast_to(mask_ext, (rows_ext, rows_y, depth_z))
 
     def solve(right_side, halo):
         lead = right_side.shape[:-3]
         flat_side = right_side.reshape((-1,) + right_side.shape[-3:])
         result = kernel_solve(
-            flat_side, face_stack, mask_full, reach - halo, first, keeps, pushes
+            flat_side, face_stack, reach - halo, first, keeps, pushes
         )
         return result.reshape(lead + result.shape[-3:]), halo - CHEB
 

time: 109 us -> 109 us (level)
  no operation moved by 1% of the time
where the time goes in v8:
time: 109 us; the launch traced here: 108 us
  Pallas kernels  36.5 us (33%)
  starting transfers between devices  30.7 us (28%)
  other arithmetic  24.7 us (23%)
  waiting for transfers between devices  7.77 us (7%)
  local copies, waits for them, and re-layouts  7.67 us (7%)
    pallas_call x6, Pallas kernels, kernel_solve(): pl.pallas_call(body, grid=(fields // block,), in_specs=[pl.BlockSpec((blo...  36.5 us
    ppermute x4, starting transfers between devices, with_halo(): lax.ppermute(tail, axis, [(i, i + 1) for i in range(ends)])  15.6 us
    ppermute x4, starting transfers between devices, with_halo(): lax.ppermute(head, axis, [(i + 1, i) for i in range(ends)])  10.4 us
    ppermute x3, waiting for transfers between devices, shards(): lax.ppermute(packed, 'test', [(i, (i + shift) % groups) for i in range(gr...  7.75 us
    ppermute x3, starting transfers between devices, shards(): lax.ppermute(packed, 'test', [(i, (i + shift) % groups) for i in range(gr...  4.67 us
    unnamed x14, local copies, waits for them, and re-layouts  3.37 us
    mul x2, other arithmetic, begin(): forcing = forcing * rows_of(mask_ext, state_halo - 1)  3 us
    reduce_sum x1, other arithmetic, shards(): contrib = jnp.sum(pairs(state[:, None], adjoint), axis=0)  2.75 us
  transfers between devices with their start and end apart: 11, of which 2 were waited for; matrix products, arithmetic and copies ran while one was open for 17% of the time, Pallas kernels for 8%

profile of v8, /device:TPU:11, one launch (start us, length us, event | category | flops | bytes accessed | tf_op | source)
XLA Modules:
  0.0 107.9 jit_solution(1054273521328510092)
XLA Ops:
  5.3 2.3 %collective-permute-start.3 = (f32[1,65552]{1,0:T(1,128)}, f32[1,65552]{1,0:T(1,128)S(1)}, u32[]{:S(2)}, u32[]{:S(2)}) collective-permute-start(f32[1,65552]{1,0:T(1,128)} %dynamic-update-slice.2), channel_id=1, source_target_pairs={{0,16},{8,24},{16,0},{24,8},{1,17},{9,25},{17,1},{25,9},{2,18},{10... | collective-permute-start | bytes 786632 | tf_op jit(solution)/shard_map/ppermute | solution.py:207
  7.6 2.2 %collective-permute-start.2 = (f32[1,65552]{1,0:T(1,128)}, f32[1,65552]{1,0:T(1,128)S(1)}, u32[]{:S(2)}, u32[]{:S(2)}) collective-permute-start(f32[1,65552]{1,0:T(1,128)} %dynamic-update-slice.2), channel_id=1, source_target_pairs={{0,8},{8,16},{16,24},{24,0},{1,9},{9,17},{17,25},{25,1},{2,10},{10... | collective-permute-start | bytes 786632 | tf_op jit(solution)/shard_map/ppermute | solution.py:207
  12.2 3.4 %collective-permute-start.1 = (f32[4,9,16,256]{3,2,1,0:T(8,128)}, f32[4,9,16,256]{3,2,1,0:T(8,128)S(1)}, u32[]{:S(2)}, u32[]{:S(2)}) collective-permute-start(f32[4,9,16,256]{3,2,1,0:T(8,128)} %get-tuple-element.32), channel_id=1, source_target_pairs={{1,0},{2,1},{3,2},{4,3},{5,4},{6,5},{7,6},{9,8},{10,9},{11,10},{12... | collective-permute-start | bytes 1769480 | tf_op jit(solution)/shard_map/ppermute | solution.py:27
  15.6 3.0 %collective-permute-start = (f32[4,9,16,256]{3,2,1,0:T(8,128)}, f32[4,9,16,256]{3,2,1,0:T(8,128)S(1)}, u32[]{:S(2)}, u32[]{:S(2)}) collective-permute-start(f32[4,9,16,256]{3,2,1,0:T(8,128)} %get-tuple-element.31), channel_id=1, source_target_pairs={{0,1},{1,2},{2,3},{3,4},{4,5},{5,6},{6,7},{8,9},{9,10},{10,11},{11... | collective-permute-start | bytes 1769480 | tf_op jit(solution)/shard_map/ppermute | solution.py:25
  22.4 2.1 %collective-permute-done.3 = f32[1,65552]{1,0:T(1,128)S(1)} collective-permute-done((f32[1,65552]{1,0:T(1,128)}, f32[1,65552]{1,0:T(1,128)S(1)}, u32[]{:S(2)}, u32[]{:S(2)}) %collective-permute-start.3) | collective-permute-done | bytes 262240 | tf_op jit(solution)/shard_map/ppermute | solution.py:207
  24.5 5.6 %collective-permute-done.2 = f32[1,65552]{1,0:T(1,128)S(1)} collective-permute-done((f32[1,65552]{1,0:T(1,128)}, f32[1,65552]{1,0:T(1,128)S(1)}, u32[]{:S(2)}, u32[]{:S(2)}) %collective-permute-start.2) | collective-permute-done | bytes 262240 | tf_op jit(solution)/shard_map/ppermute | solution.py:207
  32.2 3.1 %collective-permute-start.6 = (f32[3,9,16,256]{3,2,1,0:T(8,128)}, f32[3,9,16,256]{3,2,1,0:T(8,128)}, u32[]{:S(2)}, u32[]{:S(2)}) collective-permute-start(f32[3,9,16,256]{3,2,1,0:T(8,128)} %get-tuple-element.44), channel_id=1, source_target_pairs={{1,0},{2,1},{3,2},{4,3},{5,4},{6,5},{7,6},{9,8},{10,9},{11,10},{12... | collective-permute-start | bytes 1327112 | tf_op jit(solution)/shard_map/ppermute | solution.py:27
  35.3 3.5 %collective-permute-start.5 = (f32[3,9,16,256]{3,2,1,0:T(8,128)}, f32[3,9,16,256]{3,2,1,0:T(8,128)}, u32[]{:S(2)}, u32[]{:S(2)}) collective-permute-start(f32[3,9,16,256]{3,2,1,0:T(8,128)} %get-tuple-element.43), channel_id=1, source_target_pairs={{0,1},{1,2},{2,3},{3,4},{4,5},{5,6},{6,7},{8,9},{9,10},{10,11},{11... | collective-permute-start | bytes 1327112 | tf_op jit(solution)/shard_map/ppermute | solution.py:25
  38.9 1.8 %broadcast_compare_fusion = pred[3,8,34,16,256]{4,3,2,1,0:T(8,128)(4,1)S(1)} fusion(s32[34,16,256]{2,1,0:T(8,128)S(1)} %iota_add_fusion, s32[3,8]{1,0:T(4,128)S(1)} %get-tuple-element.36), kind=kLoop, calls=%fused_computation.1 | loop fusion | flops 3342336 | bytes 3899488 | tf_op jit(solution)/shard_map/eq | solution.py:258
  41.6 1.4 %select_reduce_fusion = f32[3,34,16,256]{3,2,1,0:T(8,128)S(1)} fusion(f32[3,8]{1,0:T(4,128)S(1)} %get-tuple-element.37, s32[34,16,256]{2,1,0:T(8,128)S(1)} %iota_add_fusion, s32[3,8]{1,0:T(4,128)S(1)} %get-tuple-element.36), kind=kLoop, calls=%fused_computation | loop fusion | flops 9609216 | bytes 2228416 | tf_op jit(solution)/shard_map/reduce_sum | solution.py:259
  45.5 1.9 %shard_map.64 = f32[1,26,16,256]{3,2,1,0:T(8,128)S(1)} custom-call(f32[1,34,16,256]{3,2,1,0:T(8,128)S(1)} %slice_add_fusion.2.b_ref, f32[7,32,16,256]{3,2,1,0:T(8,128)S(1)} %broadcast_multiply_fusion.k_ref), custom_call_target="tpu_custom_call" | custom-call | tf_op jit(solution)/shard_map/pallas_call | solution.py:90
  48.1 1.4 %negate_multiply_fusion.1 = (f32[1,2,24,16,256]{4,3,2,1,0:T(8,128)S(1)}, f32[2,24,16,256]{3,2,1,0:T(8,128)S(1)}, f32[2,24,16,256]{3,2,1,0:T(8,128)S(1)}, f32[2,2...) fusion(f32[24]{0:T(128)S(1)} %slice.275, ...), kind=kLoop, calls=%fused_computation.94 | loop fusion | flops 5701632 | bytes 10223712 | tf_op jit(solution)/shard_map/mul | solution.py:265
  49.5 1.5 %maximum_add_fusion.b_ref = f32[3,34,16,256]{3,2,1,0:T(8,128)S(1)} fusion(f32[3,34,16,256]{3,2,1,0:T(8,128)S(1)} %select_reduce_fusion, f32[3,9,16,256]{3,2,1,0:T(8,128)} %collective-permute-done.6, f32[3,16,16,256]{3,2,1,0:T(8,128)S(1)} %bitcast.116, f32[3,9,16,256]{3,2,1,0:T(8,128)} %collective-permute-done.5), kind=kLoop, calls=%fused_computation.42 | loop fusion | flops 1253376 | bytes 5013504 | tf_op jit(solution)/shard_map/add | solution.py:263
  51.0 7.2 %shard_map.65 = f32[3,26,16,256]{3,2,1,0:T(8,128)S(1)} custom-call(f32[3,34,16,256]{3,2,1,0:T(8,128)S(1)} %maximum_add_fusion.b_ref, f32[7,32,16,256]{3,2,1,0:T(8,128)} %copy-done), custom_call_target="tpu_custom_call" | custom-call | tf_op jit(solution)/shard_map/pallas_call | solution.py:90
  59.6 1.6 %negate_multiply_fusion = f32[3,2,24,16,256]{4,3,2,1,0:T(8,128)S(1)} fusion(f32[24]{0:T(128)S(1)} %slice.275, f32[3,24,16,256]{3,2,1,0:T(8,128)S(1)} %get-tuple-element.21, f32[2,24,16,256]{3,2,1,0:T(8,128)S(1)} %multiply_bitcast_fusion, f32[3,24,16,256]{3,2,1,0:T(8,128)S(1)} %get-tuple-element.20, f32[2,24,16,256]{3,2,1,0:T(8,128)S(1)} %get-tuple-element.42, ...), kind=kLoop, calls=%fused_computation.9 | loop fusion | flops 7667712 | bytes 14155872 | tf_op jit(solution)/shard_map/mul | solution.py:265
  61.5 6.5 %shard_map.66 = f32[4,16,16,256]{3,2,1,0:T(8,128)S(1)} custom-call(f32[4,24,16,256]{3,2,1,0:T(8,128)S(1)} %bitcast.112, f32[7,32,16,256]{3,2,1,0:T(8,128)} %copy-done), custom_call_target="tpu_custom_call" | custom-call | tf_op jit(solution)/shard_map/pallas_call | solution.py:90
  68.2 6.5 %shard_map.68 = f32[4,16,16,256]{3,2,1,0:T(8,128)S(1)} custom-call(f32[4,24,16,256]{3,2,1,0:T(8,128)S(1)} %bitcast.111, f32[7,32,16,256]{3,2,1,0:T(8,128)} %copy-done), custom_call_target="tpu_custom_call" | custom-call | tf_op jit(solution)/shard_map/pallas_call | solution.py:90
  75.0 1.9 %collective-permute-start.10 = (f32[4,5,16,256]{3,2,1,0:T(8,128)S(1)}, f32[4,5,16,256]{3,2,1,0:T(8,128)S(1)}, u32[]{:S(2)}, u32[]{:S(2)}) collective-permute-start(f32[4,5,16,256]{3,2,1,0:T(8,128)S(1)} %get-tuple-element.30), channel_id=1, source_target_pairs={{1,0},{2,1},{3,2},{4,3},{5,4},{6,5},{7,6},{9,8},{10,9},{11,10},{12... | collective-permute-start | bytes 983048 | tf_op jit(solution)/shard_map/ppermute | solution.py:27
  76.9 4.5 %collective-permute-start.9 = (f32[4,5,16,256]{3,2,1,0:T(8,128)S(1)}, f32[4,5,16,256]{3,2,1,0:T(8,128)S(1)}, u32[]{:S(2)}, u32[]{:S(2)}) collective-permute-start(f32[4,5,16,256]{3,2,1,0:T(8,128)S(1)} %get-tuple-element.29), channel_id=1, source_target_pairs={{0,1},{1,2},{2,3},{3,4},{4,5},{5,6},{6,7},{8,9},{9,10},{10,11},{11... | collective-permute-start | bytes 983048 | tf_op jit(solution)/shard_map/ppermute | solution.py:25
  81.5 1.9 %collective-permute-start.8 = (f32[4,5,16,256]{3,2,1,0:T(8,128)S(1)}, f32[4,5,16,256]{3,2,1,0:T(8,128)S(1)}, u32[]{:S(2)}, u32[]{:S(2)}) collective-permute-start(f32[4,5,16,256]{3,2,1,0:T(8,128)S(1)} %get-tuple-element.28), channel_id=1, source_target_pairs={{1,0},{2,1},{3,2},{4,3},{5,4},{6,5},{7,6},{9,8},{10,9},{11,10},{12... | collective-permute-start | bytes 983048 | tf_op jit(solution)/shard_map/ppermute | solution.py:27
  83.5 4.5 %collective-permute-start.7 = (f32[4,5,16,256]{3,2,1,0:T(8,128)S(1)}, f32[4,5,16,256]{3,2,1,0:T(8,128)S(1)}, u32[]{:S(2)}, u32[]{:S(2)}) collective-permute-start(f32[4,5,16,256]{3,2,1,0:T(8,128)S(1)} %get-tuple-element.27), channel_id=1, source_target_pairs={{0,1},{1,2},{2,3},{3,4},{4,5},{5,6},{6,7},{8,9},{9,10},{10,11},{11... | collective-permute-start | bytes 983048 | tf_op jit(solution)/shard_map/ppermute | solution.py:25
  89.3 7.3 %shard_map.69 = f32[4,18,16,256]{3,2,1,0:T(8,128)S(1)} custom-call(f32[4,26,16,256]{3,2,1,0:T(8,128)S(1)} %pad_maximum_fusion.3.b_ref, f32[7,32,16,256]{3,2,1,0:T(8,128)} %copy-done), custom_call_target="tpu_custom_call" | custom-call | tf_op jit(solution)/shard_map/pallas_call | solution.py:90
  96.8 7.0 %shard_map.67 = f32[4,18,16,256]{3,2,1,0:T(8,128)S(1)} custom-call(f32[4,26,16,256]{3,2,1,0:T(8,128)S(1)} %pad_maximum_fusion.2.b_ref, f32[7,32,16,256]{3,2,1,0:T(8,128)} %copy-done), custom_call_target="tpu_custom_call" | custom-call | tf_op jit(solution)/shard_map/pallas_call | solution.py:90
  104.3 2.8 %fusion.6 = f32[2,16,16,256]{3,2,1,0:T(8,128)S(1)} fusion(f32[4,2,16,16,256]{4,3,2,1,0:T(8,128)S(1)} %slice.338, f32[4,2,18,16,256]{4,3,2,1,0:T(8,128)S(1)} %bitcast.114, f32[4,16,16,256]{3,2,1,0:T(8,128)S(1)} %get-tuple-element.25, f32[4,16,16,256]{3,2,1,0:T(8,128)S(1)} %get-tuple-element.24, f32[4,16,16,256]{3,2,1,0:T(8,128)S(1)} %get-tuple-element.26, ...), kind=kLoop, calls=%fused_computation.18 | loop fusion | flops 9306112 | bytes 13107200 | tf_op jit(solution)/shard_map/reduce_sum | solution.py:294
  (84 shorter events, 22.1 us)
Async XLA Ops:
  0.0 10.9 %copy-start.1 = (f32[1,16,16,256]{3,2,1,0:T(8,128)S(1)}, f32[1,16,16,256]{3,2,1,0:T(8,128)}, u32[]{:S(2)}) copy-start(f32[1,16,16,256]{3,2,1,0:T(8,128)} %param.10) | copy-start | bytes 786436
  0.0 10.8 %copy-start.3 = (f32[2,16,16,256]{3,2,1,0:T(8,128)S(1)}, f32[2,16,16,256]{3,2,1,0:T(8,128)}, u32[]{:S(2)}) copy-start(f32[2,16,16,256]{3,2,1,0:T(8,128)} %param.7) | copy-start | bytes 1572868
  5.1 17.3 %collective-permute-start.4 = (f32[1,65552]{1,0:T(1,128)}, f32[1,65552]{1,0:T(1,128)S(1)}, u32[]{:S(2)}, u32[]{:S(2)}) collective-permute-start(f32[1,65552]{1,0:T(1,128)} %dynamic-update-slice.2), channel_id=1, source_target_pairs={{0,24},{8,0},{16,8},{24,16},{1,25},{9,1},{17,9},{25,17},{2,26},{10... | collective-permute-start | bytes 786632 | tf_op jit(solution)/shard_map/ppermute | solution.py:207
  5.3 19.2 %collective-permute-start.3 = (f32[1,65552]{1,0:T(1,128)}, f32[1,65552]{1,0:T(1,128)S(1)}, u32[]{:S(2)}, u32[]{:S(2)}) collective-permute-start(f32[1,65552]{1,0:T(1,128)} %dynamic-update-slice.2), channel_id=1, source_target_pairs={{0,16},{8,24},{16,0},{24,8},{1,17},{9,25},{17,1},{25,9},{2,18},{10... | collective-permute-start | bytes 786632 | tf_op jit(solution)/shard_map/ppermute | solution.py:207
  7.6 22.6 %collective-permute-start.2 = (f32[1,65552]{1,0:T(1,128)}, f32[1,65552]{1,0:T(1,128)S(1)}, u32[]{:S(2)}, u32[]{:S(2)}) collective-permute-start(f32[1,65552]{1,0:T(1,128)} %dynamic-update-slice.2), channel_id=1, source_target_pairs={{0,8},{8,16},{16,24},{24,0},{1,9},{9,17},{17,25},{25,1},{2,10},{10... | collective-permute-start | bytes 786632 | tf_op jit(solution)/shard_map/ppermute | solution.py:207
  11.0 9.2 %copy-start.4 = (s32[1,8]{1,0:T(1,128)S(1)}, s32[1,8]{1,0:T(1,128)}, u32[]{:S(2)}) copy-start(s32[1,8]{1,0:T(1,128)} %param.8) | copy-start | bytes 100
  12.2 30.8 %collective-permute-start.1 = (f32[4,9,16,256]{3,2,1,0:T(8,128)}, f32[4,9,16,256]{3,2,1,0:T(8,128)S(1)}, u32[]{:S(2)}, u32[]{:S(2)}) collective-permute-start(f32[4,9,16,256]{3,2,1,0:T(8,128)} %get-tuple-element.32), channel_id=1, source_target_pairs={{1,0},{2,1},{3,2},{4,3},{5,4},{6,5},{7,6},{9,8},{10,9},{11,10},{12... | collective-permute-start | bytes 1769480 | tf_op jit(solution)/shard_map/ppermute | solution.py:27
  15.6 27.4 %collective-permute-start = (f32[4,9,16,256]{3,2,1,0:T(8,128)}, f32[4,9,16,256]{3,2,1,0:T(8,128)S(1)}, u32[]{:S(2)}, u32[]{:S(2)}) collective-permute-start(f32[4,9,16,256]{3,2,1,0:T(8,128)} %get-tuple-element.31), channel_id=1, source_target_pairs={{0,1},{1,2},{2,3},{3,4},{4,5},{5,6},{6,7},{8,9},{9,10},{10,11},{11... | collective-permute-start | bytes 1769480 | tf_op jit(solution)/shard_map/ppermute | solution.py:25
  19.2 3.2 %copy-start.2 = (f32[16,16,256]{2,1,0:T(8,128)S(1)}, f32[16,16,256]{2,1,0:T(8,128)}, u32[]{:S(2)}) copy-start(f32[16,16,256]{2,1,0:T(8,128)} %param.11) | copy-start | bytes 786436
  32.2 17.3 %collective-permute-start.6 = (f32[3,9,16,256]{3,2,1,0:T(8,128)}, f32[3,9,16,256]{3,2,1,0:T(8,128)}, u32[]{:S(2)}, u32[]{:S(2)}) collective-permute-start(f32[3,9,16,256]{3,2,1,0:T(8,128)} %get-tuple-element.44), channel_id=1, source_target_pairs={{1,0},{2,1},{3,2},{4,3},{5,4},{6,5},{7,6},{9,8},{10,9},{11,10},{12... | collective-permute-start | bytes 1327112 | tf_op jit(solution)/shard_map/ppermute | solution.py:27
  35.3 14.2 %collective-permute-start.5 = (f32[3,9,16,256]{3,2,1,0:T(8,128)}, f32[3,9,16,256]{3,2,1,0:T(8,128)}, u32[]{:S(2)}, u32[]{:S(2)}) collective-permute-start(f32[3,9,16,256]{3,2,1,0:T(8,128)} %get-tuple-element.43), channel_id=1, source_target_pairs={{0,1},{1,2},{2,3},{3,4},{4,5},{5,6},{6,7},{8,9},{9,10},{10,11},{11... | collective-permute-start | bytes 1327112 | tf_op jit(solution)/shard_map/ppermute | solution.py:25
  45.5 1.9 %copy-start = (f32[7,32,16,256]{3,2,1,0:T(8,128)}, f32[7,32,16,256]{3,2,1,0:T(8,128)S(1)}, u32[]{:S(2)}) copy-start(f32[7,32,16,256]{3,2,1,0:T(8,128)S(1)} %broadcast_multiply_fusion.k_ref) | copy-start | bytes 11010052
  75.0 14.1 %collective-permute-start.10 = (f32[4,5,16,256]{3,2,1,0:T(8,128)S(1)}, f32[4,5,16,256]{3,2,1,0:T(8,128)S(1)}, u32[]{:S(2)}, u32[]{:S(2)}) collective-permute-start(f32[4,5,16,256]{3,2,1,0:T(8,128)S(1)} %get-tuple-element.30), channel_id=1, source_target_pairs={{1,0},{2,1},{3,2},{4,3},{5,4},{6,5},{7,6},{9,8},{10,9},{11,10},{12... | collective-permute-start | bytes 983048 | tf_op jit(solution)/shard_map/ppermute | solution.py:27
  76.9 12.2 %collective-permute-start.9 = (f32[4,5,16,256]{3,2,1,0:T(8,128)S(1)}, f32[4,5,16,256]{3,2,1,0:T(8,128)S(1)}, u32[]{:S(2)}, u32[]{:S(2)}) collective-permute-start(f32[4,5,16,256]{3,2,1,0:T(8,128)S(1)} %get-tuple-element.29), channel_id=1, source_target_pairs={{0,1},{1,2},{2,3},{3,4},{4,5},{5,6},{6,7},{8,9},{9,10},{10,11},{11... | collective-permute-start | bytes 983048 | tf_op jit(solution)/shard_map/ppermute | solution.py:25
  81.5 15.1 %collective-permute-start.8 = (f32[4,5,16,256]{3,2,1,0:T(8,128)S(1)}, f32[4,5,16,256]{3,2,1,0:T(8,128)S(1)}, u32[]{:S(2)}, u32[]{:S(2)}) collective-permute-start(f32[4,5,16,256]{3,2,1,0:T(8,128)S(1)} %get-tuple-element.28), channel_id=1, source_target_pairs={{1,0},{2,1},{3,2},{4,3},{5,4},{6,5},{7,6},{9,8},{10,9},{11,10},{12... | collective-permute-start | bytes 983048 | tf_op jit(solution)/shard_map/ppermute | solution.py:27
  83.5 13.1 %collective-permute-start.7 = (f32[4,5,16,256]{3,2,1,0:T(8,128)S(1)}, f32[4,5,16,256]{3,2,1,0:T(8,128)S(1)}, u32[]{:S(2)}, u32[]{:S(2)}) collective-permute-start(f32[4,5,16,256]{3,2,1,0:T(8,128)S(1)} %get-tuple-element.27), channel_id=1, source_target_pairs={{0,1},{1,2},{2,3},{3,4},{4,5},{5,6},{6,7},{8,9},{9,10},{10,11},{11... | collective-permute-start | bytes 983048 | tf_op jit(solution)/shard_map/ppermute | solution.py:25

commit v9 on v8

--- a/solution.py
+++ b/solution.py
@@ -250,7 +250,12 @@
         lead = right_side.shape[:-3]
         flat_side = right_side.reshape((-1,) + right_side.shape[-3:])
         result = kernel_solve(
-            flat_side, face_stack, reach - halo, first, keeps, pushes
+            flat_side,
+            lax.slice_in_dim(face_stack, reach - halo, reach + slab + halo - 2, axis=1),
+            0,
+            first,
+            keeps,
+            pushes,
         )
         return result.reshape(lead + result.shape[-3:]), halo - CHEB
 

time: 109 us -> 106 us (0.972)
  Pallas kernels: 36.5 us -> 27.7 us
  other arithmetic: 24.7 us -> 28.9 us
    pallas_call x6, Pallas kernels: 36.5 us -> 27.7 us  [kernel_solve(): pl.pallas_call(body, grid=(fields // block,), in_specs=[pl.BlockSpec((blo...]
    mul x2, other arithmetic: 3 us -> 4.33 us  [begin(): forcing = forcing * rows_of(mask_ext, state_halo - 1)]
    concatenate x3, other arithmetic: 0.53 us -> 1.78 us  [with_halo(): jnp.concatenate([lax.ppermute(tail, axis, [(i, i + 1) for i in range(ends...]
    unnamed x14 -> x34, local copies, waits for them, and re-layouts: 3.37 us -> 3.82 us
  transfers between devices with their start and end apart: 11 -> 11, of which waited for: 2 -> 2; matrix products, arithmetic and copies ran while one was open for 17% -> 22% of each run, Pallas kernels for 8% -> 6%
where the time goes in v9:
time: 106 us; the launch traced here: 105 us
  starting transfers between devices  30.7 us (29%)
  other arithmetic  28.9 us (27%)
  Pallas kernels  27.7 us (26%)
  waiting for transfers between devices  8.56 us (8%)
  local copies, waits for them, and re-layouts  8.49 us (8%)
    pallas_call x6, Pallas kernels, kernel_solve(): pl.pallas_call(body, grid=(fields // block,), in_specs=[pl.BlockSpec((blo...  27.7 us
    ppermute x4, starting transfers between devices, with_halo(): lax.ppermute(tail, axis, [(i, i + 1) for i in range(ends)])  15.6 us
    ppermute x4, starting transfers between devices, with_halo(): lax.ppermute(head, axis, [(i + 1, i) for i in range(ends)])  10.4 us
    ppermute x3, waiting for transfers between devices, shards(): lax.ppermute(packed, 'test', [(i, (i + shift) % groups) for i in range(gr...  8.54 us
    ppermute x3, starting transfers between devices, shards(): lax.ppermute(packed, 'test', [(i, (i + shift) % groups) for i in range(gr...  4.71 us
    mul x2, other arithmetic, begin(): forcing = forcing * rows_of(mask_ext, state_halo - 1)  4.33 us
    unnamed x34, local copies, waits for them, and re-layouts  3.82 us
    reduce_sum x1, other arithmetic, shards(): contrib = jnp.sum(pairs(state[:, None], adjoint), axis=0)  2.79 us
  transfers between devices with their start and end apart: 11, of which 2 were waited for; matrix products, arithmetic and copies ran while one was open for 22% of the time, Pallas kernels for 6%

profile of v9, /device:TPU:11, one launch (start us, length us, event | category | flops | bytes accessed | tf_op | source)
XLA Modules:
  0.0 105.1 jit_solution(2731146426466465799)
XLA Ops:
  3.1 2.3 %collective-permute-start.3 = (f32[1,65552]{1,0:T(1,128)S(1)}, f32[1,65552]{1,0:T(1,128)S(1)}, u32[]{:S(2)}, u32[]{:S(2)}) collective-permute-start(f32[1,65552]{1,0:T(1,128)S(1)} %dynamic-update-slice.2), channel_id=1, source_target_pairs={{0,16},{8,24},{16,0},{24,8},{1,17},{9,25},{17,1},{25,9},{2,18},{10... | collective-permute-start | bytes 786632 | tf_op jit(solution)/shard_map/ppermute | solution.py:207
  5.4 2.2 %collective-permute-start.2 = (f32[1,65552]{1,0:T(1,128)S(1)}, f32[1,65552]{1,0:T(1,128)S(1)}, u32[]{:S(2)}, u32[]{:S(2)}) collective-permute-start(f32[1,65552]{1,0:T(1,128)S(1)} %dynamic-update-slice.2), channel_id=1, source_target_pairs={{0,8},{8,16},{16,24},{24,0},{1,9},{9,17},{17,25},{25,1},{2,10},{10... | collective-permute-start | bytes 786632 | tf_op jit(solution)/shard_map/ppermute | solution.py:207
  7.6 1.7 %broadcast_multiply_fusion.3 = (f32[16,16,256]{2,1,0:T(8,128)}, f32[1,16,16,256]{3,2,1,0:T(8,128)S(1)}, f32[16,16,256]{2,1,0:T(8,128)S(1)}) fusion(f32[16,16,256]{2,1,0:T(8,128)} %param.6), kind=kLoop, calls=%fused_computation.149 | loop fusion | flops 65536 | bytes 1048576 | tf_op jit(solution)/shard_map/mul | solution.py:300
  10.8 3.4 %collective-permute-start.1 = (f32[4,9,16,256]{3,2,1,0:T(8,128)}, f32[4,9,16,256]{3,2,1,0:T(8,128)}, u32[]{:S(2)}, u32[]{:S(2)}) collective-permute-start(f32[4,9,16,256]{3,2,1,0:T(8,128)} %get-tuple-element.32), channel_id=1, source_target_pairs={{1,0},{2,1},{3,2},{4,3},{5,4},{6,5},{7,6},{9,8},{10,9},{11,10},{12... | collective-permute-start | bytes 1769480 | tf_op jit(solution)/shard_map/ppermute | solution.py:27
  14.2 3.0 %collective-permute-start = (f32[4,9,16,256]{3,2,1,0:T(8,128)}, f32[4,9,16,256]{3,2,1,0:T(8,128)}, u32[]{:S(2)}, u32[]{:S(2)}) collective-permute-start(f32[4,9,16,256]{3,2,1,0:T(8,128)} %get-tuple-element.31), channel_id=1, source_target_pairs={{0,1},{1,2},{2,3},{3,4},{4,5},{5,6},{6,7},{8,9},{9,10},{10,11},{11... | collective-permute-start | bytes 1769480 | tf_op jit(solution)/shard_map/ppermute | solution.py:25
  19.1 2.9 %collective-permute-done.3 = f32[1,65552]{1,0:T(1,128)S(1)} collective-permute-done((f32[1,65552]{1,0:T(1,128)S(1)}, f32[1,65552]{1,0:T(1,128)S(1)}, u32[]{:S(2)}, u32[]{:S(2)}) %collective-permute-start.3) | collective-permute-done | bytes 262240 | tf_op jit(solution)/shard_map/ppermute | solution.py:207
  22.1 5.6 %collective-permute-done.2 = f32[1,65552]{1,0:T(1,128)S(1)} collective-permute-done((f32[1,65552]{1,0:T(1,128)S(1)}, f32[1,65552]{1,0:T(1,128)S(1)}, u32[]{:S(2)}, u32[]{:S(2)}) %collective-permute-start.2) | collective-permute-done | bytes 262240 | tf_op jit(solution)/shard_map/ppermute | solution.py:207
  29.8 3.1 %collective-permute-start.6 = (f32[3,9,16,256]{3,2,1,0:T(8,128)}, f32[3,9,16,256]{3,2,1,0:T(8,128)}, u32[]{:S(2)}, u32[]{:S(2)}) collective-permute-start(f32[3,9,16,256]{3,2,1,0:T(8,128)} %get-tuple-element.44), channel_id=1, source_target_pairs={{1,0},{2,1},{3,2},{4,3},{5,4},{6,5},{7,6},{9,8},{10,9},{11,10},{12... | collective-permute-start | bytes 1327112 | tf_op jit(solution)/shard_map/ppermute | solution.py:27
  32.9 3.5 %collective-permute-start.5 = (f32[3,9,16,256]{3,2,1,0:T(8,128)}, f32[3,9,16,256]{3,2,1,0:T(8,128)}, u32[]{:S(2)}, u32[]{:S(2)}) collective-permute-start(f32[3,9,16,256]{3,2,1,0:T(8,128)} %get-tuple-element.43), channel_id=1, source_target_pairs={{0,1},{1,2},{2,3},{3,4},{4,5},{5,6},{6,7},{8,9},{9,10},{10,11},{11... | collective-permute-start | bytes 1327112 | tf_op jit(solution)/shard_map/ppermute | solution.py:25
  36.5 1.8 %broadcast_compare_fusion = pred[3,8,34,16,256]{4,3,2,1,0:T(8,128)(4,1)S(1)} fusion(s32[34,16,256]{2,1,0:T(8,128)S(1)} %iota_add_fusion, s32[3,8]{1,0:T(4,128)S(1)} %get-tuple-element.36), kind=kLoop, calls=%fused_computation.1 | loop fusion | flops 3342336 | bytes 3899488 | tf_op jit(solution)/shard_map/eq | solution.py:263
  45.1 1.7 %shard_map.64 = f32[1,26,16,256]{3,2,1,0:T(8,128)S(1)} custom-call(f32[1,34,16,256]{3,2,1,0:T(8,128)S(1)} %slice_add_fusion.2.b_ref, f32[7,32,16,256]{3,2,1,0:T(8,128)S(1)} %broadcast_multiply_fusion.k_ref), custom_call_target="tpu_custom_call" | custom-call | tf_op jit(solution)/shard_map/pallas_call | solution.py:90
  49.0 2.8 %negate_multiply_fusion.1 = (f32[1,2,24,16,256]{4,3,2,1,0:T(8,128)}, f32[2,24,16,256]{3,2,1,0:T(8,128)S(1)}, f32[2,24,16,256]{3,2,1,0:T(8,128)}, f32[2,24,16,256...) fusion(f32[24]{0:T(128)S(1)} %slice.283, f32[24,16,256]{2,1,0:T(8,128)S(1)} %get-tuple-element.50, ...), kind=kLoop, calls=%fused_computation.94 | loop fusion | flops 5701632 | bytes 10223712 | tf_op jit(solution)/shard_map/mul | solution.py:270
  51.8 1.5 %maximum_add_fusion.b_ref = f32[3,34,16,256]{3,2,1,0:T(8,128)S(1)} fusion(f32[3,34,16,256]{3,2,1,0:T(8,128)S(1)} %select_reduce_fusion, f32[3,9,16,256]{3,2,1,0:T(8,128)} %collective-permute-done.6, f32[3,16,16,256]{3,2,1,0:T(8,128)S(1)} %bitcast.116, f32[3,9,16,256]{3,2,1,0:T(8,128)} %collective-permute-done.5), kind=kLoop, calls=%fused_computation.42 | loop fusion | flops 1253376 | bytes 5013504 | tf_op jit(solution)/shard_map/add | solution.py:268
  53.3 7.2 %shard_map.65 = f32[3,26,16,256]{3,2,1,0:T(8,128)S(1)} custom-call(f32[3,34,16,256]{3,2,1,0:T(8,128)S(1)} %maximum_add_fusion.b_ref, f32[7,32,16,256]{3,2,1,0:T(8,128)} %copy-done), custom_call_target="tpu_custom_call" | custom-call | tf_op jit(solution)/shard_map/pallas_call | solution.py:90
  63.1 1.6 %negate_multiply_fusion = f32[3,2,24,16,256]{4,3,2,1,0:T(8,128)S(1)} fusion(f32[24]{0:T(128)S(1)} %slice.283, f32[3,24,16,256]{3,2,1,0:T(8,128)S(1)} %get-tuple-element.21, f32[2,24,16,256]{3,2,1,0:T(8,128)S(1)} %copy-done.6, f32[3,24,16,256]{3,2,1,0:T(8,128)S(1)} %get-tuple-element.20, f32[2,24,16,256]{3,2,1,0:T(8,128)S(1)} %copy-done.5, ...), kind=kLoop, calls=%fused_computation.9 | loop fusion | flops 7667712 | bytes 14155872 | tf_op jit(solution)/shard_map/mul | solution.py:270
  65.0 4.4 %shard_map.66 = f32[4,16,16,256]{3,2,1,0:T(8,128)S(1)} custom-call(f32[4,24,16,256]{3,2,1,0:T(8,128)S(1)} %bitcast.112, f32[7,22,16,256]{3,2,1,0:T(8,128)S(1)} %slice.342.k_ref), custom_call_target="tpu_custom_call" | custom-call | tf_op jit(solution)/shard_map/pallas_call | solution.py:90
  69.6 4.4 %shard_map.68 = f32[4,16,16,256]{3,2,1,0:T(8,128)S(1)} custom-call(f32[4,24,16,256]{3,2,1,0:T(8,128)S(1)} %bitcast.111, f32[7,22,16,256]{3,2,1,0:T(8,128)S(1)} %slice.342.k_ref), custom_call_target="tpu_custom_call" | custom-call | tf_op jit(solution)/shard_map/pallas_call | solution.py:90
  74.2 1.9 %collective-permute-start.10 = (f32[4,5,16,256]{3,2,1,0:T(8,128)S(1)}, f32[4,5,16,256]{3,2,1,0:T(8,128)S(1)}, u32[]{:S(2)}, u32[]{:S(2)}) collective-permute-start(f32[4,5,16,256]{3,2,1,0:T(8,128)S(1)} %get-tuple-element.30), channel_id=1, source_target_pairs={{1,0},{2,1},{3,2},{4,3},{5,4},{6,5},{7,6},{9,8},{10,9},{11,10},{12... | collective-permute-start | bytes 983048 | tf_op jit(solution)/shard_map/ppermute | solution.py:27
  76.1 4.5 %collective-permute-start.9 = (f32[4,5,16,256]{3,2,1,0:T(8,128)S(1)}, f32[4,5,16,256]{3,2,1,0:T(8,128)S(1)}, u32[]{:S(2)}, u32[]{:S(2)}) collective-permute-start(f32[4,5,16,256]{3,2,1,0:T(8,128)S(1)} %get-tuple-element.29), channel_id=1, source_target_pairs={{0,1},{1,2},{2,3},{3,4},{4,5},{5,6},{6,7},{8,9},{9,10},{10,11},{11... | collective-permute-start | bytes 983048 | tf_op jit(solution)/shard_map/ppermute | solution.py:25
  80.7 1.9 %collective-permute-start.8 = (f32[4,5,16,256]{3,2,1,0:T(8,128)S(1)}, f32[4,5,16,256]{3,2,1,0:T(8,128)S(1)}, u32[]{:S(2)}, u32[]{:S(2)}) collective-permute-start(f32[4,5,16,256]{3,2,1,0:T(8,128)S(1)} %get-tuple-element.28), channel_id=1, source_target_pairs={{1,0},{2,1},{3,2},{4,3},{5,4},{6,5},{7,6},{9,8},{10,9},{11,10},{12... | collective-permute-start | bytes 983048 | tf_op jit(solution)/shard_map/ppermute | solution.py:27
  82.7 4.5 %collective-permute-start.7 = (f32[4,5,16,256]{3,2,1,0:T(8,128)S(1)}, f32[4,5,16,256]{3,2,1,0:T(8,128)S(1)}, u32[]{:S(2)}, u32[]{:S(2)}) collective-permute-start(f32[4,5,16,256]{3,2,1,0:T(8,128)S(1)} %get-tuple-element.27), channel_id=1, source_target_pairs={{0,1},{1,2},{2,3},{3,4},{4,5},{5,6},{6,7},{8,9},{9,10},{10,11},{11... | collective-permute-start | bytes 983048 | tf_op jit(solution)/shard_map/ppermute | solution.py:25
  89.6 5.1 %shard_map.69 = f32[4,18,16,256]{3,2,1,0:T(8,128)S(1)} custom-call(f32[4,26,16,256]{3,2,1,0:T(8,128)S(1)} %pad_maximum_fusion.3.b_ref, f32[7,24,16,256]{3,2,1,0:T(8,128)S(1)} %slice.346.k_ref), custom_call_target="tpu_custom_call" | custom-call | tf_op jit(solution)/shard_map/pallas_call | solution.py:90
  95.0 4.9 %shard_map.67 = f32[4,18,16,256]{3,2,1,0:T(8,128)S(1)} custom-call(f32[4,26,16,256]{3,2,1,0:T(8,128)S(1)} %pad_maximum_fusion.2.b_ref, f32[7,24,16,256]{3,2,1,0:T(8,128)S(1)} %slice.346.k_ref), custom_call_target="tpu_custom_call" | custom-call | tf_op jit(solution)/shard_map/pallas_call | solution.py:90
  101.4 2.8 %fusion.6 = f32[2,16,16,256]{3,2,1,0:T(8,128)S(1)} fusion(f32[4,2,16,16,256]{4,3,2,1,0:T(8,128)S(1)} %slice.350, f32[4,2,18,16,256]{4,3,2,1,0:T(8,128)S(1)} %bitcast.114, f32[4,16,16,256]{3,2,1,0:T(8,128)S(1)} %get-tuple-element.25, f32[4,16,16,256]{3,2,1,0:T(8,128)S(1)} %get-tuple-element.24, f32[4,16,16,256]{3,2,1,0:T(8,128)S(1)} %get-tuple-element.26, ...), kind=kLoop, calls=%fused_computation.18 | loop fusion | flops 9306112 | bytes 13107200 | tf_op jit(solution)/shard_map/reduce_sum | solution.py:299
  (106 shorter events, 25.5 us)
Async XLA Ops:
  0.0 9.4 %copy-start.8 = (f32[1,16,16,256]{3,2,1,0:T(8,128)S(1)}, f32[1,16,16,256]{3,2,1,0:T(8,128)}, u32[]{:S(2)}) copy-start(f32[1,16,16,256]{3,2,1,0:T(8,128)} %param.10) | copy-start | bytes 786436
  0.0 9.4 %copy-start.12 = (f32[2,16,16,256]{3,2,1,0:T(8,128)S(1)}, f32[2,16,16,256]{3,2,1,0:T(8,128)}, u32[]{:S(2)}) copy-start(f32[2,16,16,256]{3,2,1,0:T(8,128)} %param.7) | copy-start | bytes 1572868
  2.9 16.2 %collective-permute-start.4 = (f32[1,65552]{1,0:T(1,128)S(1)}, f32[1,65552]{1,0:T(1,128)S(1)}, u32[]{:S(2)}, u32[]{:S(2)}) collective-permute-start(f32[1,65552]{1,0:T(1,128)S(1)} %dynamic-update-slice.2), channel_id=1, source_target_pairs={{0,24},{8,0},{16,8},{24,16},{1,25},{9,1},{17,9},{25,17},{2,26},{10... | collective-permute-start | bytes 786632 | tf_op jit(solution)/shard_map/ppermute | solution.py:207
  3.1 18.9 %collective-permute-start.3 = (f32[1,65552]{1,0:T(1,128)S(1)}, f32[1,65552]{1,0:T(1,128)S(1)}, u32[]{:S(2)}, u32[]{:S(2)}) collective-permute-start(f32[1,65552]{1,0:T(1,128)S(1)} %dynamic-update-slice.2), channel_id=1, source_target_pairs={{0,16},{8,24},{16,0},{24,8},{1,17},{9,25},{17,1},{25,9},{2,18},{10... | collective-permute-start | bytes 786632 | tf_op jit(solution)/shard_map/ppermute | solution.py:207
  5.4 22.2 %collective-permute-start.2 = (f32[1,65552]{1,0:T(1,128)S(1)}, f32[1,65552]{1,0:T(1,128)S(1)}, u32[]{:S(2)}, u32[]{:S(2)}) collective-permute-start(f32[1,65552]{1,0:T(1,128)S(1)} %dynamic-update-slice.2), channel_id=1, source_target_pairs={{0,8},{8,16},{16,24},{24,0},{1,9},{9,17},{17,25},{25,1},{2,10},{10... | collective-permute-start | bytes 786632 | tf_op jit(solution)/shard_map/ppermute | solution.py:207
  9.4 8.1 %copy-start.13 = (s32[1,8]{1,0:T(1,128)S(1)}, s32[1,8]{1,0:T(1,128)}, u32[]{:S(2)}) copy-start(s32[1,8]{1,0:T(1,128)} %param.8) | copy-start | bytes 100
  9.5 8.6 %copy-start.14 = (f32[1,8]{1,0:T(1,128)S(1)}, f32[1,8]{1,0:T(1,128)}, u32[]{:S(2)}) copy-start(f32[1,8]{1,0:T(1,128)} %param.9) | copy-start | bytes 100
  10.8 30.6 %collective-permute-start.1 = (f32[4,9,16,256]{3,2,1,0:T(8,128)}, f32[4,9,16,256]{3,2,1,0:T(8,128)}, u32[]{:S(2)}, u32[]{:S(2)}) collective-permute-start(f32[4,9,16,256]{3,2,1,0:T(8,128)} %get-tuple-element.32), channel_id=1, source_target_pairs={{1,0},{2,1},{3,2},{4,3},{5,4},{6,5},{7,6},{9,8},{10,9},{11,10},{12... | collective-permute-start | bytes 1769480 | tf_op jit(solution)/shard_map/ppermute | solution.py:27
  14.2 27.2 %collective-permute-start = (f32[4,9,16,256]{3,2,1,0:T(8,128)}, f32[4,9,16,256]{3,2,1,0:T(8,128)}, u32[]{:S(2)}, u32[]{:S(2)}) collective-permute-start(f32[4,9,16,256]{3,2,1,0:T(8,128)} %get-tuple-element.31), channel_id=1, source_target_pairs={{0,1},{1,2},{2,3},{3,4},{4,5},{5,6},{6,7},{8,9},{9,10},{10,11},{11... | collective-permute-start | bytes 1769480 | tf_op jit(solution)/shard_map/ppermute | solution.py:25
  17.2 1.9 %copy-start.10 = (f32[16,16,256]{2,1,0:T(8,128)S(1)}, f32[16,16,256]{2,1,0:T(8,128)}, u32[]{:S(2)}) copy-start(f32[16,16,256]{2,1,0:T(8,128)} %param.11) | copy-start | bytes 786436
  29.8 22.0 %collective-permute-start.6 = (f32[3,9,16,256]{3,2,1,0:T(8,128)}, f32[3,9,16,256]{3,2,1,0:T(8,128)}, u32[]{:S(2)}, u32[]{:S(2)}) collective-permute-start(f32[3,9,16,256]{3,2,1,0:T(8,128)} %get-tuple-element.44), channel_id=1, source_target_pairs={{1,0},{2,1},{3,2},{4,3},{5,4},{6,5},{7,6},{9,8},{10,9},{11,10},{12... | collective-permute-start | bytes 1327112 | tf_op jit(solution)/shard_map/ppermute | solution.py:27
  32.9 18.9 %collective-permute-start.5 = (f32[3,9,16,256]{3,2,1,0:T(8,128)}, f32[3,9,16,256]{3,2,1,0:T(8,128)}, u32[]{:S(2)}, u32[]{:S(2)}) collective-permute-start(f32[3,9,16,256]{3,2,1,0:T(8,128)} %get-tuple-element.43), channel_id=1, source_target_pairs={{0,1},{1,2},{2,3},{3,4},{4,5},{5,6},{6,7},{8,9},{9,10},{10,11},{11... | collective-permute-start | bytes 1327112 | tf_op jit(solution)/shard_map/ppermute | solution.py:25
  45.1 3.5 %copy-start = (f32[7,32,16,256]{3,2,1,0:T(8,128)}, f32[7,32,16,256]{3,2,1,0:T(8,128)S(1)}, u32[]{:S(2)}) copy-start(f32[7,32,16,256]{3,2,1,0:T(8,128)S(1)} %broadcast_multiply_fusion.k_ref) | copy-start | bytes 11010052
  61.0 1.4 %copy-start.3 = (f32[2,24,16,256]{3,2,1,0:T(8,128)S(1)}, f32[2,24,16,256]{3,2,1,0:T(8,128)}, u32[]{:S(2)}) copy-start(f32[2,24,16,256]{3,2,1,0:T(8,128)} %get-tuple-element.40) | copy-start | bytes 2359300
  61.0 1.6 %copy-start.4 = (f32[2,24,16,256]{3,2,1,0:T(8,128)S(1)}, f32[2,24,16,256]{3,2,1,0:T(8,128)}, u32[]{:S(2)}) copy-start(f32[2,24,16,256]{3,2,1,0:T(8,128)} %get-tuple-element.41) | copy-start | bytes 2359300
  61.0 1.8 %copy-start.5 = (f32[2,24,16,256]{3,2,1,0:T(8,128)S(1)}, f32[2,24,16,256]{3,2,1,0:T(8,128)}, u32[]{:S(2)}) copy-start(f32[2,24,16,256]{3,2,1,0:T(8,128)} %get-tuple-element.42) | copy-start | bytes 2359300
  61.0 2.1 %copy-start.6 = (f32[2,24,16,256]{3,2,1,0:T(8,128)S(1)}, f32[2,24,16,256]{3,2,1,0:T(8,128)}, u32[]{:S(2)}) copy-start(f32[2,24,16,256]{3,2,1,0:T(8,128)} %multiply_bitcast_fusion) | copy-start | bytes 2359300
  63.1 1.6 %copy-start.7 = (f32[1,2,24,16,256]{4,3,2,1,0:T(8,128)S(1)}, f32[1,2,24,16,256]{4,3,2,1,0:T(8,128)}, u32[]{:S(2)}) copy-start(f32[1,2,24,16,256]{4,3,2,1,0:T(8,128)} %get-tuple-element.33) | copy-start | bytes 2359300
  65.0 4.4 %copy-start.9 = (f32[2,16,16,256]{3,2,1,0:T(8,128)S(1)}, f32[2,16,16,256]{3,2,1,0:T(8,128)}, u32[]{:S(2)}) copy-start(f32[2,16,16,256]{3,2,1,0:T(8,128)} %get-tuple-element.39) | copy-start | bytes 1572868
  74.2 15.2 %collective-permute-start.10 = (f32[4,5,16,256]{3,2,1,0:T(8,128)S(1)}, f32[4,5,16,256]{3,2,1,0:T(8,128)S(1)}, u32[]{:S(2)}, u32[]{:S(2)}) collective-permute-start(f32[4,5,16,256]{3,2,1,0:T(8,128)S(1)} %get-tuple-element.30), channel_id=1, source_target_pairs={{1,0},{2,1},{3,2},{4,3},{5,4},{6,5},{7,6},{9,8},{10,9},{11,10},{12... | collective-permute-start | bytes 983048 | tf_op jit(solution)/shard_map/ppermute | solution.py:27
  76.1 13.3 %collective-permute-start.9 = (f32[4,5,16,256]{3,2,1,0:T(8,128)S(1)}, f32[4,5,16,256]{3,2,1,0:T(8,128)S(1)}, u32[]{:S(2)}, u32[]{:S(2)}) collective-permute-start(f32[4,5,16,256]{3,2,1,0:T(8,128)S(1)} %get-tuple-element.29), channel_id=1, source_target_pairs={{0,1},{1,2},{2,3},{3,4},{4,5},{5,6},{6,7},{8,9},{9,10},{10,11},{11... | collective-permute-start | bytes 983048 | tf_op jit(solution)/shard_map/ppermute | solution.py:25
  80.7 14.0 %collective-permute-start.8 = (f32[4,5,16,256]{3,2,1,0:T(8,128)S(1)}, f32[4,5,16,256]{3,2,1,0:T(8,128)S(1)}, u32[]{:S(2)}, u32[]{:S(2)}) collective-permute-start(f32[4,5,16,256]{3,2,1,0:T(8,128)S(1)} %get-tuple-element.28), channel_id=1, source_target_pairs={{1,0},{2,1},{3,2},{4,3},{5,4},{6,5},{7,6},{9,8},{10,9},{11,10},{12... | collective-permute-start | bytes 983048 | tf_op jit(solution)/shard_map/ppermute | solution.py:27
  82.7 12.1 %collective-permute-start.7 = (f32[4,5,16,256]{3,2,1,0:T(8,128)S(1)}, f32[4,5,16,256]{3,2,1,0:T(8,128)S(1)}, u32[]{:S(2)}, u32[]{:S(2)}) collective-permute-start(f32[4,5,16,256]{3,2,1,0:T(8,128)S(1)} %get-tuple-element.27), channel_id=1, source_target_pairs={{0,1},{1,2},{2,3},{3,4},{4,5},{5,6},{6,7},{8,9},{9,10},{10,11},{11... | collective-permute-start | bytes 983048 | tf_op jit(solution)/shard_map/ppermute | solution.py:25
  101.4 2.8 %copy-start.11 = (f32[16,16,256]{2,1,0:T(8,128)S(1)}, f32[16,16,256]{2,1,0:T(8,128)}, u32[]{:S(2)}) copy-start(f32[16,16,256]{2,1,0:T(8,128)} %get-tuple-element.52) | copy-start | bytes 786436
  (2 other events, 2.4 us)
